TPU v7x, 256 devices: a whole 4x4x8 slice. The times are simulated.
256 devices in a mesh: blk: 64 (over x, y, z_hi, core), mode: 4 (over z_lo).
Axes of the slice: x: 4, y: 4, z: 8 (z_hi: 2, z_lo: 4; z = z_hi * 4 + z_lo), core: 2. Of those that a mesh axis runs over, the one named last changes fastest.
Arguments:
- direct: float32 [16, 2, 5, 128, 8, 512], P('mode', None, None, 'blk'), may hold values from -6 to 6
- adjoint: float32 [16, 2, 5, 128, 8, 512], P('mode', None, None, 'blk'), may hold values from -6 to 6
- density: float32 [128, 8, 512], P('blk'), may hold values from 0.7 to 1.4
- velocity: float32 [2, 128, 8, 512], P(None, 'blk'), may hold values from -0.8 to 0.8
- pressure: float32 [128, 8, 512], P('blk'), may hold values from 0.5 to 1
- block_home: int32 [128], replicated, may hold values from 0 to 127, as said below
- face_nbr: int32 [128, 4], P('blk'), may hold values from -1 to 127, as said below
- face_flip: int32 [128, 4], P('blk'), may hold values from 0 to 1, as said below
Outputs:
- direct_out: float32 [16, 2, 5, 128, 8, 512], P('mode', None, None, 'blk')
- adjoint_out: float32 [16, 2, 5, 128, 8, 512], P('mode', None, None, 'blk')
- sensitivity: float32 [128, 8, 512], P('blk')
Inputs may be any that keep to these rules, and one draw needn't show every extreme that they name: Block g lies on blk device g // 2; block_home is a permutation of positions that keeps each block on its device. `face_nbr`: the low-i neighbour of a block on device d lies on device d - 1 and the high-i one on device d + 1 (cyclically along blk), the high-i face of one meeting the low-i face of the other; j neighbours lie on the same device or are walls (-1); connections are mutual. `face_flip`: both sides of a connection carry the same flag; j faces carry 0.
All inputs are finite; a program needn't handle non-finite values.
Results may differ from a plain program's by a relative error of at most 0.0001.
Values sent between devices are 32-bit elements; how exact they have to be, the bound alone decides.
No kernel may reach another device: no remote copies, remote signals or barrier semaphores. Data moves between devices by JAX's collectives and lax.ppermute only.
A program may use at most 64 MiB of HBM per device.

v0:
```python
import functools

import jax
import jax.numpy as jnp
from jax import lax
from jax.experimental import pallas as pl
from jax.experimental.pallas import tpu as pltpu
from jax.sharding import PartitionSpec as P

STEPS = 2

HEAT_RATIO = 1.4
VISCOSITY = 0.25
TIME_STEP = 0.05
SPAN_WAVE = 0.5
BASE_FREQ = 0.2

NV = 5
ENTRIES = 8


def shifted(block, axis, distance):
    n = lax.axis_size(axis)
    route = [((i - distance) % n, i) for i in range(n)]
    return lax.ppermute(block, axis, route)


def direct_rates(bf, X, Y, dsX, dcX, lapX, dsY, dcY, lapY, w):
    r, ir, u, v, kp = bf
    b = SPAN_WAVE
    damp = SPAN_WAVE * SPAN_WAVE

    def conv(ds, dc):
        return [
            u * ds[0] + r * ds[1] + (v * dc[0] + r * dc[2]),
            u * ds[1] + ds[4] * ir + v * dc[1],
            u * ds[2] + (v * dc[2] + dc[4] * ir),
            u * ds[3] + v * dc[3],
            kp * ds[1] + u * ds[4] + (kp * dc[2] + v * dc[4]),
        ]

    def span(f):
        return [r * f[3], None, None, f[4] * ir, kp * f[3]]

    cX = conv(dsX, dcX)
    cY = conv(dsY, dcY)
    sX = span(X)
    sY = span(Y)
    re, im = [], []
    for n in range(NV):
        a = -cX[n] + VISCOSITY * (lapX[n] - damp * X[n])
        if sY[n] is not None:
            a = a + b * sY[n]
        a = a + w * Y[n]
        c = -cY[n] + VISCOSITY * (lapY[n] - damp * Y[n])
        if sX[n] is not None:
            c = c - b * sX[n]
        c = c - w * X[n]
        re.append(a)
        im.append(c)
    return re, im


def adjoint_rates(bf, X, Y, dsX, dcX, lapX, dsY, dcY, lapY, w):
    r, ir, u, v, kp = bf
    b = SPAN_WAVE
    damp = SPAN_WAVE * SPAN_WAVE

    def conv(ds, dc):
        return [
            u * ds[0] + v * dc[0],
            r * ds[0] + u * ds[1] + kp * ds[4] + v * dc[1],
            u * ds[2] + (r * dc[0] + v * dc[2] + kp * dc[4]),
            u * ds[3] + v * dc[3],
            ds[1] * ir + u * ds[4] + (dc[2] * ir + v * dc[4]),
        ]

    def span(f):
        return [None, None, None, r * f[0] + kp * f[4], f[3] * ir]

    cX = conv(dsX, dcX)
    cY = conv(dsY, dcY)
    sX = span(X)
    sY = span(Y)
    re, im = [], []
    for n in range(NV):
        a = cX[n] + VISCOSITY * (lapX[n] - damp * X[n])
        if sY[n] is not None:
            a = a - b * sY[n]
        a = a - w * Y[n]
        c = cY[n] + VISCOSITY * (lapY[n] - damp * Y[n])
        if sX[n] is not None:
            c = c + b * sX[n]
        c = c + w * X[n]
        re.append(a)
        im.append(c)
    return re, im


def step_kernel(tbl, x_ref, a_ref, rlo_ref, rhi_ref, rho_ref, vel_ref, prs_ref, *rest, modes_total, first):
    if first:
        xo_ref, ao_ref, sens_ref, elo_ref, ehi_ref, rev_ref = rest
    else:
        sin_ref, xo_ref, ao_ref, sens_ref, rev_ref = rest
    m = pl.program_id(0)
    slots = x_ref.shape[3]
    height = x_ref.shape[4]
    width = x_ref.shape[5]
    shape = (height, width)

    @pl.when(m == 0)
    def _init():
        ri = lax.broadcasted_iota(jnp.int32, (width, width), 0)
        ci = lax.broadcasted_iota(jnp.int32, (width, width), 1)
        rev_ref[...] = jnp.where(ri + ci == width - 1, 1.0, 0.0).astype(jnp.float32)
        if first:
            sens_ref[...] = jnp.zeros(sens_ref.shape, jnp.float32)
        else:
            sens_ref[...] = sin_ref[...]

    kf = (tbl[slots * ENTRIES] + m).astype(jnp.float32)
    w = BASE_FREQ * (jnp.zeros(shape, jnp.float32) + (kf - modes_total / 2 + 0.5))
    row = lax.broadcasted_iota(jnp.int32, shape, 0)
    col = lax.broadcasted_iota(jnp.int32, shape, 1)
    zero_i = jnp.zeros(shape, jnp.int32)
    rev = rev_ref[...]

    def flip_rows(rows, flag):
        turned = jnp.dot(rows, rev, precision=lax.Precision.HIGHEST, preferred_element_type=jnp.float32)
        mask = (jnp.zeros(rows.shape, jnp.int32) + flag) != 0
        return jnp.where(mask, turned, rows)

    for s in range(slots):
        base = s * ENTRIES
        lo_t, lo_f = tbl[base + 0], tbl[base + 1]
        hi_t, hi_f = tbl[base + 2], tbl[base + 3]
        jl_s, jl_live = tbl[base + 4], tbl[base + 5]
        jh_s, jh_live = tbl[base + 6], tbl[base + 7]
        jl_mask = (zero_i + jl_live) != 0
        jh_mask = (zero_i + jh_live) != 0
        r = rho_ref[s]
        ir = 1.0 / r
        u = vel_ref[0, s]
        v = vel_ref[1, s]
        kp = HEAT_RATIO * prs_ref[s]
        bf = (r, ir, u, v, kp)
        news = []
        for arr, (src, dst, rates) in enumerate(((x_ref, xo_ref, direct_rates), (a_ref, ao_ref, adjoint_rates))):
            lo_rows = flip_rows(rlo_ref[arr, 0, lo_t], lo_f)
            hi_rows = flip_rows(rhi_ref[arr, 0, hi_t], hi_f)
            vals, dss, dcs, laps = [], [], [], []
            for p in range(2):
                for n in range(NV):
                    k = p * NV + n
                    g = src[0, p, n, s]
                    lo_b = jnp.broadcast_to(lo_rows[k:k + 1, :], shape)
                    hi_b = jnp.broadcast_to(hi_rows[k:k + 1, :], shape)
                    im1 = jnp.where(row == 0, lo_b, pltpu.roll(g, 1, 0))
                    ip1 = jnp.where(row == height - 1, hi_b, pltpu.roll(g, height - 1, 0))
                    nl = pltpu.roll(src[0, p, n, jl_s], 1, 1)
                    nh = pltpu.roll(src[0, p, n, jh_s], width - 1, 1)
                    jm1 = jnp.where(col == 0, jnp.where(jl_mask, nl, 0.0), pltpu.roll(g, 1, 1))
                    jp1 = jnp.where(col == width - 1, jnp.where(jh_mask, nh, 0.0), pltpu.roll(g, width - 1, 1))
                    vals.append(g)
                    dss.append((ip1 - im1) * 0.5)
                    dcs.append((jp1 - jm1) * 0.5)
                    laps.append(ip1 + im1 + jp1 + jm1 - 4.0 * g)
            X, Y = vals[:NV], vals[NV:]
            re, im = rates(bf, X, Y, dss[:NV], dcs[:NV], laps[:NV], dss[NV:], dcs[NV:], laps[NV:], w)
            total = None
            for p, rate in enumerate((re, im)):
                for n in range(NV):
                    k = p * NV + n
                    nv = vals[k] + TIME_STEP * rate[n]
                    dst[0, p, n, s] = nv
                    if first:
                        elo_ref[arr, 0, s, pl.ds(k, 1), :] = nv[0:1, :]
                        ehi_ref[arr, 0, s, pl.ds(k, 1), :] = nv[height - 1:height, :]
                    sq = nv * nv
                    total = sq if total is None else total + sq
            news.append(total / 10.0)
        sens_ref[s] = sens_ref[s] + news[0] * news[1]


def run_step(tbl, x, a, rlo, rhi, density, velocity, pressure, sens_in, modes_total, first):
    modes, parts, nv, slots, height, width = x.shape
    state_block = (1, parts, nv, slots, height, width)
    edge_block = (2, 1, slots, parts * nv, width)
    state_spec = pl.BlockSpec(state_block, lambda m, t: (m, 0, 0, 0, 0, 0))
    edge_spec = pl.BlockSpec(edge_block, lambda m, t: (0, m, 0, 0, 0))
    flow_spec = pl.BlockSpec((slots, height, width), lambda m, t: (0, 0, 0))
    vel_spec = pl.BlockSpec((2, slots, height, width), lambda m, t: (0, 0, 0, 0))
    in_specs = [state_spec, state_spec, edge_spec, edge_spec, flow_spec, vel_spec, flow_spec]
    args = [x, a, rlo, rhi, density, velocity, pressure]
    if not first:
        in_specs.append(flow_spec)
        args.append(sens_in)
    out_shape = [
        jax.ShapeDtypeStruct(x.shape, jnp.float32),
        jax.ShapeDtypeStruct(a.shape, jnp.float32),
        jax.ShapeDtypeStruct((slots, height, width), jnp.float32),
    ]
    out_specs = [state_spec, state_spec, flow_spec]
    if first:
        edge_shape = jax.ShapeDtypeStruct((2, modes, slots, parts * nv, width), jnp.float32)
        out_shape += [edge_shape, edge_shape]
        out_specs += [edge_spec, edge_spec]
    grid_spec = pltpu.PrefetchScalarGridSpec(
        num_scalar_prefetch=1,
        grid=(modes,),
        in_specs=in_specs,
        out_specs=out_specs,
        scratch_shapes=[pltpu.VMEM((width, width), jnp.float32)],
    )
    kernel = functools.partial(step_kernel, modes_total=modes_total, first=first)
    return pl.pallas_call(
        kernel,
        grid_spec=grid_spec,
        out_shape=out_shape,
        compiler_params=pltpu.CompilerParams(dimension_semantics=("arbitrary",)),
    )(tbl, *args)


def edges(x, row):
    modes, parts, nv, slots, height, width = x.shape
    e = x[:, :, :, :, row, :]
    return jnp.transpose(e, (0, 3, 1, 2, 4)).reshape(modes, slots, parts * nv, width)


def per_device(direct, adjoint, density, velocity, pressure, block_home, face_nbr, face_flip):
    modes, parts, nv, slots, height, width = direct.shape
    modes_total = modes * lax.axis_size("mode")
    live = (face_nbr >= 0).astype(jnp.int32)
    positions = jnp.take(block_home, jnp.maximum(face_nbr, 0), axis=0)
    slot_of = positions % slots
    table = jnp.stack(
        [
            slot_of[:, 0], face_flip[:, 0], slot_of[:, 1], face_flip[:, 1],
            slot_of[:, 2], live[:, 2], slot_of[:, 3], live[:, 3],
        ],
        axis=1,
    ).reshape(-1)
    mode_base = (lax.axis_index("mode") * modes).astype(jnp.int32)
    table = jnp.concatenate([table.astype(jnp.int32), mode_base[None]])

    with jax.named_scope("edge_exchange_0"):
        up = jnp.stack([edges(direct, height - 1), edges(adjoint, height - 1)])
        down = jnp.stack([edges(direct, 0), edges(adjoint, 0)])
        rlo = shifted(up, "blk", 1)
        rhi = shifted(down, "blk", -1)
    with jax.named_scope("flow_step_0"):
        q1, a1, sens, elo, ehi = run_step(
            table, direct, adjoint, rlo, rhi, density, velocity, pressure, None, modes_total, True
        )
    with jax.named_scope("edge_exchange_1"):
        rlo = shifted(ehi, "blk", 1)
        rhi = shifted(elo, "blk", -1)
    with jax.named_scope("flow_step_1"):
        q2, a2, sens = run_step(
            table, q1, a1, rlo, rhi, density, velocity, pressure, sens, modes_total, False
        )
    with jax.named_scope("mode_reduce"):
        count = lax.axis_size("mode")
        me = lax.axis_index("mode")
        stacked = jnp.stack([sens] + [shifted(sens, "mode", k) for k in range(1, count)])
        total = None
        for j in range(count):
            part = lax.dynamic_index_in_dim(stacked, (me - j) % count, axis=0, keepdims=False)
            total = part if total is None else total + part
        sensitivity = total / (STEPS * modes_total)
    return (q2, a2, sensitivity)


def solution(mesh):
    placed = (
        P("mode", None, None, "blk", None, None),
        P("mode", None, None, "blk", None, None),
        P("blk", None, None),
        P(None, "blk", None, None),
        P("blk", None, None),
        P(),
        P("blk", None),
        P("blk", None),
    )
    return jax.shard_map(
        per_device,
        mesh=mesh,
        in_specs=placed,
        out_specs=(
            P("mode", None, None, "blk", None, None),
            P("mode", None, None, "blk", None, None),
            P("blk", None, None),
        ),
        check_vma=False,
    )
```

profile of v0, /device:TPU:32, one launch (start us, length us, event | category | flops | bytes accessed | tf_op | source)
XLA Modules:
  0.0 114.3 jit_solution(9236632044151252637)
XLA Ops:
  0.6 0.0 copy-start
  0.6 2.2 %fusion.1 = (f32[4,2,5,2,1,512]{5,4,3,2,1,0:T(1,128)S(1)}, f32[4,2,5,2,1,512]{5,4,3,2,1,0:T(1,128)S(1)}) fusion(f32[4,2,5,2,8,512]{5,4,3,2,1,0:T(8,128)} %x_ref.1), kind=kLoop, calls=%fused_computation.14 | loop fusion | bytes 655360 | tf_op jit(solution)/shard_map/edge_exchange_0/slice | solution.py:226
  2.9 0.1 copy.19
  3.0 2.1 %fusion.2 = (f32[4,2,5,2,1,512]{5,4,3,2,1,0:T(1,128)S(1)}, f32[4,2,5,2,1,512]{5,4,3,2,1,0:T(1,128)S(1)}) fusion(f32[4,2,5,2,8,512]{5,4,3,2,1,0:T(8,128)} %a_ref.1), kind=kLoop, calls=%fused_computation.15 | loop fusion | bytes 655360 | tf_op jit(solution)/shard_map/edge_exchange_0/slice | solution.py:226
  5.1 0.1 copy.20
  5.3 0.0 copy-start.5
  5.3 0.1 collective-permute-start
  5.4 0.1 copy.21
  5.5 0.1 copy.22
  5.6 0.0 copy-start.6
  5.8 10.5 %collective-permute-start.1 = (f32[2,4,2,10,512]{4,3,2,1,0:T(8,128)S(1)}, f32[2,4,2,10,512]{4,3,2,1,0:T(8,128)S(1)}, u32[]{:S(2)}, u32[]{:S(2)}) collective-permute-start(f32[2,4,2,10,512]{4,3,2,1,0:T(8,128)S(1)} %pad_maximum_fusion.1), channel_id=1, source_target_pairs={{4,0},{8,4},{12,8},{16,12},{20,16},{24,20},{28,24},{32,28},{36,32}... | collective-permute-start | bytes 983048 | tf_op jit(solution)/shard_map/edge_exchange_0/ppermute | solution.py:25
  16.2 0.0 copy-done.5
  16.2 0.1 reshape.38
  16.3 0.0 copy-done
  16.3 0.6 gather_fusion
  17.0 0.1 reshape.37
  17.1 0.1 fusion.3
  17.1 0.0 copy-done.6
  17.1 0.1 fusion.5
  17.2 0.1 stack.24
  17.3 0.1 reshape.31
  17.4 0.7 pad_add_fusion.tbl
  18.1 18.1 %collective-permute-done.rlo_ref = f32[2,4,2,10,512]{4,3,2,1,0:T(8,128)S(1)} collective-permute-done((f32[2,4,2,10,512]{4,3,2,1,0:T(8,128)S(1)}, f32[2,4,2,10,512]{4,3,2,1,0:T(8,128)S(1)}, u32[]{:S(2)}, u32[]{:S(2)}) %collective-permute-start) | collective-permute-done | bytes 327712 | tf_op jit(solution)/shard_map/edge_exchange_0/ppermute | solution.py:25
  36.2 0.0 copy-start.1
  36.2 0.0 collective-permute-done.1.rhi_ref
  36.2 0.8 copy-done.1
  37.0 0.0 copy-start.2
  37.0 0.8 copy-done.2
  37.8 17.9 %flow_step_0.1 = (f32[4,2,5,2,8,512]{5,4,3,2,1,0:T(8,128)}, f32[4,2,5,2,8,512]{5,4,3,2,1,0:T(8,128)}, f32[2,8,512]{2,1,0:T(8,128)}, f32[2,4,2,10,512]{4,3,2,1,0:T(8,128)}, f32[2,4,2,10,512]{4,3,2,1,0:T(8,128)}) custom-call(s32[17]{0:T(128)} %pad_add_fusion.tbl, f32[4,2,5,2,8,512]{5,4,3,2,1,0:T(8,128)} %x_ref.1, f32[4,2,5,2,8,512]{5,4,3,2,1,0:T(8,128)} %a_ref.1, ...), custom_call_target="tpu_custom_call" | custom-call | tf_op jit(solution)/shard_map/flow_step_0/pallas_call | solution.py:216
  55.7 0.1 collective-permute-start.2
  55.8 9.9 %collective-permute-start.3 = (f32[2,4,2,10,512]{4,3,2,1,0:T(8,128)}, f32[2,4,2,10,512]{4,3,2,1,0:T(8,128)S(1)}, u32[]{:S(2)}, u32[]{:S(2)}) collective-permute-start(f32[2,4,2,10,512]{4,3,2,1,0:T(8,128)} %get-tuple-element.14), channel_id=1, source_target_pairs={{4,0},{8,4},{12,8},{16,12},{20,16},{24,20},{28,24},{32,28},{36,32}... | collective-permute-start | bytes 983048 | tf_op jit(solution)/shard_map/edge_exchange_1/ppermute | solution.py:25
  65.6 21.1 %collective-permute-done.2.rlo_ref = f32[2,4,2,10,512]{4,3,2,1,0:T(8,128)S(1)} collective-permute-done((f32[2,4,2,10,512]{4,3,2,1,0:T(8,128)}, f32[2,4,2,10,512]{4,3,2,1,0:T(8,128)S(1)}, u32[]{:S(2)}, u32[]{:S(2)}) %collective-permute-start.2) | collective-permute-done | bytes 327712 | tf_op jit(solution)/shard_map/edge_exchange_1/ppermute | solution.py:25
  86.7 0.0 copy-start.3
  86.7 0.0 collective-permute-done.3.rhi_ref
  86.7 0.0 copy-start.4
  86.7 0.8 copy-done.3
  87.5 0.2 copy-done.4
  87.6 17.6 %flow_step_1.1 = (f32[4,2,5,2,8,512]{5,4,3,2,1,0:T(8,128)}, f32[4,2,5,2,8,512]{5,4,3,2,1,0:T(8,128)}, f32[2,8,512]{2,1,0:T(8,128)}) custom-call(s32[17]{0:T(128)} %pad_add_fusion.tbl, f32[4,2,5,2,8,512]{5,4,3,2,1,0:T(8,128)} %get-tuple-element.11.x_ref, f32[4,2,5,2,8,512]{5,4,3,2,1,0:T(8,128)} %get-tuple-element.12.a_ref, f32[2,4,2,10,512]{4,3,2,1,0:T(8,128)} %copy-done.3, ...), custom_call_target="tpu_custom_call" | custom-call | tf_op jit(solution)/shard_map/flow_step_1/pallas_call | solution.py:216
  105.2 1.0 collective-permute-start.4
  106.2 2.5 %collective-permute-start.5 = (f32[2,8,512]{2,1,0:T(8,128)}, f32[2,8,512]{2,1,0:T(8,128)S(1)}, u32[]{:S(2)}, u32[]{:S(2)}) collective-permute-start(f32[2,8,512]{2,1,0:T(8,128)} %get-tuple-element.18), channel_id=1, source_target_pairs={{2,0},{3,1},{0,2},{1,3},{6,4},{7,5},{4,6},{5,7},{10,8},{11,9},{8,1... | collective-permute-start | bytes 98312 | tf_op jit(solution)/shard_map/mode_reduce/ppermute | solution.py:25
  108.8 0.0 collective-permute-start.6
  108.8 0.9 collective-permute-done.4
  109.7 1.6 %collective-permute-done.5 = f32[2,8,512]{2,1,0:T(8,128)S(1)} collective-permute-done((f32[2,8,512]{2,1,0:T(8,128)}, f32[2,8,512]{2,1,0:T(8,128)S(1)}, u32[]{:S(2)}, u32[]{:S(2)}) %collective-permute-start.5) | collective-permute-done | bytes 32800 | tf_op jit(solution)/shard_map/mode_reduce/ppermute | solution.py:25
  111.3 1.6 %collective-permute-done.6 = f32[2,8,512]{2,1,0:T(8,128)S(1)} collective-permute-done((f32[2,8,512]{2,1,0:T(8,128)}, f32[2,8,512]{2,1,0:T(8,128)S(1)}, u32[]{:S(2)}, u32[]{:S(2)}) %collective-permute-start.6) | collective-permute-done | bytes 32800 | tf_op jit(solution)/shard_map/mode_reduce/ppermute | solution.py:25
  112.9 0.8 pad_maximum_fusion.2
  113.7 0.6 multiply_bitcast_fusion
  (10 shorter events, 0.3 us)
Async XLA Ops:
  0.6 15.7 %copy-start = (s32[128]{0:T(128)S(1)}, s32[128]{0:T(128)}, u32[]{:S(2)}) copy-start(s32[128]{0:T(128)} %param.13) | copy-start | bytes 1540
  5.3 10.9 %copy-start.5 = (s32[2,4]{1,0:T(2,128)S(1)}, s32[2,4]{1,0:T(2,128)}, u32[]{:S(2)}) copy-start(s32[2,4]{1,0:T(2,128)} %param.14) | copy-start | bytes 100
  5.3 30.9 %collective-permute-start = (f32[2,4,2,10,512]{4,3,2,1,0:T(8,128)S(1)}, f32[2,4,2,10,512]{4,3,2,1,0:T(8,128)S(1)}, u32[]{:S(2)}, u32[]{:S(2)}) collective-permute-start(f32[2,4,2,10,512]{4,3,2,1,0:T(8,128)S(1)} %pad_maximum_fusion), channel_id=1, source_target_pairs={{252,0},{0,4},{4,8},{8,12},{12,16},{16,20},{20,24},{24,28},{28,32}... | collective-permute-start | bytes 983048 | tf_op jit(solution)/shard_map/edge_exchange_0/ppermute | solution.py:25
  5.6 11.5 %copy-start.6 = (s32[2,4]{1,0:T(2,128)S(1)}, s32[2,4]{1,0:T(2,128)}, u32[]{:S(2)}) copy-start(s32[2,4]{1,0:T(2,128)} %param.15) | copy-start | bytes 100
  5.8 30.4 %collective-permute-start.1 = (f32[2,4,2,10,512]{4,3,2,1,0:T(8,128)S(1)}, f32[2,4,2,10,512]{4,3,2,1,0:T(8,128)S(1)}, u32[]{:S(2)}, u32[]{:S(2)}) collective-permute-start(f32[2,4,2,10,512]{4,3,2,1,0:T(8,128)S(1)} %pad_maximum_fusion.1), channel_id=1, source_target_pairs={{4,0},{8,4},{12,8},{16,12},{20,16},{24,20},{28,24},{32,28},{36,32}... | collective-permute-start | bytes 983048 | tf_op jit(solution)/shard_map/edge_exchange_0/ppermute | solution.py:25
  36.2 0.8 copy-start.1
  37.0 0.8 copy-start.2
  55.7 31.0 %collective-permute-start.2 = (f32[2,4,2,10,512]{4,3,2,1,0:T(8,128)}, f32[2,4,2,10,512]{4,3,2,1,0:T(8,128)S(1)}, u32[]{:S(2)}, u32[]{:S(2)}) collective-permute-start(f32[2,4,2,10,512]{4,3,2,1,0:T(8,128)} %get-tuple-element.13), channel_id=1, source_target_pairs={{252,0},{0,4},{4,8},{8,12},{12,16},{16,20},{20,24},{24,28},{28,32}... | collective-permute-start | bytes 983048 | tf_op jit(solution)/shard_map/edge_exchange_1/ppermute | solution.py:25
  55.8 30.9 %collective-permute-start.3 = (f32[2,4,2,10,512]{4,3,2,1,0:T(8,128)}, f32[2,4,2,10,512]{4,3,2,1,0:T(8,128)S(1)}, u32[]{:S(2)}, u32[]{:S(2)}) collective-permute-start(f32[2,4,2,10,512]{4,3,2,1,0:T(8,128)} %get-tuple-element.14), channel_id=1, source_target_pairs={{4,0},{8,4},{12,8},{16,12},{20,16},{24,20},{28,24},{32,28},{36,32}... | collective-permute-start | bytes 983048 | tf_op jit(solution)/shard_map/edge_exchange_1/ppermute | solution.py:25
  86.7 0.8 copy-start.3
  86.7 1.0 copy-start.4
  105.2 4.5 %collective-permute-start.4 = (f32[2,8,512]{2,1,0:T(8,128)}, f32[2,8,512]{2,1,0:T(8,128)S(1)}, u32[]{:S(2)}, u32[]{:S(2)}) collective-permute-start(f32[2,8,512]{2,1,0:T(8,128)} %get-tuple-element.18), channel_id=1, source_target_pairs={{3,0},{0,1},{1,2},{2,3},{7,4},{4,5},{5,6},{6,7},{11,8},{8,9},{9,10... | collective-permute-start | bytes 98312 | tf_op jit(solution)/shard_map/mode_reduce/ppermute | solution.py:25
  106.2 5.1 %collective-permute-start.5 = (f32[2,8,512]{2,1,0:T(8,128)}, f32[2,8,512]{2,1,0:T(8,128)S(1)}, u32[]{:S(2)}, u32[]{:S(2)}) collective-permute-start(f32[2,8,512]{2,1,0:T(8,128)} %get-tuple-element.18), channel_id=1, source_target_pairs={{2,0},{3,1},{0,2},{1,3},{6,4},{7,5},{4,6},{5,7},{10,8},{11,9},{8,1... | collective-permute-start | bytes 98312 | tf_op jit(solution)/shard_map/mode_reduce/ppermute | solution.py:25
  108.8 4.1 %collective-permute-start.6 = (f32[2,8,512]{2,1,0:T(8,128)}, f32[2,8,512]{2,1,0:T(8,128)S(1)}, u32[]{:S(2)}, u32[]{:S(2)}) collective-permute-start(f32[2,8,512]{2,1,0:T(8,128)} %get-tuple-element.18), channel_id=1, source_target_pairs={{1,0},{2,1},{3,2},{0,3},{5,4},{6,5},{7,6},{4,7},{9,8},{10,9},{11,1... | collective-permute-start | bytes 98312 | tf_op jit(solution)/shard_map/mode_reduce/ppermute | solution.py:25
where the time goes:
time: 115 us; the launch traced here: 114 us
  waiting for transfers between devices  43.3 us (38%)
  Pallas kernels  35.5 us (31%)
  starting transfers between devices  24 us (21%)
  local copies, waits for them, and re-layouts  8.52 us (7%)
  other arithmetic  2.18 us (2%)
    ppermute x7, waiting for transfers between devices, shifted(): return lax.ppermute(block, axis, route)  43.3 us
    pallas_call x2, Pallas kernels, run_step(): pl.pallas_call(kernel, grid_spec=grid_spec, out_shape=out_shape, compiler...  35.5 us
    ppermute x7, starting transfers between devices, shifted(): return lax.ppermute(block, axis, route)  24 us
    slice x2, local copies, waits for them, and re-layouts, edges(): e = x[:, :, :, :, row, :]  4.31 us
    unnamed x18, local copies, waits for them, and re-layouts  2.9 us
  transfers between devices with their start and end apart: 7, of which 5 were waited for; matrix products, arithmetic and copies ran while one was open for 2% of the time, Pallas kernels for 0%

commit v1 on v0

--- a/solution.py
+++ b/solution.py
@@ -97,89 +97,117 @@
     return re, im
 
 
+LANES = 128
+
+
+def lane_reverse_into(dst, rows):
+    height = rows.shape[0]
+    chunks = rows.shape[1] // LANES
+    lane = lax.broadcasted_iota(jnp.int32, (height, LANES), 1)
+    for b in range(chunks):
+        y = rows[:, b * LANES:(b + 1) * LANES]
+        k = 1
+        while k < LANES:
+            y = jnp.where((lane & k) != 0, pltpu.roll(y, k, 1), pltpu.roll(y, LANES - k, 1))
+            k *= 2
+        c = chunks - 1 - b
+        dst[:, c * LANES:(c + 1) * LANES] = y
+
+
 def step_kernel(tbl, x_ref, a_ref, rlo_ref, rhi_ref, rho_ref, vel_ref, prs_ref, *rest, modes_total, first):
     if first:
-        xo_ref, ao_ref, sens_ref, elo_ref, ehi_ref, rev_ref = rest
+        xo_ref, ao_ref, sens_ref, elo_ref, ehi_ref, gh_ref = rest
     else:
-        sin_ref, xo_ref, ao_ref, sens_ref, rev_ref = rest
+        sin_ref, xo_ref, ao_ref, sens_ref, gh_ref = rest
     m = pl.program_id(0)
     slots = x_ref.shape[3]
     height = x_ref.shape[4]
     width = x_ref.shape[5]
-    shape = (height, width)
+    chunks = width // LANES
+    shape = (height, LANES)
 
     @pl.when(m == 0)
     def _init():
-        ri = lax.broadcasted_iota(jnp.int32, (width, width), 0)
-        ci = lax.broadcasted_iota(jnp.int32, (width, width), 1)
-        rev_ref[...] = jnp.where(ri + ci == width - 1, 1.0, 0.0).astype(jnp.float32)
         if first:
             sens_ref[...] = jnp.zeros(sens_ref.shape, jnp.float32)
         else:
             sens_ref[...] = sin_ref[...]
 
+    for s in range(slots):
+        for side, (recv, tcol, fcol) in enumerate(((rlo_ref, 0, 1), (rhi_ref, 2, 3))):
+            t = tbl[s * ENTRIES + tcol]
+            f = tbl[s * ENTRIES + fcol]
+            for arr in range(2):
+                gh_ref[arr, side, s] = recv[arr, 0, t]
+
+                @pl.when(f != 0)
+                def _turn():
+                    lane_reverse_into(gh_ref.at[arr, side, s], recv[arr, 0, t])
+
     kf = (tbl[slots * ENTRIES] + m).astype(jnp.float32)
     w = BASE_FREQ * (jnp.zeros(shape, jnp.float32) + (kf - modes_total / 2 + 0.5))
     row = lax.broadcasted_iota(jnp.int32, shape, 0)
-    col = lax.broadcasted_iota(jnp.int32, shape, 1)
+    lane = lax.broadcasted_iota(jnp.int32, shape, 1)
     zero_i = jnp.zeros(shape, jnp.int32)
-    rev = rev_ref[...]
-
-    def flip_rows(rows, flag):
-        turned = jnp.dot(rows, rev, precision=lax.Precision.HIGHEST, preferred_element_type=jnp.float32)
-        mask = (jnp.zeros(rows.shape, jnp.int32) + flag) != 0
-        return jnp.where(mask, turned, rows)
+    first_row = row == 0
+    last_row = row == height - 1
+    first_lane = lane == 0
+    last_lane = lane == LANES - 1
 
     for s in range(slots):
         base = s * ENTRIES
-        lo_t, lo_f = tbl[base + 0], tbl[base + 1]
-        hi_t, hi_f = tbl[base + 2], tbl[base + 3]
         jl_s, jl_live = tbl[base + 4], tbl[base + 5]
         jh_s, jh_live = tbl[base + 6], tbl[base + 7]
         jl_mask = (zero_i + jl_live) != 0
         jh_mask = (zero_i + jh_live) != 0
-        r = rho_ref[s]
-        ir = 1.0 / r
-        u = vel_ref[0, s]
-        v = vel_ref[1, s]
-        kp = HEAT_RATIO * prs_ref[s]
-        bf = (r, ir, u, v, kp)
-        news = []
-        for arr, (src, dst, rates) in enumerate(((x_ref, xo_ref, direct_rates), (a_ref, ao_ref, adjoint_rates))):
-            lo_rows = flip_rows(rlo_ref[arr, 0, lo_t], lo_f)
-            hi_rows = flip_rows(rhi_ref[arr, 0, hi_t], hi_f)
-            vals, dss, dcs, laps = [], [], [], []
-            for p in range(2):
-                for n in range(NV):
-                    k = p * NV + n
-                    g = src[0, p, n, s]
-                    lo_b = jnp.broadcast_to(lo_rows[k:k + 1, :], shape)
-                    hi_b = jnp.broadcast_to(hi_rows[k:k + 1, :], shape)
-                    im1 = jnp.where(row == 0, lo_b, pltpu.roll(g, 1, 0))
-                    ip1 = jnp.where(row == height - 1, hi_b, pltpu.roll(g, height - 1, 0))
-                    nl = pltpu.roll(src[0, p, n, jl_s], 1, 1)
-                    nh = pltpu.roll(src[0, p, n, jh_s], width - 1, 1)
-                    jm1 = jnp.where(col == 0, jnp.where(jl_mask, nl, 0.0), pltpu.roll(g, 1, 1))
-                    jp1 = jnp.where(col == width - 1, jnp.where(jh_mask, nh, 0.0), pltpu.roll(g, width - 1, 1))
-                    vals.append(g)
-                    dss.append((ip1 - im1) * 0.5)
-                    dcs.append((jp1 - jm1) * 0.5)
-                    laps.append(ip1 + im1 + jp1 + jm1 - 4.0 * g)
-            X, Y = vals[:NV], vals[NV:]
-            re, im = rates(bf, X, Y, dss[:NV], dcs[:NV], laps[:NV], dss[NV:], dcs[NV:], laps[NV:], w)
-            total = None
-            for p, rate in enumerate((re, im)):
-                for n in range(NV):
-                    k = p * NV + n
-                    nv = vals[k] + TIME_STEP * rate[n]
-                    dst[0, p, n, s] = nv
-                    if first:
-                        elo_ref[arr, 0, s, pl.ds(k, 1), :] = nv[0:1, :]
-                        ehi_ref[arr, 0, s, pl.ds(k, 1), :] = nv[height - 1:height, :]
-                    sq = nv * nv
-                    total = sq if total is None else total + sq
-            news.append(total / 10.0)
-        sens_ref[s] = sens_ref[s] + news[0] * news[1]
+        for b in range(chunks):
+            cs = slice(b * LANES, (b + 1) * LANES)
+            r = rho_ref[s, :, cs]
+            ir = 1.0 / r
+            u = vel_ref[0, s, :, cs]
+            v = vel_ref[1, s, :, cs]
+            kp = HEAT_RATIO * prs_ref[s, :, cs]
+            bf = (r, ir, u, v, kp)
+            means = []
+            for arr, (src, dst, rates) in enumerate(((x_ref, xo_ref, direct_rates), (a_ref, ao_ref, adjoint_rates))):
+                vals, dss, dcs, laps = [], [], [], []
+                for p in range(2):
+                    for n in range(NV):
+                        k = p * NV + n
+                        g = src[0, p, n, s, :, cs]
+                        lo_b = jnp.broadcast_to(gh_ref[arr, 0, s, k:k + 1, cs], shape)
+                        hi_b = jnp.broadcast_to(gh_ref[arr, 1, s, k:k + 1, cs], shape)
+                        im1 = jnp.where(first_row, lo_b, pltpu.roll(g, 1, 0))
+                        ip1 = jnp.where(last_row, hi_b, pltpu.roll(g, height - 1, 0))
+                        if b > 0:
+                            left = src[0, p, n, s, :, (b - 1) * LANES:b * LANES]
+                        else:
+                            left = jnp.where(jl_mask, src[0, p, n, jl_s, :, width - LANES:width], 0.0)
+                        if b < chunks - 1:
+                            right = src[0, p, n, s, :, (b + 1) * LANES:(b + 2) * LANES]
+                        else:
+                            right = jnp.where(jh_mask, src[0, p, n, jh_s, :, 0:LANES], 0.0)
+                        jm1 = jnp.where(first_lane, pltpu.roll(left, 1, 1), pltpu.roll(g, 1, 1))
+                        jp1 = jnp.where(last_lane, pltpu.roll(right, LANES - 1, 1), pltpu.roll(g, LANES - 1, 1))
+                        vals.append(g)
+                        dss.append((ip1 - im1) * 0.5)
+                        dcs.append((jp1 - jm1) * 0.5)
+                        laps.append(ip1 + im1 + jp1 + jm1 - 4.0 * g)
+                X, Y = vals[:NV], vals[NV:]
+                re, im = rates(bf, X, Y, dss[:NV], dcs[:NV], laps[:NV], dss[NV:], dcs[NV:], laps[NV:], w)
+                total = None
+                for p, rate in enumerate((re, im)):
+                    for n in range(NV):
+                        k = p * NV + n
+                        nv = vals[k] + TIME_STEP * rate[n]
+                        dst[0, p, n, s, :, cs] = nv
+                        if first:
+                            elo_ref[arr, 0, s, pl.ds(k, 1), cs] = nv[0:1, :]
+                            ehi_ref[arr, 0, s, pl.ds(k, 1), cs] = nv[height - 1:height, :]
+                        sq = nv * nv
+                        total = sq if total is None else total + sq
+                means.append(total / 10.0)
+            sens_ref[s, :, cs] = sens_ref[s, :, cs] + means[0] * means[1]
 
 
 def run_step(tbl, x, a, rlo, rhi, density, velocity, pressure, sens_in, modes_total, first):
@@ -210,7 +238,7 @@
         grid=(modes,),
         in_specs=in_specs,
         out_specs=out_specs,
-        scratch_shapes=[pltpu.VMEM((width, width), jnp.float32)],
+        scratch_shapes=[pltpu.VMEM((2, 2, slots, parts * nv, width), jnp.float32)],
     )
     kernel = functools.partial(step_kernel, modes_total=modes_total, first=first)
     return pl.pallas_call(

time: 115 us -> 120 us (1.043)
  the two profiles are of different devices: /device:TPU:32 before, /device:TPU:17 now
where the time goes in v1:
time: 120 us; the launch traced here: 118 us
  waiting for transfers between devices  45.1 us (38%)
  Pallas kernels  44.4 us (37%)
  starting transfers between devices  17.5 us (15%)
  local copies, waits for them, and re-layouts  8.35 us (7%)
  other arithmetic  2.18 us (2%)
    ppermute x7, waiting for transfers between devices, shifted(): return lax.ppermute(block, axis, route)  45.1 us
    pallas_call x2, Pallas kernels, run_step(): pl.pallas_call(kernel, grid_spec=grid_spec, out_shape=out_shape, compiler...  44.4 us
    ppermute x7, starting transfers between devices, shifted(): return lax.ppermute(block, axis, route)  17.5 us
    slice x2, local copies, waits for them, and re-layouts, edges(): e = x[:, :, :, :, row, :]  4.31 us
    unnamed x18, local copies, waits for them, and re-layouts  2.74 us
  transfers between devices with their start and end apart: 7, of which 5 were waited for; matrix products, arithmetic and copies ran while one was open for 2% of the time, Pallas kernels for 0%

profile of v1, /device:TPU:17, one launch (start us, length us, event | category | flops | bytes accessed | tf_op | source)
XLA Modules:
  0.0 118.4 jit_solution(1699697463572891934)
XLA Ops:
  0.6 0.0 copy-start
  0.6 2.2 %fusion.1 = (f32[4,2,5,2,1,512]{5,4,3,2,1,0:T(1,128)S(1)}, f32[4,2,5,2,1,512]{5,4,3,2,1,0:T(1,128)S(1)}) fusion(f32[4,2,5,2,8,512]{5,4,3,2,1,0:T(8,128)} %x_ref.1), kind=kLoop, calls=%fused_computation.14 | loop fusion | bytes 655360 | tf_op jit(solution)/shard_map/edge_exchange_0/slice | solution.py:254
  2.9 0.1 copy.19
  3.0 2.1 %fusion.2 = (f32[4,2,5,2,1,512]{5,4,3,2,1,0:T(1,128)S(1)}, f32[4,2,5,2,1,512]{5,4,3,2,1,0:T(1,128)S(1)}) fusion(f32[4,2,5,2,8,512]{5,4,3,2,1,0:T(8,128)} %a_ref.1), kind=kLoop, calls=%fused_computation.15 | loop fusion | bytes 655360 | tf_op jit(solution)/shard_map/edge_exchange_0/slice | solution.py:254
  5.1 0.1 copy.20
  5.3 0.0 copy-start.5
  5.3 7.5 %collective-permute-start = (f32[2,4,2,10,512]{4,3,2,1,0:T(8,128)S(1)}, f32[2,4,2,10,512]{4,3,2,1,0:T(8,128)S(1)}, u32[]{:S(2)}, u32[]{:S(2)}) collective-permute-start(f32[2,4,2,10,512]{4,3,2,1,0:T(8,128)S(1)} %pad_maximum_fusion), channel_id=1, source_target_pairs={{252,0},{0,4},{4,8},{8,12},{12,16},{16,20},{20,24},{24,28},{28,32}... | collective-permute-start | bytes 983048 | tf_op jit(solution)/shard_map/edge_exchange_0/ppermute | solution.py:25
  12.9 0.1 copy.21
  13.0 0.1 copy.22
  13.1 0.0 copy-start.6
  13.2 0.1 collective-permute-start.1
  13.3 0.0 copy-done.5
  13.3 0.1 reshape.38
  13.4 0.0 copy-done
  13.4 0.6 gather_fusion
  14.1 0.1 reshape.37
  14.2 0.1 fusion.3
  14.2 0.0 copy-done.6
  14.2 0.1 fusion.5
  14.3 0.1 stack.24
  14.4 0.1 reshape.31
  14.5 0.7 pad_add_fusion.tbl
  15.2 20.2 %collective-permute-done.rlo_ref = f32[2,4,2,10,512]{4,3,2,1,0:T(8,128)S(1)} collective-permute-done((f32[2,4,2,10,512]{4,3,2,1,0:T(8,128)S(1)}, f32[2,4,2,10,512]{4,3,2,1,0:T(8,128)S(1)}, u32[]{:S(2)}, u32[]{:S(2)}) %collective-permute-start) | collective-permute-done | bytes 327712 | tf_op jit(solution)/shard_map/edge_exchange_0/ppermute | solution.py:25
  35.4 0.0 copy-start.1
  35.4 0.0 collective-permute-done.1.rhi_ref
  35.4 0.8 copy-done.1
  36.2 0.0 copy-start.2
  36.2 0.8 copy-done.2
  36.9 22.3 %flow_step_0.1 = (f32[4,2,5,2,8,512]{5,4,3,2,1,0:T(8,128)}, f32[4,2,5,2,8,512]{5,4,3,2,1,0:T(8,128)}, f32[2,8,512]{2,1,0:T(8,128)}, f32[2,4,2,10,512]{4,3,2,1,0:T(8,128)}, f32[2,4,2,10,512]{4,3,2,1,0:T(8,128)}) custom-call(s32[17]{0:T(128)} %pad_add_fusion.tbl, f32[4,2,5,2,8,512]{5,4,3,2,1,0:T(8,128)} %x_ref.1, f32[4,2,5,2,8,512]{5,4,3,2,1,0:T(8,128)} %a_ref.1, ...), custom_call_target="tpu_custom_call" | custom-call | tf_op jit(solution)/shard_map/flow_step_0/pallas_call | solution.py:244
  59.2 6.6 %collective-permute-start.2 = (f32[2,4,2,10,512]{4,3,2,1,0:T(8,128)}, f32[2,4,2,10,512]{4,3,2,1,0:T(8,128)S(1)}, u32[]{:S(2)}, u32[]{:S(2)}) collective-permute-start(f32[2,4,2,10,512]{4,3,2,1,0:T(8,128)} %get-tuple-element.13), channel_id=1, source_target_pairs={{252,0},{0,4},{4,8},{8,12},{12,16},{16,20},{20,24},{24,28},{28,32}... | collective-permute-start | bytes 983048 | tf_op jit(solution)/shard_map/edge_exchange_1/ppermute | solution.py:25
  65.8 0.0 collective-permute-start.3
  65.8 17.5 %collective-permute-done.2.rlo_ref = f32[2,4,2,10,512]{4,3,2,1,0:T(8,128)S(1)} collective-permute-done((f32[2,4,2,10,512]{4,3,2,1,0:T(8,128)}, f32[2,4,2,10,512]{4,3,2,1,0:T(8,128)S(1)}, u32[]{:S(2)}, u32[]{:S(2)}) %collective-permute-start.2) | collective-permute-done | bytes 327712 | tf_op jit(solution)/shard_map/edge_exchange_1/ppermute | solution.py:25
  83.3 0.0 copy-start.3
  83.3 5.6 %collective-permute-done.3.rhi_ref = f32[2,4,2,10,512]{4,3,2,1,0:T(8,128)S(1)} collective-permute-done((f32[2,4,2,10,512]{4,3,2,1,0:T(8,128)}, f32[2,4,2,10,512]{4,3,2,1,0:T(8,128)S(1)}, u32[]{:S(2)}, u32[]{:S(2)}) %collective-permute-start.3) | collective-permute-done | bytes 327712 | tf_op jit(solution)/shard_map/edge_exchange_1/ppermute | solution.py:25
  88.9 0.0 copy-start.4
  88.9 0.0 copy-done.3
  88.9 0.8 copy-done.4
  89.7 22.1 %flow_step_1.1 = (f32[4,2,5,2,8,512]{5,4,3,2,1,0:T(8,128)}, f32[4,2,5,2,8,512]{5,4,3,2,1,0:T(8,128)}, f32[2,8,512]{2,1,0:T(8,128)}) custom-call(s32[17]{0:T(128)} %pad_add_fusion.tbl, f32[4,2,5,2,8,512]{5,4,3,2,1,0:T(8,128)} %get-tuple-element.11.x_ref, f32[4,2,5,2,8,512]{5,4,3,2,1,0:T(8,128)} %get-tuple-element.12.a_ref, f32[2,4,2,10,512]{4,3,2,1,0:T(8,128)} %copy-done.3, ...), custom_call_target="tpu_custom_call" | custom-call | tf_op jit(solution)/shard_map/flow_step_1/pallas_call | solution.py:244
  111.8 0.1 collective-permute-start.4
  111.9 0.1 collective-permute-start.5
  112.0 3.2 %collective-permute-start.6 = (f32[2,8,512]{2,1,0:T(8,128)}, f32[2,8,512]{2,1,0:T(8,128)S(1)}, u32[]{:S(2)}, u32[]{:S(2)}) collective-permute-start(f32[2,8,512]{2,1,0:T(8,128)} %get-tuple-element.18), channel_id=1, source_target_pairs={{1,0},{2,1},{3,2},{0,3},{5,4},{6,5},{7,6},{4,7},{9,8},{10,9},{11,1... | collective-permute-start | bytes 98312 | tf_op jit(solution)/shard_map/mode_reduce/ppermute | solution.py:25
  115.1 1.5 %collective-permute-done.4 = f32[2,8,512]{2,1,0:T(8,128)S(1)} collective-permute-done((f32[2,8,512]{2,1,0:T(8,128)}, f32[2,8,512]{2,1,0:T(8,128)S(1)}, u32[]{:S(2)}, u32[]{:S(2)}) %collective-permute-start.4) | collective-permute-done | bytes 32800 | tf_op jit(solution)/shard_map/mode_reduce/ppermute | solution.py:25
  116.6 0.0 collective-permute-done.5
  116.6 0.3 collective-permute-done.6
  117.0 0.8 pad_maximum_fusion.2
  117.8 0.6 multiply_bitcast_fusion
  (10 shorter events, 0.3 us)
Async XLA Ops:
  0.6 12.8 %copy-start = (s32[128]{0:T(128)S(1)}, s32[128]{0:T(128)}, u32[]{:S(2)}) copy-start(s32[128]{0:T(128)} %param.13) | copy-start | bytes 1540
  5.3 8.0 %copy-start.5 = (s32[2,4]{1,0:T(2,128)S(1)}, s32[2,4]{1,0:T(2,128)}, u32[]{:S(2)}) copy-start(s32[2,4]{1,0:T(2,128)} %param.14) | copy-start | bytes 100
  5.3 30.0 %collective-permute-start = (f32[2,4,2,10,512]{4,3,2,1,0:T(8,128)S(1)}, f32[2,4,2,10,512]{4,3,2,1,0:T(8,128)S(1)}, u32[]{:S(2)}, u32[]{:S(2)}) collective-permute-start(f32[2,4,2,10,512]{4,3,2,1,0:T(8,128)S(1)} %pad_maximum_fusion), channel_id=1, source_target_pairs={{252,0},{0,4},{4,8},{8,12},{12,16},{16,20},{20,24},{24,28},{28,32}... | collective-permute-start | bytes 983048 | tf_op jit(solution)/shard_map/edge_exchange_0/ppermute | solution.py:25
  13.1 1.2 copy-start.6
  13.2 22.2 %collective-permute-start.1 = (f32[2,4,2,10,512]{4,3,2,1,0:T(8,128)S(1)}, f32[2,4,2,10,512]{4,3,2,1,0:T(8,128)S(1)}, u32[]{:S(2)}, u32[]{:S(2)}) collective-permute-start(f32[2,4,2,10,512]{4,3,2,1,0:T(8,128)S(1)} %pad_maximum_fusion.1), channel_id=1, source_target_pairs={{4,0},{8,4},{12,8},{16,12},{20,16},{24,20},{28,24},{32,28},{36,32}... | collective-permute-start | bytes 983048 | tf_op jit(solution)/shard_map/edge_exchange_0/ppermute | solution.py:25
  35.4 0.8 copy-start.1
  36.2 0.8 copy-start.2
  59.2 24.1 %collective-permute-start.2 = (f32[2,4,2,10,512]{4,3,2,1,0:T(8,128)}, f32[2,4,2,10,512]{4,3,2,1,0:T(8,128)S(1)}, u32[]{:S(2)}, u32[]{:S(2)}) collective-permute-start(f32[2,4,2,10,512]{4,3,2,1,0:T(8,128)} %get-tuple-element.13), channel_id=1, source_target_pairs={{252,0},{0,4},{4,8},{8,12},{12,16},{16,20},{20,24},{24,28},{28,32}... | collective-permute-start | bytes 983048 | tf_op jit(solution)/shard_map/edge_exchange_1/ppermute | solution.py:25
  65.8 23.0 %collective-permute-start.3 = (f32[2,4,2,10,512]{4,3,2,1,0:T(8,128)}, f32[2,4,2,10,512]{4,3,2,1,0:T(8,128)S(1)}, u32[]{:S(2)}, u32[]{:S(2)}) collective-permute-start(f32[2,4,2,10,512]{4,3,2,1,0:T(8,128)} %get-tuple-element.14), channel_id=1, source_target_pairs={{4,0},{8,4},{12,8},{16,12},{20,16},{24,20},{28,24},{32,28},{36,32}... | collective-permute-start | bytes 983048 | tf_op jit(solution)/shard_map/edge_exchange_1/ppermute | solution.py:25
  83.3 5.6 %copy-start.3 = (f32[2,4,2,10,512]{4,3,2,1,0:T(8,128)}, f32[2,4,2,10,512]{4,3,2,1,0:T(8,128)S(1)}, u32[]{:S(2)}) copy-start(f32[2,4,2,10,512]{4,3,2,1,0:T(8,128)S(1)} %collective-permute-done.2.rlo_ref) | copy-start | bytes 983044
  88.9 0.8 copy-start.4
  111.8 4.8 %collective-permute-start.4 = (f32[2,8,512]{2,1,0:T(8,128)}, f32[2,8,512]{2,1,0:T(8,128)S(1)}, u32[]{:S(2)}, u32[]{:S(2)}) collective-permute-start(f32[2,8,512]{2,1,0:T(8,128)} %get-tuple-element.18), channel_id=1, source_target_pairs={{3,0},{0,1},{1,2},{2,3},{7,4},{4,5},{5,6},{6,7},{11,8},{8,9},{9,10... | collective-permute-start | bytes 98312 | tf_op jit(solution)/shard_map/mode_reduce/ppermute | solution.py:25
  111.9 4.8 %collective-permute-start.5 = (f32[2,8,512]{2,1,0:T(8,128)}, f32[2,8,512]{2,1,0:T(8,128)S(1)}, u32[]{:S(2)}, u32[]{:S(2)}) collective-permute-start(f32[2,8,512]{2,1,0:T(8,128)} %get-tuple-element.18), channel_id=1, source_target_pairs={{2,0},{3,1},{0,2},{1,3},{6,4},{7,5},{4,6},{5,7},{10,8},{11,9},{8,1... | collective-permute-start | bytes 98312 | tf_op jit(solution)/shard_map/mode_reduce/ppermute | solution.py:25
  112.0 5.0 %collective-permute-start.6 = (f32[2,8,512]{2,1,0:T(8,128)}, f32[2,8,512]{2,1,0:T(8,128)S(1)}, u32[]{:S(2)}, u32[]{:S(2)}) collective-permute-start(f32[2,8,512]{2,1,0:T(8,128)} %get-tuple-element.18), channel_id=1, source_target_pairs={{1,0},{2,1},{3,2},{0,3},{5,4},{6,5},{7,6},{4,7},{9,8},{10,9},{11,1... | collective-permute-start | bytes 98312 | tf_op jit(solution)/shard_map/mode_reduce/ppermute | solution.py:25

commit v2 on v1

--- a/solution.py
+++ b/solution.py
@@ -100,21 +100,7 @@
 LANES = 128
 
 
-def lane_reverse_into(dst, rows):
-    height = rows.shape[0]
-    chunks = rows.shape[1] // LANES
-    lane = lax.broadcasted_iota(jnp.int32, (height, LANES), 1)
-    for b in range(chunks):
-        y = rows[:, b * LANES:(b + 1) * LANES]
-        k = 1
-        while k < LANES:
-            y = jnp.where((lane & k) != 0, pltpu.roll(y, k, 1), pltpu.roll(y, LANES - k, 1))
-            k *= 2
-        c = chunks - 1 - b
-        dst[:, c * LANES:(c + 1) * LANES] = y
-
-
-def step_kernel(tbl, x_ref, a_ref, rlo_ref, rhi_ref, rho_ref, vel_ref, prs_ref, *rest, modes_total, first):
+def step_kernel(tbl, x_ref, a_ref, recv_ref, turn_ref, rho_ref, vel_ref, prs_ref, *rest, modes_total, first):
     if first:
         xo_ref, ao_ref, sens_ref, elo_ref, ehi_ref, gh_ref = rest
     else:
@@ -125,6 +111,7 @@
     width = x_ref.shape[5]
     chunks = width // LANES
     shape = (height, LANES)
+    full = (height, width)
 
     @pl.when(m == 0)
     def _init():
@@ -134,15 +121,14 @@
             sens_ref[...] = sin_ref[...]
 
     for s in range(slots):
-        for side, (recv, tcol, fcol) in enumerate(((rlo_ref, 0, 1), (rhi_ref, 2, 3))):
+        for side, (tcol, fcol) in enumerate(((0, 1), (2, 3))):
             t = tbl[s * ENTRIES + tcol]
             f = tbl[s * ENTRIES + fcol]
             for arr in range(2):
-                gh_ref[arr, side, s] = recv[arr, 0, t]
-
-                @pl.when(f != 0)
-                def _turn():
-                    lane_reverse_into(gh_ref.at[arr, side, s], recv[arr, 0, t])
+                plain = recv_ref[side, arr, 0, t]
+                turned = turn_ref[side, arr, 0, t]
+                flag = (jnp.zeros(plain.shape, jnp.int32) + f) != 0
+                gh_ref[arr, side, s] = jnp.where(flag, turned, plain)
 
     kf = (tbl[slots * ENTRIES] + m).astype(jnp.float32)
     w = BASE_FREQ * (jnp.zeros(shape, jnp.float32) + (kf - modes_total / 2 + 0.5))
@@ -153,7 +139,6 @@
     last_row = row == height - 1
     first_lane = lane == 0
     last_lane = lane == LANES - 1
-
     for s in range(slots):
         base = s * ENTRIES
         jl_s, jl_live = tbl[base + 4], tbl[base + 5]
@@ -210,16 +195,17 @@
             sens_ref[s, :, cs] = sens_ref[s, :, cs] + means[0] * means[1]
 
 
-def run_step(tbl, x, a, rlo, rhi, density, velocity, pressure, sens_in, modes_total, first):
+def run_step(tbl, x, a, recv, turned, density, velocity, pressure, sens_in, modes_total, first):
     modes, parts, nv, slots, height, width = x.shape
     state_block = (1, parts, nv, slots, height, width)
     edge_block = (2, 1, slots, parts * nv, width)
     state_spec = pl.BlockSpec(state_block, lambda m, t: (m, 0, 0, 0, 0, 0))
     edge_spec = pl.BlockSpec(edge_block, lambda m, t: (0, m, 0, 0, 0))
+    both_spec = pl.BlockSpec((2,) + edge_block, lambda m, t: (0, 0, m, 0, 0, 0))
     flow_spec = pl.BlockSpec((slots, height, width), lambda m, t: (0, 0, 0))
     vel_spec = pl.BlockSpec((2, slots, height, width), lambda m, t: (0, 0, 0, 0))
-    in_specs = [state_spec, state_spec, edge_spec, edge_spec, flow_spec, vel_spec, flow_spec]
-    args = [x, a, rlo, rhi, density, velocity, pressure]
+    in_specs = [state_spec, state_spec, both_spec, both_spec, flow_spec, vel_spec, flow_spec]
+    args = [x, a, recv, turned, density, velocity, pressure]
     if not first:
         in_specs.append(flow_spec)
         args.append(sens_in)
@@ -238,7 +224,9 @@
         grid=(modes,),
         in_specs=in_specs,
         out_specs=out_specs,
-        scratch_shapes=[pltpu.VMEM((2, 2, slots, parts * nv, width), jnp.float32)],
+        scratch_shapes=[
+            pltpu.VMEM((2, 2, slots, parts * nv, width), jnp.float32),
+        ],
     )
     kernel = functools.partial(step_kernel, modes_total=modes_total, first=first)
     return pl.pallas_call(
@@ -247,6 +235,16 @@
         out_shape=out_shape,
         compiler_params=pltpu.CompilerParams(dimension_semantics=("arbitrary",)),
     )(tbl, *args)
+
+
+def reverse_lanes(rows):
+    width = rows.shape[-1]
+    ri = lax.broadcasted_iota(jnp.int32, (width, width), 0)
+    ci = lax.broadcasted_iota(jnp.int32, (width, width), 1)
+    turn = jnp.where(ri + ci == width - 1, 1.0, 0.0).astype(jnp.float32)
+    flat = rows.reshape(-1, width)
+    out = jnp.dot(flat, turn, precision=lax.Precision.HIGHEST, preferred_element_type=jnp.float32)
+    return out.reshape(rows.shape)
 
 
 def edges(x, row):
@@ -274,18 +272,18 @@
     with jax.named_scope("edge_exchange_0"):
         up = jnp.stack([edges(direct, height - 1), edges(adjoint, height - 1)])
         down = jnp.stack([edges(direct, 0), edges(adjoint, 0)])
-        rlo = shifted(up, "blk", 1)
-        rhi = shifted(down, "blk", -1)
+        recv = jnp.stack([shifted(up, "blk", 1), shifted(down, "blk", -1)])
+        turned = reverse_lanes(recv)
     with jax.named_scope("flow_step_0"):
         q1, a1, sens, elo, ehi = run_step(
-            table, direct, adjoint, rlo, rhi, density, velocity, pressure, None, modes_total, True
+            table, direct, adjoint, recv, turned, density, velocity, pressure, None, modes_total, True
         )
     with jax.named_scope("edge_exchange_1"):
-        rlo = shifted(ehi, "blk", 1)
-        rhi = shifted(elo, "blk", -1)
+        recv = jnp.stack([shifted(ehi, "blk", 1), shifted(elo, "blk", -1)])
+        turned = reverse_lanes(recv)
     with jax.named_scope("flow_step_1"):
         q2, a2, sens = run_step(
-            table, q1, a1, rlo, rhi, density, velocity, pressure, sens, modes_total, False
+            table, q1, a1, recv, turned, density, velocity, pressure, sens, modes_total, False
         )
     with jax.named_scope("mode_reduce"):
         count = lax.axis_size("mode")

time: 120 us -> 104 us (0.87)
  the two profiles are of different devices: /device:TPU:17 before, /device:TPU:32 now
where the time goes in v2:
time: 104 us; the launch traced here: 103 us
  waiting for transfers between devices  48 us (46%)
  starting transfers between devices  24.9 us (24%)
  Pallas kernels  14 us (13%)
  local copies, waits for them, and re-layouts  5.81 us (6%)
  matrix products  5.51 us (5%)
  other arithmetic  4.29 us (4%)
    ppermute x7, waiting for transfers between devices, shifted(): return lax.ppermute(block, axis, route)  48 us
    ppermute x7, starting transfers between devices, shifted(): return lax.ppermute(block, axis, route)  24.9 us
    pallas_call x2, Pallas kernels, run_step(): pl.pallas_call(kernel, grid_spec=grid_spec, out_shape=out_shape, compiler...  14 us
    dot_general x2, matrix products, reverse_lanes(): jnp.dot(flat, turn, precision=lax.Precision.HIGHEST, preferred_element_ty...  5.51 us
    slice x2, local copies, waits for them, and re-layouts, edges(): e = x[:, :, :, :, row, :]  4.14 us
  transfers between devices with their start and end apart: 7, of which 5 were waited for; matrix products, arithmetic and copies ran while one was open for 2% of the time, Pallas kernels for 0%

profile of v2, /device:TPU:32, one launch (start us, length us, event | category | flops | bytes accessed | tf_op | source)
XLA Modules:
  0.0 103.3 jit_solution(6807535421308796965)
XLA Ops:
  0.6 0.0 copy-start
  0.6 2.1 %fusion.19 = (f32[4,2,5,2,1,512]{5,4,3,2,1,0:T(1,128)S(1)}, f32[4,2,5,2,1,512]{5,4,3,2,1,0:T(1,128)S(1)}) fusion(f32[4,2,5,2,8,512]{5,4,3,2,1,0:T(8,128)} %x_ref.1), kind=kLoop, calls=%fused_computation.35 | loop fusion | bytes 655360 | tf_op jit(solution)/shard_map/edge_exchange_0/slice | solution.py:252
  2.7 0.1 copy.22
  2.9 2.0 %fusion.20 = (f32[4,2,5,2,1,512]{5,4,3,2,1,0:T(1,128)S(1)}, f32[4,2,5,2,1,512]{5,4,3,2,1,0:T(1,128)S(1)}) fusion(f32[4,2,5,2,8,512]{5,4,3,2,1,0:T(8,128)} %a_ref.1), kind=kLoop, calls=%fused_computation.36 | loop fusion | bytes 655360 | tf_op jit(solution)/shard_map/edge_exchange_0/slice | solution.py:252
  4.9 0.1 copy.23
  5.1 0.0 copy-start.1
  5.1 10.5 %collective-permute-start.1 = (f32[2,4,2,10,512]{4,3,2,1,0:T(8,128)S(1)}, f32[2,4,2,10,512]{4,3,2,1,0:T(8,128)S(1)}, u32[]{:S(2)}, u32[]{:S(2)}) collective-permute-start(f32[2,4,2,10,512]{4,3,2,1,0:T(8,128)S(1)} %pad_maximum_fusion.3), channel_id=1, source_target_pairs={{4,0},{8,4},{12,8},{16,12},{20,16},{24,20},{28,24},{32,28},{36,32}... | collective-permute-start | bytes 983048 | tf_op jit(solution)/shard_map/edge_exchange_0/ppermute | solution.py:25
  15.6 0.1 copy.20
  15.7 0.1 copy.21
  15.8 0.0 copy-start.2
  15.9 0.1 collective-permute-start
  16.0 0.0 copy-done.1
  16.1 0.1 reshape.46
  16.2 0.0 copy-done
  16.2 0.6 gather_fusion
  16.8 0.1 reshape.45
  16.9 0.1 fusion.21
  17.0 0.0 copy-done.2
  17.0 0.1 fusion.23
  17.0 0.1 stack.42
  17.2 0.1 reshape.39
  17.2 0.6 pad_add_fusion.tbl
  17.8 16.9 %collective-permute-done.1 = f32[2,4,2,10,512]{4,3,2,1,0:T(8,128)S(1)} collective-permute-done((f32[2,4,2,10,512]{4,3,2,1,0:T(8,128)S(1)}, f32[2,4,2,10,512]{4,3,2,1,0:T(8,128)S(1)}, u32[]{:S(2)}, u32[]{:S(2)}) %collective-permute-start.1) | collective-permute-done | bytes 327712 | tf_op jit(solution)/shard_map/edge_exchange_0/ppermute | solution.py:25
  34.8 4.7 %collective-permute-done = f32[2,4,2,10,512]{4,3,2,1,0:T(8,128)S(1)} collective-permute-done((f32[2,4,2,10,512]{4,3,2,1,0:T(8,128)S(1)}, f32[2,4,2,10,512]{4,3,2,1,0:T(8,128)S(1)}, u32[]{:S(2)}, u32[]{:S(2)}) %collective-permute-start) | collective-permute-done | bytes 327712 | tf_op jit(solution)/shard_map/edge_exchange_0/ppermute | solution.py:25
  39.4 2.8 %fusion.2.turn_ref = f32[2,2,4,2,10,512]{5,4,3,2,1,0:T(8,128)} fusion(f32[1,2,4,2,10,512]{5,4,3,2,1,0:T(8,128)S(1)} %bitcast.42, f32[1,2,4,2,10,512]{5,4,3,2,1,0:T(8,128)S(1)} %bitcast.44), kind=kOutput, calls=%fused_computation.5 | convolution fusion | flops 1007583232 | bytes 1310720 | tf_op jit(solution)/shard_map/edge_exchange_0/dot_general | solution.py:246
  42.2 1.1 %pad_maximum_fusion.recv_ref = f32[2,2,4,2,10,512]{5,4,3,2,1,0:T(8,128)} fusion(f32[1,2,4,2,10,512]{5,4,3,2,1,0:T(8,128)S(1)} %bitcast.43, f32[1,2,4,2,10,512]{5,4,3,2,1,0:T(8,128)S(1)} %bitcast.45), kind=kLoop, calls=%fused_computation.1 | loop fusion | flops 163840 | bytes 1310720 | tf_op jit(solution)/shard_map/edge_exchange_0/stack | solution.py:275
  43.3 7.1 %flow_step_0.1 = (f32[4,2,5,2,8,512]{5,4,3,2,1,0:T(8,128)}, f32[4,2,5,2,8,512]{5,4,3,2,1,0:T(8,128)}, f32[2,8,512]{2,1,0:T(8,128)}, f32[2,4,2,10,512]{4,3,2,1,0:T(8,128)}, f32[2,4,2,10,512]{4,3,2,1,0:T(8,128)}) custom-call(s32[17]{0:T(128)} %pad_add_fusion.tbl, f32[4,2,5,2,8,512]{5,4,3,2,1,0:T(8,128)} %x_ref.1, f32[4,2,5,2,8,512]{5,4,3,2,1,0:T(8,128)} %a_ref.1, ...), custom_call_target="tpu_custom_call" | custom-call | tf_op jit(solution)/shard_map/flow_step_0/pallas_call | solution.py:232
  50.4 0.1 collective-permute-start.2
  50.5 9.9 %collective-permute-start.3 = (f32[2,4,2,10,512]{4,3,2,1,0:T(8,128)}, f32[2,4,2,10,512]{4,3,2,1,0:T(8,128)S(1)}, u32[]{:S(2)}, u32[]{:S(2)}) collective-permute-start(f32[2,4,2,10,512]{4,3,2,1,0:T(8,128)} %get-tuple-element.14), channel_id=1, source_target_pairs={{4,0},{8,4},{12,8},{16,12},{20,16},{24,20},{28,24},{32,28},{36,32}... | collective-permute-start | bytes 983048 | tf_op jit(solution)/shard_map/edge_exchange_1/ppermute | solution.py:25
  60.3 22.3 %collective-permute-done.2 = f32[2,4,2,10,512]{4,3,2,1,0:T(8,128)S(1)} collective-permute-done((f32[2,4,2,10,512]{4,3,2,1,0:T(8,128)}, f32[2,4,2,10,512]{4,3,2,1,0:T(8,128)S(1)}, u32[]{:S(2)}, u32[]{:S(2)}) %collective-permute-start.2) | collective-permute-done | bytes 327712 | tf_op jit(solution)/shard_map/edge_exchange_1/ppermute | solution.py:25
  82.6 0.0 collective-permute-done.3
  82.6 2.8 %fusion.turn_ref = f32[2,2,4,2,10,512]{5,4,3,2,1,0:T(8,128)} fusion(f32[1,2,4,2,10,512]{5,4,3,2,1,0:T(8,128)S(1)} %bitcast.48, f32[1,2,4,2,10,512]{5,4,3,2,1,0:T(8,128)S(1)} %bitcast.46), kind=kOutput, calls=%fused_computation.3 | convolution fusion | flops 1007583232 | bytes 1310720 | tf_op jit(solution)/shard_map/edge_exchange_1/dot_general | solution.py:246
  85.4 1.1 %pad_maximum_fusion.1.recv_ref = f32[2,2,4,2,10,512]{5,4,3,2,1,0:T(8,128)} fusion(f32[1,2,4,2,10,512]{5,4,3,2,1,0:T(8,128)S(1)} %bitcast.49, f32[1,2,4,2,10,512]{5,4,3,2,1,0:T(8,128)S(1)} %bitcast.47), kind=kLoop, calls=%fused_computation.2 | loop fusion | flops 163840 | bytes 1310720 | tf_op jit(solution)/shard_map/edge_exchange_1/stack | solution.py:282
  86.5 6.8 %flow_step_1.1 = (f32[4,2,5,2,8,512]{5,4,3,2,1,0:T(8,128)}, f32[4,2,5,2,8,512]{5,4,3,2,1,0:T(8,128)}, f32[2,8,512]{2,1,0:T(8,128)}) custom-call(s32[17]{0:T(128)} %pad_add_fusion.tbl, f32[4,2,5,2,8,512]{5,4,3,2,1,0:T(8,128)} %get-tuple-element.11.x_ref, f32[4,2,5,2,8,512]{5,4,3,2,1,0:T(8,128)} %get-tuple-element.12.a_ref, ...), custom_call_target="tpu_custom_call" | custom-call | tf_op jit(solution)/shard_map/flow_step_1/pallas_call | solution.py:232
  93.3 0.1 collective-permute-start.4
  93.4 4.3 %collective-permute-start.5 = (f32[2,8,512]{2,1,0:T(8,128)}, f32[2,8,512]{2,1,0:T(8,128)S(1)}, u32[]{:S(2)}, u32[]{:S(2)}) collective-permute-start(f32[2,8,512]{2,1,0:T(8,128)} %get-tuple-element.18), channel_id=1, source_target_pairs={{2,0},{3,1},{0,2},{1,3},{6,4},{7,5},{4,6},{5,7},{10,8},{11,9},{8,1... | collective-permute-start | bytes 98312 | tf_op jit(solution)/shard_map/mode_reduce/ppermute | solution.py:25
  97.7 0.0 collective-permute-start.6
  97.7 0.0 collective-permute-done.4
  97.7 2.4 %collective-permute-done.5 = f32[2,8,512]{2,1,0:T(8,128)S(1)} collective-permute-done((f32[2,8,512]{2,1,0:T(8,128)}, f32[2,8,512]{2,1,0:T(8,128)S(1)}, u32[]{:S(2)}, u32[]{:S(2)}) %collective-permute-start.5) | collective-permute-done | bytes 32800 | tf_op jit(solution)/shard_map/mode_reduce/ppermute | solution.py:25
  100.2 1.7 %collective-permute-done.6 = f32[2,8,512]{2,1,0:T(8,128)S(1)} collective-permute-done((f32[2,8,512]{2,1,0:T(8,128)}, f32[2,8,512]{2,1,0:T(8,128)S(1)}, u32[]{:S(2)}, u32[]{:S(2)}) %collective-permute-start.6) | collective-permute-done | bytes 32800 | tf_op jit(solution)/shard_map/mode_reduce/ppermute | solution.py:25
  101.8 0.8 pad_maximum_fusion.4
  102.6 0.6 multiply_bitcast_fusion
  (10 shorter events, 0.3 us)
Async XLA Ops:
  0.6 15.5 %copy-start = (s32[128]{0:T(128)S(1)}, s32[128]{0:T(128)}, u32[]{:S(2)}) copy-start(s32[128]{0:T(128)} %param.13) | copy-start | bytes 1540
  5.1 10.9 %copy-start.1 = (s32[2,4]{1,0:T(2,128)S(1)}, s32[2,4]{1,0:T(2,128)}, u32[]{:S(2)}) copy-start(s32[2,4]{1,0:T(2,128)} %param.14) | copy-start | bytes 100
  5.1 29.6 %collective-permute-start.1 = (f32[2,4,2,10,512]{4,3,2,1,0:T(8,128)S(1)}, f32[2,4,2,10,512]{4,3,2,1,0:T(8,128)S(1)}, u32[]{:S(2)}, u32[]{:S(2)}) collective-permute-start(f32[2,4,2,10,512]{4,3,2,1,0:T(8,128)S(1)} %pad_maximum_fusion.3), channel_id=1, source_target_pairs={{4,0},{8,4},{12,8},{16,12},{20,16},{24,20},{28,24},{32,28},{36,32}... | collective-permute-start | bytes 983048 | tf_op jit(solution)/shard_map/edge_exchange_0/ppermute | solution.py:25
  15.8 1.2 %copy-start.2 = (s32[2,4]{1,0:T(2,128)S(1)}, s32[2,4]{1,0:T(2,128)}, u32[]{:S(2)}) copy-start(s32[2,4]{1,0:T(2,128)} %param.15) | copy-start | bytes 100
  15.9 23.5 %collective-permute-start = (f32[2,4,2,10,512]{4,3,2,1,0:T(8,128)S(1)}, f32[2,4,2,10,512]{4,3,2,1,0:T(8,128)S(1)}, u32[]{:S(2)}, u32[]{:S(2)}) collective-permute-start(f32[2,4,2,10,512]{4,3,2,1,0:T(8,128)S(1)} %pad_maximum_fusion.2), channel_id=1, source_target_pairs={{252,0},{0,4},{4,8},{8,12},{12,16},{16,20},{20,24},{24,28},{28,32}... | collective-permute-start | bytes 983048 | tf_op jit(solution)/shard_map/edge_exchange_0/ppermute | solution.py:25
  50.4 32.2 %collective-permute-start.2 = (f32[2,4,2,10,512]{4,3,2,1,0:T(8,128)}, f32[2,4,2,10,512]{4,3,2,1,0:T(8,128)S(1)}, u32[]{:S(2)}, u32[]{:S(2)}) collective-permute-start(f32[2,4,2,10,512]{4,3,2,1,0:T(8,128)} %get-tuple-element.13), channel_id=1, source_target_pairs={{252,0},{0,4},{4,8},{8,12},{12,16},{16,20},{20,24},{24,28},{28,32}... | collective-permute-start | bytes 983048 | tf_op jit(solution)/shard_map/edge_exchange_1/ppermute | solution.py:25
  50.5 32.1 %collective-permute-start.3 = (f32[2,4,2,10,512]{4,3,2,1,0:T(8,128)}, f32[2,4,2,10,512]{4,3,2,1,0:T(8,128)S(1)}, u32[]{:S(2)}, u32[]{:S(2)}) collective-permute-start(f32[2,4,2,10,512]{4,3,2,1,0:T(8,128)} %get-tuple-element.14), channel_id=1, source_target_pairs={{4,0},{8,4},{12,8},{16,12},{20,16},{24,20},{28,24},{32,28},{36,32}... | collective-permute-start | bytes 983048 | tf_op jit(solution)/shard_map/edge_exchange_1/ppermute | solution.py:25
  93.3 4.4 %collective-permute-start.4 = (f32[2,8,512]{2,1,0:T(8,128)}, f32[2,8,512]{2,1,0:T(8,128)S(1)}, u32[]{:S(2)}, u32[]{:S(2)}) collective-permute-start(f32[2,8,512]{2,1,0:T(8,128)} %get-tuple-element.18), channel_id=1, source_target_pairs={{3,0},{0,1},{1,2},{2,3},{7,4},{4,5},{5,6},{6,7},{11,8},{8,9},{9,10... | collective-permute-start | bytes 98312 | tf_op jit(solution)/shard_map/mode_reduce/ppermute | solution.py:25
  93.4 6.8 %collective-permute-start.5 = (f32[2,8,512]{2,1,0:T(8,128)}, f32[2,8,512]{2,1,0:T(8,128)S(1)}, u32[]{:S(2)}, u32[]{:S(2)}) collective-permute-start(f32[2,8,512]{2,1,0:T(8,128)} %get-tuple-element.18), channel_id=1, source_target_pairs={{2,0},{3,1},{0,2},{1,3},{6,4},{7,5},{4,6},{5,7},{10,8},{11,9},{8,1... | collective-permute-start | bytes 98312 | tf_op jit(solution)/shard_map/mode_reduce/ppermute | solution.py:25
  97.7 4.1 %collective-permute-start.6 = (f32[2,8,512]{2,1,0:T(8,128)}, f32[2,8,512]{2,1,0:T(8,128)S(1)}, u32[]{:S(2)}, u32[]{:S(2)}) collective-permute-start(f32[2,8,512]{2,1,0:T(8,128)} %get-tuple-element.18), channel_id=1, source_target_pairs={{1,0},{2,1},{3,2},{0,3},{5,4},{6,5},{7,6},{4,7},{9,8},{10,9},{11,1... | collective-permute-start | bytes 98312 | tf_op jit(solution)/shard_map/mode_reduce/ppermute | solution.py:25

commit v3 on v2

--- a/solution.py
+++ b/solution.py
@@ -100,7 +100,7 @@
 LANES = 128
 
 
-def step_kernel(tbl, x_ref, a_ref, recv_ref, turn_ref, rho_ref, vel_ref, prs_ref, *rest, modes_total, first):
+def step_kernel(tbl, x_ref, a_ref, rlo_ref, rhi_ref, tlo_ref, thi_ref, rho_ref, vel_ref, prs_ref, *rest, modes_total, first):
     if first:
         xo_ref, ao_ref, sens_ref, elo_ref, ehi_ref, gh_ref = rest
     else:
@@ -121,12 +121,12 @@
             sens_ref[...] = sin_ref[...]
 
     for s in range(slots):
-        for side, (tcol, fcol) in enumerate(((0, 1), (2, 3))):
+        for side, (recv_ref, turn_ref, tcol, fcol) in enumerate(((rlo_ref, tlo_ref, 0, 1), (rhi_ref, thi_ref, 2, 3))):
             t = tbl[s * ENTRIES + tcol]
             f = tbl[s * ENTRIES + fcol]
             for arr in range(2):
-                plain = recv_ref[side, arr, 0, t]
-                turned = turn_ref[side, arr, 0, t]
+                plain = recv_ref[arr, 0, t]
+                turned = turn_ref[arr, 0, t]
                 flag = (jnp.zeros(plain.shape, jnp.int32) + f) != 0
                 gh_ref[arr, side, s] = jnp.where(flag, turned, plain)
 
@@ -195,17 +195,16 @@
             sens_ref[s, :, cs] = sens_ref[s, :, cs] + means[0] * means[1]
 
 
-def run_step(tbl, x, a, recv, turned, density, velocity, pressure, sens_in, modes_total, first):
+def run_step(tbl, x, a, rlo, rhi, density, velocity, pressure, sens_in, modes_total, first):
     modes, parts, nv, slots, height, width = x.shape
     state_block = (1, parts, nv, slots, height, width)
     edge_block = (2, 1, slots, parts * nv, width)
     state_spec = pl.BlockSpec(state_block, lambda m, t: (m, 0, 0, 0, 0, 0))
     edge_spec = pl.BlockSpec(edge_block, lambda m, t: (0, m, 0, 0, 0))
-    both_spec = pl.BlockSpec((2,) + edge_block, lambda m, t: (0, 0, m, 0, 0, 0))
     flow_spec = pl.BlockSpec((slots, height, width), lambda m, t: (0, 0, 0))
     vel_spec = pl.BlockSpec((2, slots, height, width), lambda m, t: (0, 0, 0, 0))
-    in_specs = [state_spec, state_spec, both_spec, both_spec, flow_spec, vel_spec, flow_spec]
-    args = [x, a, recv, turned, density, velocity, pressure]
+    in_specs = [state_spec, state_spec, edge_spec, edge_spec, edge_spec, edge_spec, flow_spec, vel_spec, flow_spec]
+    args = [x, a, rlo, rhi, reverse_lanes(rlo), reverse_lanes(rhi), density, velocity, pressure]
     if not first:
         in_specs.append(flow_spec)
         args.append(sens_in)
@@ -247,10 +246,30 @@
     return out.reshape(rows.shape)
 
 
-def edges(x, row):
+def edge_kernel(x_ref, a_ref, lo_ref, hi_ref):
+    nv = x_ref.shape[2]
+    height = x_ref.shape[4]
+    for arr, src in enumerate((x_ref, a_ref)):
+        for p in range(x_ref.shape[1]):
+            for n in range(nv):
+                k = p * nv + n
+                for s in range(x_ref.shape[3]):
+                    lo_ref[arr, 0, s, pl.ds(k, 1), :] = src[0, p, n, s, 0:1, :]
+                    hi_ref[arr, 0, s, pl.ds(k, 1), :] = src[0, p, n, s, height - 1:height, :]
+
+
+def edge_rows(x, a):
     modes, parts, nv, slots, height, width = x.shape
-    e = x[:, :, :, :, row, :]
-    return jnp.transpose(e, (0, 3, 1, 2, 4)).reshape(modes, slots, parts * nv, width)
+    state_spec = pl.BlockSpec((1, parts, nv, slots, height, width), lambda m: (m, 0, 0, 0, 0, 0))
+    edge_spec = pl.BlockSpec((2, 1, slots, parts * nv, width), lambda m: (0, m, 0, 0, 0))
+    edge_shape = jax.ShapeDtypeStruct((2, modes, slots, parts * nv, width), jnp.float32)
+    return pl.pallas_call(
+        edge_kernel,
+        grid=(modes,),
+        in_specs=[state_spec, state_spec],
+        out_specs=[edge_spec, edge_spec],
+        out_shape=[edge_shape, edge_shape],
+    )(x, a)
 
 
 def per_device(direct, adjoint, density, velocity, pressure, block_home, face_nbr, face_flip):
@@ -270,20 +289,19 @@
     table = jnp.concatenate([table.astype(jnp.int32), mode_base[None]])
 
     with jax.named_scope("edge_exchange_0"):
-        up = jnp.stack([edges(direct, height - 1), edges(adjoint, height - 1)])
-        down = jnp.stack([edges(direct, 0), edges(adjoint, 0)])
-        recv = jnp.stack([shifted(up, "blk", 1), shifted(down, "blk", -1)])
-        turned = reverse_lanes(recv)
+        down, up = edge_rows(direct, adjoint)
+        rlo = shifted(up, "blk", 1)
+        rhi = shifted(down, "blk", -1)
     with jax.named_scope("flow_step_0"):
         q1, a1, sens, elo, ehi = run_step(
-            table, direct, adjoint, recv, turned, density, velocity, pressure, None, modes_total, True
+            table, direct, adjoint, rlo, rhi, density, velocity, pressure, None, modes_total, True
         )
     with jax.named_scope("edge_exchange_1"):
-        recv = jnp.stack([shifted(ehi, "blk", 1), shifted(elo, "blk", -1)])
-        turned = reverse_lanes(recv)
+        rlo = shifted(ehi, "blk", 1)
+        rhi = shifted(elo, "blk", -1)
     with jax.named_scope("flow_step_1"):
         q2, a2, sens = run_step(
-            table, q1, a1, recv, turned, density, velocity, pressure, sens, modes_total, False
+            table, q1, a1, rlo, rhi, density, velocity, pressure, sens, modes_total, False
         )
     with jax.named_scope("mode_reduce"):
         count = lax.axis_size("mode")

time: 104 us -> 94.2 us (0.906)
  starting transfers between devices: 24.9 us -> 19 us
  local copies, waits for them, and re-layouts: 5.81 us -> 1.18 us
  Pallas kernels: 14 us -> 17.7 us
  other arithmetic: 4.29 us -> 2 us
  waiting for transfers between devices: 48 us -> 46.2 us
  matrix products: 5.51 us -> 7.08 us
    ppermute x7, starting transfers between devices: 24.9 us -> 19 us  [shifted(): return lax.ppermute(block, axis, route)]
    slice x2 -> x0, local copies, waits for them, and re-layouts: 4.14 us -> none  [edges(): e = x[:, :, :, :, row, :]]
    pallas_call x0 -> x1, Pallas kernels: none -> 3.69 us  [edge_rows(): pl.pallas_call(edge_kernel, grid=(modes,), in_specs=[state_spec, state_sp...]
    another operation x4 -> x0, other arithmetic: 2.27 us -> none  [the longest x1 1.1 us: per_device(): recv = jnp.stack([shifted(ehi, 'blk', 1), shifted(elo, 'blk', -1)])]
    ppermute x7, waiting for transfers between devices: 48 us -> 46.2 us  [shifted(): return lax.ppermute(block, axis, route)]
    dot_general x2 -> x4, matrix products: 5.51 us -> 7.08 us  [reverse_lanes(): jnp.dot(flat, turn, precision=lax.Precision.HIGHEST, preferred_element_ty...]
  transfers between devices with their start and end apart: 7 -> 7, of which waited for: 5 -> 7; matrix products, arithmetic and copies ran while one was open for 2% -> 6% of each run, Pallas kernels for 0% -> 0%
where the time goes in v3:
time: 94.2 us; the launch traced here: 93.8 us
  waiting for transfers between devices  46.2 us (49%)
  starting transfers between devices  19 us (20%)
  Pallas kernels  17.7 us (19%)
  matrix products  7.08 us (8%)
  other arithmetic  2 us (2%)
  local copies, waits for them, and re-layouts  1.18 us (1%)
    ppermute x7, waiting for transfers between devices, shifted(): return lax.ppermute(block, axis, route)  46.2 us
    ppermute x7, starting transfers between devices, shifted(): return lax.ppermute(block, axis, route)  19 us
    pallas_call x2, Pallas kernels, run_step(): pl.pallas_call(kernel, grid_spec=grid_spec, out_shape=out_shape, compiler...  14 us
    dot_general x4, matrix products, reverse_lanes(): jnp.dot(flat, turn, precision=lax.Precision.HIGHEST, preferred_element_ty...  7.08 us
    pallas_call x1, Pallas kernels, edge_rows(): pl.pallas_call(edge_kernel, grid=(modes,), in_specs=[state_spec, state_sp...  3.69 us
  transfers between devices with their start and end apart: 7, of which 7 were waited for; matrix products, arithmetic and copies ran while one was open for 6% of the time, Pallas kernels for 0%

profile of v3, /device:TPU:32, one launch (start us, length us, event | category | flops | bytes accessed | tf_op | source)
XLA Modules:
  0.0 93.8 jit_solution(11816079205365271836)
XLA Ops:
  0.6 0.0 copy-start
  0.6 0.0 copy-start.5
  0.7 0.0 copy-start.6
  0.7 3.7 %edge_exchange_0.1 = (f32[2,4,2,10,512]{4,3,2,1,0:T(8,128)}, f32[2,4,2,10,512]{4,3,2,1,0:T(8,128)}) custom-call(f32[4,2,5,2,8,512]{5,4,3,2,1,0:T(8,128)} %x_ref.3, f32[4,2,5,2,8,512]{5,4,3,2,1,0:T(8,128)} %a_ref.3), custom_call_target="tpu_custom_call" | custom-call | tf_op jit(solution)/shard_map/edge_exchange_0/pallas_call | solution.py:266
  4.4 10.4 %collective-permute-start.1 = (f32[2,4,2,10,512]{4,3,2,1,0:T(8,128)}, f32[2,4,2,10,512]{4,3,2,1,0:T(8,128)S(1)}, u32[]{:S(2)}, u32[]{:S(2)}) collective-permute-start(f32[2,4,2,10,512]{4,3,2,1,0:T(8,128)} %get-tuple-element.14), channel_id=1, source_target_pairs={{4,0},{8,4},{12,8},{16,12},{20,16},{24,20},{28,24},{32,28},{36,32}... | collective-permute-start | bytes 983048 | tf_op jit(solution)/shard_map/edge_exchange_0/ppermute | solution.py:25
  14.7 0.0 collective-permute-start
  14.7 0.0 copy-done.5
  14.8 0.1 reshape.38
  14.8 0.0 copy-done
  14.9 0.6 gather_fusion
  15.5 0.1 reshape.37
  15.6 0.1 fusion.37
  15.7 0.0 copy-done.6
  15.7 0.1 fusion.39
  15.7 0.1 stack.18
  15.8 0.1 reshape.35
  15.9 0.6 pad_add_fusion.tbl
  16.5 17.5 %collective-permute-done.1.rhi_ref = f32[2,4,2,10,512]{4,3,2,1,0:T(8,128)S(1)} collective-permute-done((f32[2,4,2,10,512]{4,3,2,1,0:T(8,128)}, f32[2,4,2,10,512]{4,3,2,1,0:T(8,128)S(1)}, u32[]{:S(2)}, u32[]{:S(2)}) %collective-permute-start.1) | collective-permute-done | bytes 327712 | tf_op jit(solution)/shard_map/edge_exchange_0/ppermute | solution.py:25
  34.0 0.0 copy-start.1
  34.0 1.8 %fusion.4.thi_ref = f32[2,4,2,10,512]{4,3,2,1,0:T(8,128)} fusion(f32[2,4,2,10,512]{4,3,2,1,0:T(8,128)S(1)} %collective-permute-done.1.rhi_ref), kind=kOutput, calls=%fused_computation.5 | convolution fusion | flops 504102912 | bytes 655360 | tf_op jit(solution)/shard_map/flow_step_0/dot_general | solution.py:245
  35.8 3.5 %collective-permute-done.rlo_ref = f32[2,4,2,10,512]{4,3,2,1,0:T(8,128)S(1)} collective-permute-done((f32[2,4,2,10,512]{4,3,2,1,0:T(8,128)}, f32[2,4,2,10,512]{4,3,2,1,0:T(8,128)S(1)}, u32[]{:S(2)}, u32[]{:S(2)}) %collective-permute-start) | collective-permute-done | bytes 327712 | tf_op jit(solution)/shard_map/edge_exchange_0/ppermute | solution.py:25
  39.3 0.0 copy-start.2
  39.3 1.8 %fusion.6.tlo_ref = f32[2,4,2,10,512]{4,3,2,1,0:T(8,128)} fusion(f32[2,4,2,10,512]{4,3,2,1,0:T(8,128)S(1)} %collective-permute-done.rlo_ref), kind=kOutput, calls=%fused_computation.7 | convolution fusion | flops 504102912 | bytes 655360 | tf_op jit(solution)/shard_map/flow_step_0/dot_general | solution.py:245
  41.1 0.0 copy-done.1
  41.1 0.0 copy-done.2
  41.1 7.2 %flow_step_0.1 = (f32[4,2,5,2,8,512]{5,4,3,2,1,0:T(8,128)}, f32[4,2,5,2,8,512]{5,4,3,2,1,0:T(8,128)}, f32[2,8,512]{2,1,0:T(8,128)}, f32[2,4,2,10,512]{4,3,2,1,0:T(8,128)}, f32[2,4,2,10,512]{4,3,2,1,0:T(8,128)}) custom-call(s32[17]{0:T(128)} %pad_add_fusion.tbl, f32[4,2,5,2,8,512]{5,4,3,2,1,0:T(8,128)} %x_ref.3, f32[4,2,5,2,8,512]{5,4,3,2,1,0:T(8,128)} %a_ref.3, ...), custom_call_target="tpu_custom_call" | custom-call | tf_op jit(solution)/shard_map/flow_step_0/pallas_call | solution.py:231
  48.2 6.5 %collective-permute-start.3 = (f32[2,4,2,10,512]{4,3,2,1,0:T(8,128)}, f32[2,4,2,10,512]{4,3,2,1,0:T(8,128)S(1)}, u32[]{:S(2)}, u32[]{:S(2)}) collective-permute-start(f32[2,4,2,10,512]{4,3,2,1,0:T(8,128)} %get-tuple-element.18), channel_id=1, source_target_pairs={{4,0},{8,4},{12,8},{16,12},{20,16},{24,20},{28,24},{32,28},{36,32}... | collective-permute-start | bytes 983048 | tf_op jit(solution)/shard_map/edge_exchange_1/ppermute | solution.py:25
  54.7 0.0 collective-permute-start.2
  54.7 14.8 %collective-permute-done.3.rhi_ref = f32[2,4,2,10,512]{4,3,2,1,0:T(8,128)S(1)} collective-permute-done((f32[2,4,2,10,512]{4,3,2,1,0:T(8,128)}, f32[2,4,2,10,512]{4,3,2,1,0:T(8,128)S(1)}, u32[]{:S(2)}, u32[]{:S(2)}) %collective-permute-start.3) | collective-permute-done | bytes 327712 | tf_op jit(solution)/shard_map/edge_exchange_1/ppermute | solution.py:25
  69.5 0.0 copy-start.3
  69.5 1.8 %fusion.thi_ref = f32[2,4,2,10,512]{4,3,2,1,0:T(8,128)} fusion(f32[2,4,2,10,512]{4,3,2,1,0:T(8,128)S(1)} %collective-permute-done.3.rhi_ref), kind=kOutput, calls=%fused_computation.1 | convolution fusion | flops 504102912 | bytes 655360 | tf_op jit(solution)/shard_map/flow_step_1/dot_general | solution.py:245
  71.3 6.5 %collective-permute-done.2.rlo_ref = f32[2,4,2,10,512]{4,3,2,1,0:T(8,128)S(1)} collective-permute-done((f32[2,4,2,10,512]{4,3,2,1,0:T(8,128)}, f32[2,4,2,10,512]{4,3,2,1,0:T(8,128)S(1)}, u32[]{:S(2)}, u32[]{:S(2)}) %collective-permute-start.2) | collective-permute-done | bytes 327712 | tf_op jit(solution)/shard_map/edge_exchange_1/ppermute | solution.py:25
  77.8 0.0 copy-start.4
  77.8 1.8 %fusion.2.tlo_ref = f32[2,4,2,10,512]{4,3,2,1,0:T(8,128)} fusion(f32[2,4,2,10,512]{4,3,2,1,0:T(8,128)S(1)} %collective-permute-done.2.rlo_ref), kind=kOutput, calls=%fused_computation.3 | convolution fusion | flops 504102912 | bytes 655360 | tf_op jit(solution)/shard_map/flow_step_1/dot_general | solution.py:245
  79.5 0.0 copy-done.3
  79.5 0.0 copy-done.4
  79.5 6.8 %flow_step_1.1 = (f32[4,2,5,2,8,512]{5,4,3,2,1,0:T(8,128)}, f32[4,2,5,2,8,512]{5,4,3,2,1,0:T(8,128)}, f32[2,8,512]{2,1,0:T(8,128)}) custom-call(s32[17]{0:T(128)} %pad_add_fusion.tbl, f32[4,2,5,2,8,512]{5,4,3,2,1,0:T(8,128)} %get-tuple-element.15.x_ref, f32[4,2,5,2,8,512]{5,4,3,2,1,0:T(8,128)} %get-tuple-element.16.a_ref, f32[2,4,2,10,512]{4,3,2,1,0:T(8,128)} %copy-done.4, ...), custom_call_target="tpu_custom_call" | custom-call | tf_op jit(solution)/shard_map/flow_step_1/pallas_call | solution.py:231
  86.4 0.2 collective-permute-start.4
  86.6 1.3 %collective-permute-start.5 = (f32[2,8,512]{2,1,0:T(8,128)}, f32[2,8,512]{2,1,0:T(8,128)S(1)}, u32[]{:S(2)}, u32[]{:S(2)}) collective-permute-start(f32[2,8,512]{2,1,0:T(8,128)} %get-tuple-element.22), channel_id=1, source_target_pairs={{2,0},{3,1},{0,2},{1,3},{6,4},{7,5},{4,6},{5,7},{10,8},{11,9},{8,1... | collective-permute-start | bytes 98312 | tf_op jit(solution)/shard_map/mode_reduce/ppermute | solution.py:25
  87.9 0.6 collective-permute-start.6
  88.5 2.1 %collective-permute-done.4 = f32[2,8,512]{2,1,0:T(8,128)S(1)} collective-permute-done((f32[2,8,512]{2,1,0:T(8,128)}, f32[2,8,512]{2,1,0:T(8,128)S(1)}, u32[]{:S(2)}, u32[]{:S(2)}) %collective-permute-start.4) | collective-permute-done | bytes 32800 | tf_op jit(solution)/shard_map/mode_reduce/ppermute | solution.py:25
  90.6 1.0 %collective-permute-done.5 = f32[2,8,512]{2,1,0:T(8,128)S(1)} collective-permute-done((f32[2,8,512]{2,1,0:T(8,128)}, f32[2,8,512]{2,1,0:T(8,128)S(1)}, u32[]{:S(2)}, u32[]{:S(2)}) %collective-permute-start.5) | collective-permute-done | bytes 32800 | tf_op jit(solution)/shard_map/mode_reduce/ppermute | solution.py:25
  91.6 0.8 collective-permute-done.6
  92.4 0.8 pad_maximum_fusion
  93.2 0.6 multiply_bitcast_fusion
  (4 shorter events, 0.0 us)
Async XLA Ops:
  0.6 14.2 %copy-start = (s32[128]{0:T(128)S(1)}, s32[128]{0:T(128)}, u32[]{:S(2)}) copy-start(s32[128]{0:T(128)} %param.13) | copy-start | bytes 1540
  0.6 14.1 %copy-start.5 = (s32[2,4]{1,0:T(2,128)S(1)}, s32[2,4]{1,0:T(2,128)}, u32[]{:S(2)}) copy-start(s32[2,4]{1,0:T(2,128)} %param.14) | copy-start | bytes 100
  0.7 15.0 %copy-start.6 = (s32[2,4]{1,0:T(2,128)S(1)}, s32[2,4]{1,0:T(2,128)}, u32[]{:S(2)}) copy-start(s32[2,4]{1,0:T(2,128)} %param.15) | copy-start | bytes 100
  4.4 29.6 %collective-permute-start.1 = (f32[2,4,2,10,512]{4,3,2,1,0:T(8,128)}, f32[2,4,2,10,512]{4,3,2,1,0:T(8,128)S(1)}, u32[]{:S(2)}, u32[]{:S(2)}) collective-permute-start(f32[2,4,2,10,512]{4,3,2,1,0:T(8,128)} %get-tuple-element.14), channel_id=1, source_target_pairs={{4,0},{8,4},{12,8},{16,12},{20,16},{24,20},{28,24},{32,28},{36,32}... | collective-permute-start | bytes 983048 | tf_op jit(solution)/shard_map/edge_exchange_0/ppermute | solution.py:25
  14.7 24.6 %collective-permute-start = (f32[2,4,2,10,512]{4,3,2,1,0:T(8,128)}, f32[2,4,2,10,512]{4,3,2,1,0:T(8,128)S(1)}, u32[]{:S(2)}, u32[]{:S(2)}) collective-permute-start(f32[2,4,2,10,512]{4,3,2,1,0:T(8,128)} %get-tuple-element.13), channel_id=1, source_target_pairs={{252,0},{0,4},{4,8},{8,12},{12,16},{16,20},{20,24},{24,28},{28,32}... | collective-permute-start | bytes 983048 | tf_op jit(solution)/shard_map/edge_exchange_0/ppermute | solution.py:25
  34.0 7.1 %copy-start.1 = (f32[2,4,2,10,512]{4,3,2,1,0:T(8,128)}, f32[2,4,2,10,512]{4,3,2,1,0:T(8,128)S(1)}, u32[]{:S(2)}) copy-start(f32[2,4,2,10,512]{4,3,2,1,0:T(8,128)S(1)} %collective-permute-done.1.rhi_ref) | copy-start | bytes 983044
  39.3 1.8 %copy-start.2 = (f32[2,4,2,10,512]{4,3,2,1,0:T(8,128)}, f32[2,4,2,10,512]{4,3,2,1,0:T(8,128)S(1)}, u32[]{:S(2)}) copy-start(f32[2,4,2,10,512]{4,3,2,1,0:T(8,128)S(1)} %collective-permute-done.rlo_ref) | copy-start | bytes 983044
  48.2 21.3 %collective-permute-start.3 = (f32[2,4,2,10,512]{4,3,2,1,0:T(8,128)}, f32[2,4,2,10,512]{4,3,2,1,0:T(8,128)S(1)}, u32[]{:S(2)}, u32[]{:S(2)}) collective-permute-start(f32[2,4,2,10,512]{4,3,2,1,0:T(8,128)} %get-tuple-element.18), channel_id=1, source_target_pairs={{4,0},{8,4},{12,8},{16,12},{20,16},{24,20},{28,24},{32,28},{36,32}... | collective-permute-start | bytes 983048 | tf_op jit(solution)/shard_map/edge_exchange_1/ppermute | solution.py:25
  54.7 23.0 %collective-permute-start.2 = (f32[2,4,2,10,512]{4,3,2,1,0:T(8,128)}, f32[2,4,2,10,512]{4,3,2,1,0:T(8,128)S(1)}, u32[]{:S(2)}, u32[]{:S(2)}) collective-permute-start(f32[2,4,2,10,512]{4,3,2,1,0:T(8,128)} %get-tuple-element.17), channel_id=1, source_target_pairs={{252,0},{0,4},{4,8},{8,12},{12,16},{16,20},{20,24},{24,28},{28,32}... | collective-permute-start | bytes 983048 | tf_op jit(solution)/shard_map/edge_exchange_1/ppermute | solution.py:25
  69.5 10.0 %copy-start.3 = (f32[2,4,2,10,512]{4,3,2,1,0:T(8,128)}, f32[2,4,2,10,512]{4,3,2,1,0:T(8,128)S(1)}, u32[]{:S(2)}) copy-start(f32[2,4,2,10,512]{4,3,2,1,0:T(8,128)S(1)} %collective-permute-done.3.rhi_ref) | copy-start | bytes 983044
  77.8 1.8 %copy-start.4 = (f32[2,4,2,10,512]{4,3,2,1,0:T(8,128)}, f32[2,4,2,10,512]{4,3,2,1,0:T(8,128)S(1)}, u32[]{:S(2)}) copy-start(f32[2,4,2,10,512]{4,3,2,1,0:T(8,128)S(1)} %collective-permute-done.2.rlo_ref) | copy-start | bytes 983044
  86.4 4.2 %collective-permute-start.4 = (f32[2,8,512]{2,1,0:T(8,128)}, f32[2,8,512]{2,1,0:T(8,128)S(1)}, u32[]{:S(2)}, u32[]{:S(2)}) collective-permute-start(f32[2,8,512]{2,1,0:T(8,128)} %get-tuple-element.22), channel_id=1, source_target_pairs={{3,0},{0,1},{1,2},{2,3},{7,4},{4,5},{5,6},{6,7},{11,8},{8,9},{9,10... | collective-permute-start | bytes 98312 | tf_op jit(solution)/shard_map/mode_reduce/ppermute | solution.py:25
  86.6 5.0 %collective-permute-start.5 = (f32[2,8,512]{2,1,0:T(8,128)}, f32[2,8,512]{2,1,0:T(8,128)S(1)}, u32[]{:S(2)}, u32[]{:S(2)}) collective-permute-start(f32[2,8,512]{2,1,0:T(8,128)} %get-tuple-element.22), channel_id=1, source_target_pairs={{2,0},{3,1},{0,2},{1,3},{6,4},{7,5},{4,6},{5,7},{10,8},{11,9},{8,1... | collective-permute-start | bytes 98312 | tf_op jit(solution)/shard_map/mode_reduce/ppermute | solution.py:25
  87.9 4.5 %collective-permute-start.6 = (f32[2,8,512]{2,1,0:T(8,128)}, f32[2,8,512]{2,1,0:T(8,128)S(1)}, u32[]{:S(2)}, u32[]{:S(2)}) collective-permute-start(f32[2,8,512]{2,1,0:T(8,128)} %get-tuple-element.22), channel_id=1, source_target_pairs={{1,0},{2,1},{3,2},{0,3},{5,4},{6,5},{7,6},{4,7},{9,8},{10,9},{11,1... | collective-permute-start | bytes 98312 | tf_op jit(solution)/shard_map/mode_reduce/ppermute | solution.py:25

commit v4 on v3

--- a/solution.py
+++ b/solution.py
@@ -100,18 +100,30 @@
 LANES = 128
 
 
-def step_kernel(tbl, x_ref, a_ref, rlo_ref, rhi_ref, tlo_ref, thi_ref, rho_ref, vel_ref, prs_ref, *rest, modes_total, first):
+def step_kernel(tbl, *refs, modes_total, first, ghosts, patched):
+    refs = list(refs)
+    x_ref, a_ref = refs[0], refs[1]
+    refs = refs[2:]
+    if ghosts:
+        rlo_ref, rhi_ref, tlo_ref, thi_ref = refs[:4]
+        refs = refs[4:]
+    if patched:
+        c0_ref, c7_ref = refs[:2]
+        refs = refs[2:]
+    rho_ref, vel_ref, prs_ref = refs[:3]
+    refs = refs[3:]
+    if not first:
+        sin_ref = refs.pop(0)
     if first:
-        xo_ref, ao_ref, sens_ref, elo_ref, ehi_ref, gh_ref = rest
+        xo_ref, ao_ref, sens_ref, elo_ref, ehi_ref, gh_ref = refs
     else:
-        sin_ref, xo_ref, ao_ref, sens_ref, gh_ref = rest
+        xo_ref, ao_ref, sens_ref, gh_ref = refs
     m = pl.program_id(0)
     slots = x_ref.shape[3]
     height = x_ref.shape[4]
     width = x_ref.shape[5]
     chunks = width // LANES
     shape = (height, LANES)
-    full = (height, width)
 
     @pl.when(m == 0)
     def _init():
@@ -121,14 +133,18 @@
             sens_ref[...] = sin_ref[...]
 
     for s in range(slots):
-        for side, (recv_ref, turn_ref, tcol, fcol) in enumerate(((rlo_ref, tlo_ref, 0, 1), (rhi_ref, thi_ref, 2, 3))):
+        for side, (tcol, fcol) in enumerate(((0, 1), (2, 3))):
             t = tbl[s * ENTRIES + tcol]
             f = tbl[s * ENTRIES + fcol]
             for arr in range(2):
-                plain = recv_ref[arr, 0, t]
-                turned = turn_ref[arr, 0, t]
-                flag = (jnp.zeros(plain.shape, jnp.int32) + f) != 0
-                gh_ref[arr, side, s] = jnp.where(flag, turned, plain)
+                if ghosts:
+                    recv_ref, turn_ref = ((rlo_ref, tlo_ref), (rhi_ref, thi_ref))[side]
+                    plain = recv_ref[arr, 0, t]
+                    turned = turn_ref[arr, 0, t]
+                    flag = (jnp.zeros(plain.shape, jnp.int32) + f) != 0
+                    gh_ref[arr, side, s] = jnp.where(flag, turned, plain)
+                else:
+                    gh_ref[arr, side, s] = jnp.zeros(gh_ref.shape[3:], jnp.float32)
 
     kf = (tbl[slots * ENTRIES] + m).astype(jnp.float32)
     w = BASE_FREQ * (jnp.zeros(shape, jnp.float32) + (kf - modes_total / 2 + 0.5))
@@ -139,6 +155,16 @@
     last_row = row == height - 1
     first_lane = lane == 0
     last_lane = lane == LANES - 1
+    def load(src, arr, p, n, slot, k, cols):
+        g = src[0, p, n, slot, :, cols]
+        if patched:
+            top = jnp.broadcast_to(c0_ref[arr, 0, slot, pl.ds(k, 1), cols], shape)
+            bottom = jnp.broadcast_to(c7_ref[arr, 0, slot, pl.ds(k, 1), cols], shape)
+            g = jnp.where(first_row, top, jnp.where(last_row, bottom, g))
+        return g
+
+    inner = (row > 0) & (row < height - 1)
+
     for s in range(slots):
         base = s * ENTRIES
         jl_s, jl_live = tbl[base + 4], tbl[base + 5]
@@ -159,19 +185,19 @@
                 for p in range(2):
                     for n in range(NV):
                         k = p * NV + n
-                        g = src[0, p, n, s, :, cs]
+                        g = load(src, arr, p, n, s, k, cs)
                         lo_b = jnp.broadcast_to(gh_ref[arr, 0, s, k:k + 1, cs], shape)
                         hi_b = jnp.broadcast_to(gh_ref[arr, 1, s, k:k + 1, cs], shape)
                         im1 = jnp.where(first_row, lo_b, pltpu.roll(g, 1, 0))
                         ip1 = jnp.where(last_row, hi_b, pltpu.roll(g, height - 1, 0))
                         if b > 0:
-                            left = src[0, p, n, s, :, (b - 1) * LANES:b * LANES]
+                            left = load(src, arr, p, n, s, k, slice((b - 1) * LANES, b * LANES))
                         else:
-                            left = jnp.where(jl_mask, src[0, p, n, jl_s, :, width - LANES:width], 0.0)
+                            left = jnp.where(jl_mask, load(src, arr, p, n, jl_s, k, slice(width - LANES, width)), 0.0)
                         if b < chunks - 1:
-                            right = src[0, p, n, s, :, (b + 1) * LANES:(b + 2) * LANES]
+                            right = load(src, arr, p, n, s, k, slice((b + 1) * LANES, (b + 2) * LANES))
                         else:
-                            right = jnp.where(jh_mask, src[0, p, n, jh_s, :, 0:LANES], 0.0)
+                            right = jnp.where(jh_mask, load(src, arr, p, n, jh_s, k, slice(0, LANES)), 0.0)
                         jm1 = jnp.where(first_lane, pltpu.roll(left, 1, 1), pltpu.roll(g, 1, 1))
                         jp1 = jnp.where(last_lane, pltpu.roll(right, LANES - 1, 1), pltpu.roll(g, LANES - 1, 1))
                         vals.append(g)
@@ -192,10 +218,13 @@
                         sq = nv * nv
                         total = sq if total is None else total + sq
                 means.append(total / 10.0)
-            sens_ref[s, :, cs] = sens_ref[s, :, cs] + means[0] * means[1]
-
-
-def run_step(tbl, x, a, rlo, rhi, density, velocity, pressure, sens_in, modes_total, first):
+            term = means[0] * means[1]
+            if not ghosts:
+                term = jnp.where(inner, term, 0.0)
+            sens_ref[s, :, cs] = sens_ref[s, :, cs] + term
+
+
+def run_step(tbl, x, a, rlo, rhi, patch, density, velocity, pressure, sens_in, modes_total, first):
     modes, parts, nv, slots, height, width = x.shape
     state_block = (1, parts, nv, slots, height, width)
     edge_block = (2, 1, slots, parts * nv, width)
@@ -203,8 +232,18 @@
     edge_spec = pl.BlockSpec(edge_block, lambda m, t: (0, m, 0, 0, 0))
     flow_spec = pl.BlockSpec((slots, height, width), lambda m, t: (0, 0, 0))
     vel_spec = pl.BlockSpec((2, slots, height, width), lambda m, t: (0, 0, 0, 0))
-    in_specs = [state_spec, state_spec, edge_spec, edge_spec, edge_spec, edge_spec, flow_spec, vel_spec, flow_spec]
-    args = [x, a, rlo, rhi, reverse_lanes(rlo), reverse_lanes(rhi), density, velocity, pressure]
+    ghosts = rlo is not None
+    patched = patch is not None
+    in_specs = [state_spec, state_spec]
+    args = [x, a]
+    if ghosts:
+        in_specs += [edge_spec] * 4
+        args += [rlo, rhi, reverse_lanes(rlo), reverse_lanes(rhi)]
+    if patched:
+        in_specs += [edge_spec] * 2
+        args += list(patch)
+    in_specs += [flow_spec, vel_spec, flow_spec]
+    args += [density, velocity, pressure]
     if not first:
         in_specs.append(flow_spec)
         args.append(sens_in)
@@ -227,13 +266,56 @@
             pltpu.VMEM((2, 2, slots, parts * nv, width), jnp.float32),
         ],
     )
-    kernel = functools.partial(step_kernel, modes_total=modes_total, first=first)
+    kernel = functools.partial(step_kernel, modes_total=modes_total, first=first, ghosts=ghosts, patched=patched)
     return pl.pallas_call(
         kernel,
         grid_spec=grid_spec,
         out_shape=out_shape,
         compiler_params=pltpu.CompilerParams(dimension_semantics=("arbitrary",)),
     )(tbl, *args)
+
+
+def ghost_term(f, r, ir, u, kp, transpose):
+    if transpose:
+        return [u * f[0], r * f[0] + u * f[1] + kp * f[4], u * f[2], u * f[3], f[1] * ir + u * f[4]]
+    return [u * f[0] + r * f[1], u * f[1] + f[4] * ir, u * f[2], u * f[3], kp * f[1] + u * f[4]]
+
+
+def fix_rows(partial0, partial7, rlo, rhi, slot_of, face_flip, density, velocity, pressure):
+    _, modes, slots, rows, width = partial0.shape
+    height = density.shape[1]
+
+    def picked(recv, side):
+        plain = jnp.take(recv, slot_of[:, side], axis=2)
+        turned = reverse_lanes(plain)
+        flag = (face_flip[:, side] != 0)[None, None, :, None, None]
+        return jnp.where(flag, turned, plain)
+
+    ghost = {0: picked(rlo, 0), height - 1: picked(rhi, 1)}
+    partial = {0: partial0, height - 1: partial7}
+    fixed = {}
+    sens_rows = {}
+    for row in (0, height - 1):
+        r = density[:, row, :]
+        ir = 1.0 / r
+        u = velocity[0][:, row, :]
+        kp = HEAT_RATIO * pressure[:, row, :]
+        half = 0.5 if row == 0 else -0.5
+        out = []
+        for arr, sign in ((0, 1.0), (1, -1.0)):
+            g = ghost[row][arr].reshape(modes, slots, 2, NV, width)
+            res = []
+            for p in range(2):
+                f = [g[:, :, p, n, :] for n in range(NV)]
+                conv = ghost_term(f, r, ir, u, kp, arr == 1)
+                for n in range(NV):
+                    res.append(sign * half * conv[n] + VISCOSITY * f[n])
+            delta = jnp.stack(res, axis=2)
+            out.append(partial[row][arr] + TIME_STEP * delta)
+        fixed[row] = jnp.stack(out)
+        means = jnp.sum(fixed[row] * fixed[row], axis=3) / 10.0
+        sens_rows[row] = jnp.sum(means[0] * means[1], axis=0)
+    return fixed[0], fixed[height - 1], sens_rows[0], sens_rows[height - 1]
 
 
 def reverse_lanes(rows):
@@ -294,14 +376,17 @@
         rhi = shifted(down, "blk", -1)
     with jax.named_scope("flow_step_0"):
         q1, a1, sens, elo, ehi = run_step(
-            table, direct, adjoint, rlo, rhi, density, velocity, pressure, None, modes_total, True
+            table, direct, adjoint, None, None, None, density, velocity, pressure, None, modes_total, True
         )
+    with jax.named_scope("edge_fix_0"):
+        c0, c7, s0, s7 = fix_rows(elo, ehi, rlo, rhi, slot_of, face_flip, density, velocity, pressure)
+        sens = sens.at[:, 0, :].add(s0).at[:, height - 1, :].add(s7)
     with jax.named_scope("edge_exchange_1"):
-        rlo = shifted(ehi, "blk", 1)
-        rhi = shifted(elo, "blk", -1)
+        rlo = shifted(c7, "blk", 1)
+        rhi = shifted(c0, "blk", -1)
     with jax.named_scope("flow_step_1"):
         q2, a2, sens = run_step(
-            table, q1, a1, rlo, rhi, density, velocity, pressure, sens, modes_total, False
+            table, q1, a1, rlo, rhi, (c0, c7), density, velocity, pressure, sens, modes_total, False
         )
     with jax.named_scope("mode_reduce"):
         count = lax.axis_size("mode")

time: 94.2 us -> 92.9 us (0.986); the launches traced: 93.8 us -> 91.2 us
  waiting for transfers between devices: 46.2 us -> 32.5 us
  local copies, waits for them, and re-layouts: 1.18 us -> 7.79 us
  other arithmetic: 2 us -> 6.19 us
  matrix products: 7.08 us -> 5.67 us
  starting transfers between devices: 19 us -> 20.2 us
    ppermute x7, waiting for transfers between devices: 46.2 us -> 32.5 us  [shifted(): return lax.ppermute(block, axis, route)]
    scatter-add x0 -> x2, local copies, waits for them, and re-layouts: none -> 2.78 us  [per_device(): sens = sens.at[:, 0, :].add(s0).at[:, height - 1, :].add(s7)]
    add x0 -> x4, other arithmetic: none -> 1.73 us  [the longest x2 1.53 us: per_device(): sens = sens.at[:, 0, :].add(s0).at[:, height - 1, :].add(s7)]
    slice x1 -> x13, local copies, waits for them, and re-layouts: 0.08 us -> 1.7 us  [the longest x1 0.84 us: fix_rows(): r = density[:, row, :]]
    dot_general x4, matrix products: 7.08 us -> 5.67 us  [reverse_lanes(): jnp.dot(flat, turn, precision=lax.Precision.HIGHEST, preferred_element_ty...]
    ppermute x7, starting transfers between devices: 19 us -> 20.2 us  [shifted(): return lax.ppermute(block, axis, route)]
    gather x0 -> x2, local copies, waits for them, and re-layouts: none -> 1.16 us  [picked(): plain = jnp.take(recv, slot_of[:, side], axis=2)]
    another operation x0 -> x4, local copies, waits for them, and re-layouts: none -> 1.02 us  [fix_rows(): delta = jnp.stack(res, axis=2)]
  transfers between devices with their start and end apart: 7 -> 7, of which waited for: 7 -> 4; matrix products, arithmetic and copies ran while one was open for 6% -> 14% of each run, Pallas kernels for 0% -> 7%
where the time goes in v4:
time: 92.9 us; the launch traced here: 91.2 us
  waiting for transfers between devices  32.5 us (35%)
  starting transfers between devices  20.2 us (22%)
  Pallas kernels  17.9 us (19%)
  local copies, waits for them, and re-layouts  7.79 us (8%)
  other arithmetic  6.19 us (7%)
  matrix products  5.67 us (6%)
  between operations  1.05 us (1%)
    ppermute x7, waiting for transfers between devices, shifted(): return lax.ppermute(block, axis, route)  32.5 us
    ppermute x7, starting transfers between devices, shifted(): return lax.ppermute(block, axis, route)  20.2 us
    pallas_call x2, Pallas kernels, run_step(): pl.pallas_call(kernel, grid_spec=grid_spec, out_shape=out_shape, compiler...  14.1 us
    dot_general x4, matrix products, reverse_lanes(): jnp.dot(flat, turn, precision=lax.Precision.HIGHEST, preferred_element_ty...  5.67 us
    pallas_call x1, Pallas kernels, edge_rows(): pl.pallas_call(edge_kernel, grid=(modes,), in_specs=[state_spec, state_sp...  3.77 us
    scatter-add x2, local copies, waits for them, and re-layouts, per_device(): sens = sens.at[:, 0, :].add(s0).at[:, height - 1, :].add(s7)  2.78 us
  transfers between devices with their start and end apart: 7, of which 4 were waited for; matrix products, arithmetic and copies ran while one was open for 14% of the time, Pallas kernels for 7%

profile of v4, /device:TPU:32, one launch (start us, length us, event | category | flops | bytes accessed | tf_op | source)
XLA Modules:
  0.0 91.2 jit_solution(9360135447771931394)
XLA Ops:
  0.7 3.8 %edge_exchange_0.1 = (f32[2,4,2,10,512]{4,3,2,1,0:T(8,128)}, f32[2,4,2,10,512]{4,3,2,1,0:T(8,128)}) custom-call(f32[4,2,5,2,8,512]{5,4,3,2,1,0:T(8,128)} %x_ref.1, f32[4,2,5,2,8,512]{5,4,3,2,1,0:T(8,128)} %a_ref.1), custom_call_target="tpu_custom_call" | custom-call | tf_op jit(solution)/shard_map/edge_exchange_0/pallas_call | solution.py:348
  4.4 10.4 %collective-permute-start = (f32[2,4,2,10,512]{4,3,2,1,0:T(8,128)}, f32[2,4,2,10,512]{4,3,2,1,0:T(8,128)S(1)}, u32[]{:S(2)}, u32[]{:S(2)}) collective-permute-start(f32[2,4,2,10,512]{4,3,2,1,0:T(8,128)} %get-tuple-element.41), channel_id=1, source_target_pairs={{4,0},{8,4},{12,8},{16,12},{20,16},{24,20},{28,24},{32,28},{36,32}... | collective-permute-start | bytes 983048 | tf_op jit(solution)/shard_map/edge_exchange_0/ppermute | solution.py:25
  15.0 0.6 gather_fusion
  15.7 0.2 slice_reduce_fusion.1
  15.9 0.8 fusion.45
  16.8 0.2 compare_reduce_fusion
  17.1 0.8 slice_multiply_fusion.2
  18.0 0.1 stack.160
  18.1 0.1 reshape.2374
  18.2 0.6 pad_add_fusion.tbl
  18.8 6.6 %flow_step_0.1 = (f32[4,2,5,2,8,512]{5,4,3,2,1,0:T(8,128)}, f32[4,2,5,2,8,512]{5,4,3,2,1,0:T(8,128)}, f32[2,8,512]{2,1,0:T(8,128)}, f32[2,4,2,10,512]{4,3,2,1,0:T(8,128)}, f32[2,4,2,10,512]{4,3,2,1,0:T(8,128)}) custom-call(s32[17]{0:T(128)} %pad_add_fusion.tbl, f32[4,2,5,2,8,512]{5,4,3,2,1,0:T(8,128)} %x_ref.1, f32[4,2,5,2,8,512]{5,4,3,2,1,0:T(8,128)} %a_ref.1, ...), custom_call_target="tpu_custom_call" | custom-call | tf_op jit(solution)/shard_map/flow_step_0/pallas_call | solution.py:270
  25.4 10.4 %collective-permute-done.2 = f32[2,4,2,10,512]{4,3,2,1,0:T(8,128)S(1)} collective-permute-done((f32[2,4,2,10,512]{4,3,2,1,0:T(8,128)}, f32[2,4,2,10,512]{4,3,2,1,0:T(8,128)S(1)}, u32[]{:S(2)}, u32[]{:S(2)}) %collective-permute-start.2) | collective-permute-done | bytes 327712 | tf_op jit(solution)/shard_map/edge_exchange_0/ppermute | solution.py:25
  35.8 0.6 gather_fusion.2
  36.4 1.1 %convolution_select_fusion = f32[2,4,2,10,512]{4,3,1,0,2:T(8,128)S(1)} fusion(f32[2,2,4,10,512]{4,3,2,1,0:T(8,128)S(1)} %gather_fusion.2, pred[2]{0:T(512)(128)(4,1)S(1)} %compare_and_fusion, pred[2]{0:T(512)(128)(4,1)S(1)} %get-tuple-element.48), kind=kOutput, calls=%fused_computation.5 | convolution fusion | flops 504348672 | bytes 655364 | tf_op jit(solution)/shard_map/edge_fix_0/dot_general | solution.py:327
  37.6 0.1 copy.140
  37.7 0.1 copy.152
  37.9 0.1 add_bitcast_fusion.12
  38.0 0.4 add_bitcast_fusion.11
  38.4 0.3 stack.205
  38.6 0.3 stack.194
  38.9 0.1 multiply_add_fusion.1
  39.0 0.2 multiply_reduce_fusion.1
  39.2 0.6 gather_fusion.1
  39.8 1.1 %convolution_select_fusion.1 = f32[2,4,2,10,512]{4,3,1,0,2:T(8,128)S(1)} fusion(f32[2,2,4,10,512]{4,3,2,1,0:T(8,128)S(1)} %gather_fusion.1, pred[2]{0:T(512)(128)(4,1)S(1)} %compare_and_fusion.1, pred[2]{0:T(512)(128)(4,1)S(1)} %get-tuple-element.49), kind=kOutput, calls=%fused_computation.6 | convolution fusion | flops 504348672 | bytes 655364 | tf_op jit(solution)/shard_map/edge_fix_0/dot_general | solution.py:327
  41.0 0.1 copy.127
  41.1 0.1 copy.116
  41.3 0.1 add_bitcast_fusion.32
  41.4 0.4 add_bitcast_fusion.31
  41.8 0.3 stack.182
  42.1 0.3 stack.171
  42.3 0.1 multiply_add_fusion.3
  42.4 0.2 multiply_reduce_fusion
  42.6 0.5 collective-permute-start.3
  43.1 0.1 collective-permute-start.1
  43.2 0.8 reshape_add_fusion
  44.0 1.4 %scatter-add.6 = f32[2,8,512]{2,1,0:T(8,128)} dynamic-update-slice(f32[2,8,512]{2,1,0:T(8,128)} %get-tuple-element.44, f32[2,1,512]{2,1,0:T(1,128)S(1)} %reshape_add_fusion, s32[]{:T(128)} %constant.145.clone.1, s32[]{:T(128)} %constant.145.clone.1, s32[]{:T(128)} %constant.145.clone.1) | dynamic-update-slice | bytes 8196 | tf_op jit(solution)/shard_map/edge_fix_0/scatter-add | solution.py:383
  45.4 0.8 slice_add_fusion
  46.2 1.4 %scatter-add.9.refs_11_ = f32[2,8,512]{2,1,0:T(8,128)} dynamic-update-slice(f32[2,8,512]{2,1,0:T(8,128)} %scatter-add.6, f32[2,1,512]{2,1,0:T(1,128)S(1)} %slice_add_fusion, s32[]{:T(128)} %constant.145.clone.1, s32[]{:T(128)} %constant.161.clone.1, s32[]{:T(128)} %constant.145.clone.1) | dynamic-update-slice | bytes 8196 | tf_op jit(solution)/shard_map/edge_fix_0/scatter-add | solution.py:383
  47.5 18.5 %collective-permute-done.3.refs_3_ = f32[2,4,2,10,512]{4,3,2,1,0:T(8,128)S(1)} collective-permute-done((f32[2,4,2,10,512]{4,3,2,1,0:T(8,128)S(1)}, f32[2,4,2,10,512]{4,3,2,1,0:T(8,128)S(1)}, u32[]{:S(2)}, u32[]{:S(2)}) %collective-permute-start.3) | collective-permute-done | bytes 327712 | tf_op jit(solution)/shard_map/edge_exchange_1/ppermute | solution.py:25
  66.1 1.8 %fusion.refs_5_ = f32[2,4,2,10,512]{4,3,2,1,0:T(8,128)} fusion(f32[2,4,2,10,512]{4,3,2,1,0:T(8,128)S(1)} %collective-permute-done.3.refs_3_), kind=kOutput, calls=%fused_computation.7 | convolution fusion | flops 504102912 | bytes 655360 | tf_op jit(solution)/shard_map/flow_step_1/dot_general | solution.py:327
  67.9 1.8 %fusion.1.refs_4_ = f32[2,4,2,10,512]{4,3,2,1,0:T(8,128)} fusion(f32[2,4,2,10,512]{4,3,2,1,0:T(8,128)S(1)} %collective-permute-done.1.refs_2_), kind=kOutput, calls=%fused_computation.8 | convolution fusion | flops 504102912 | bytes 655360 | tf_op jit(solution)/shard_map/flow_step_1/dot_general | solution.py:327
  69.6 7.5 %flow_step_1.1 = (f32[4,2,5,2,8,512]{5,4,3,2,1,0:T(8,128)}, f32[4,2,5,2,8,512]{5,4,3,2,1,0:T(8,128)}, f32[2,8,512]{2,1,0:T(8,128)}) custom-call(s32[17]{0:T(128)} %pad_add_fusion.tbl, f32[4,2,5,2,8,512]{5,4,3,2,1,0:T(8,128)} %get-tuple-element.38.refs_0_, f32[4,2,5,2,8,512]{5,4,3,2,1,0:T(8,128)} %get-tuple-element.39.refs_1_, ...), custom_call_target="tpu_custom_call" | custom-call | tf_op jit(solution)/shard_map/flow_step_1/pallas_call | solution.py:270
  77.1 7.7 %collective-permute-start.4 = (f32[2,8,512]{2,1,0:T(8,128)}, f32[2,8,512]{2,1,0:T(8,128)S(1)}, u32[]{:S(2)}, u32[]{:S(2)}) collective-permute-start(f32[2,8,512]{2,1,0:T(8,128)} %get-tuple-element.47), channel_id=1, source_target_pairs={{3,0},{0,1},{1,2},{2,3},{7,4},{4,5},{5,6},{6,7},{11,8},{8,9},{9,10... | collective-permute-start | bytes 98312 | tf_op jit(solution)/shard_map/mode_reduce/ppermute | solution.py:25
  84.8 1.6 %collective-permute-start.6 = (f32[2,8,512]{2,1,0:T(8,128)}, f32[2,8,512]{2,1,0:T(8,128)S(1)}, u32[]{:S(2)}, u32[]{:S(2)}) collective-permute-start(f32[2,8,512]{2,1,0:T(8,128)} %get-tuple-element.47), channel_id=1, source_target_pairs={{1,0},{2,1},{3,2},{0,3},{5,4},{6,5},{7,6},{4,7},{9,8},{10,9},{11,1... | collective-permute-start | bytes 98312 | tf_op jit(solution)/shard_map/mode_reduce/ppermute | solution.py:25
  86.4 0.4 collective-permute-done.4
  86.7 3.1 %collective-permute-done.5 = f32[2,8,512]{2,1,0:T(8,128)S(1)} collective-permute-done((f32[2,8,512]{2,1,0:T(8,128)}, f32[2,8,512]{2,1,0:T(8,128)S(1)}, u32[]{:S(2)}, u32[]{:S(2)}) %collective-permute-start.5) | collective-permute-done | bytes 32800 | tf_op jit(solution)/shard_map/mode_reduce/ppermute | solution.py:25
  89.8 0.8 pad_maximum_fusion.2
  90.6 0.6 multiply_bitcast_fusion
  (54 shorter events, 0.6 us)
Async XLA Ops:
  0.6 14.3 %copy-start = (s32[128]{0:T(128)S(1)}, s32[128]{0:T(128)}, u32[]{:S(2)}) copy-start(s32[128]{0:T(128)} %param.19) | copy-start | bytes 1540
  0.6 14.2 %copy-start.9 = (s32[2,4]{1,0:T(2,128)S(1)}, s32[2,4]{1,0:T(2,128)}, u32[]{:S(2)}) copy-start(s32[2,4]{1,0:T(2,128)} %param.20) | copy-start | bytes 100
  0.7 16.1 %copy-start.8 = (s32[2,4]{1,0:T(2,128)S(1)}, s32[2,4]{1,0:T(2,128)}, u32[]{:S(2)}) copy-start(s32[2,4]{1,0:T(2,128)} %param.21) | copy-start | bytes 100
  0.7 16.4 %copy-start.7 = (f32[2,2,8,512]{3,2,1,0:T(8,128)S(1)}, f32[2,2,8,512]{3,2,1,0:T(8,128)}, u32[]{:S(2)}) copy-start(f32[2,2,8,512]{3,2,1,0:T(8,128)} %refs_9_.1) | copy-start | bytes 196612
  4.4 31.4 %collective-permute-start.2 = (f32[2,4,2,10,512]{4,3,2,1,0:T(8,128)}, f32[2,4,2,10,512]{4,3,2,1,0:T(8,128)S(1)}, u32[]{:S(2)}, u32[]{:S(2)}) collective-permute-start(f32[2,4,2,10,512]{4,3,2,1,0:T(8,128)} %get-tuple-element.43), channel_id=1, source_target_pairs={{252,0},{0,4},{4,8},{8,12},{12,16},{16,20},{20,24},{24,28},{28,32}... | collective-permute-start | bytes 983048 | tf_op jit(solution)/shard_map/edge_exchange_0/ppermute | solution.py:25
  4.4 34.8 %collective-permute-start = (f32[2,4,2,10,512]{4,3,2,1,0:T(8,128)}, f32[2,4,2,10,512]{4,3,2,1,0:T(8,128)S(1)}, u32[]{:S(2)}, u32[]{:S(2)}) collective-permute-start(f32[2,4,2,10,512]{4,3,2,1,0:T(8,128)} %get-tuple-element.41), channel_id=1, source_target_pairs={{4,0},{8,4},{12,8},{16,12},{20,16},{24,20},{28,24},{32,28},{36,32}... | collective-permute-start | bytes 983048 | tf_op jit(solution)/shard_map/edge_exchange_0/ppermute | solution.py:25
  37.7 1.2 %copy-start.4 = (f32[2,4,2,10,512]{4,3,2,1,0:T(8,128)S(1)}, f32[2,4,2,10,512]{4,3,2,1,0:T(8,128)}, u32[]{:S(2)}) copy-start(f32[2,4,2,10,512]{4,3,2,1,0:T(8,128)} %get-tuple-element.42) | copy-start | bytes 983044
  39.2 3.4 %copy-start.1 = (f32[2,4,2,10,512]{4,3,2,1,0:T(8,128)}, f32[2,4,2,10,512]{4,3,2,1,0:T(8,128)S(1)}, u32[]{:S(2)}) copy-start(f32[2,4,2,10,512]{4,3,2,1,0:T(8,128)S(1)} %get-tuple-element.55.refs_6_) | copy-start | bytes 983044
  41.1 1.2 %copy-start.3 = (f32[2,4,2,10,512]{4,3,2,1,0:T(8,128)S(1)}, f32[2,4,2,10,512]{4,3,2,1,0:T(8,128)}, u32[]{:S(2)}) copy-start(f32[2,4,2,10,512]{4,3,2,1,0:T(8,128)} %get-tuple-element.40) | copy-start | bytes 983044
  42.6 27.1 %copy-start.2 = (f32[2,4,2,10,512]{4,3,2,1,0:T(8,128)}, f32[2,4,2,10,512]{4,3,2,1,0:T(8,128)S(1)}, u32[]{:S(2)}) copy-start(f32[2,4,2,10,512]{4,3,2,1,0:T(8,128)S(1)} %get-tuple-element.53.refs_7_) | copy-start | bytes 983044
  42.6 23.5 %collective-permute-start.3 = (f32[2,4,2,10,512]{4,3,2,1,0:T(8,128)S(1)}, f32[2,4,2,10,512]{4,3,2,1,0:T(8,128)S(1)}, u32[]{:S(2)}, u32[]{:S(2)}) collective-permute-start(f32[2,4,2,10,512]{4,3,2,1,0:T(8,128)S(1)} %get-tuple-element.55.refs_6_), channel_id=1, source_target_pairs={{4,0},{8,4},{12,8},{16,12},{20,16},{24,20},{28,24},{32,28},{36,32}... | collective-permute-start | bytes 983048 | tf_op jit(solution)/shard_map/edge_exchange_1/ppermute | solution.py:25
  43.1 24.8 %collective-permute-start.1 = (f32[2,4,2,10,512]{4,3,2,1,0:T(8,128)S(1)}, f32[2,4,2,10,512]{4,3,2,1,0:T(8,128)S(1)}, u32[]{:S(2)}, u32[]{:S(2)}) collective-permute-start(f32[2,4,2,10,512]{4,3,2,1,0:T(8,128)S(1)} %get-tuple-element.53.refs_7_), channel_id=1, source_target_pairs={{252,0},{0,4},{4,8},{8,12},{12,16},{16,20},{20,24},{24,28},{28,32}... | collective-permute-start | bytes 983048 | tf_op jit(solution)/shard_map/edge_exchange_1/ppermute | solution.py:25
  66.1 3.6 %copy-start.5 = (f32[2,4,2,10,512]{4,3,2,1,0:T(8,128)}, f32[2,4,2,10,512]{4,3,2,1,0:T(8,128)S(1)}, u32[]{:S(2)}) copy-start(f32[2,4,2,10,512]{4,3,2,1,0:T(8,128)S(1)} %collective-permute-done.3.refs_3_) | copy-start | bytes 983044
  67.9 1.8 %copy-start.6 = (f32[2,4,2,10,512]{4,3,2,1,0:T(8,128)}, f32[2,4,2,10,512]{4,3,2,1,0:T(8,128)S(1)}, u32[]{:S(2)}) copy-start(f32[2,4,2,10,512]{4,3,2,1,0:T(8,128)S(1)} %collective-permute-done.1.refs_2_) | copy-start | bytes 983044
  77.1 9.6 %collective-permute-start.4 = (f32[2,8,512]{2,1,0:T(8,128)}, f32[2,8,512]{2,1,0:T(8,128)S(1)}, u32[]{:S(2)}, u32[]{:S(2)}) collective-permute-start(f32[2,8,512]{2,1,0:T(8,128)} %get-tuple-element.47), channel_id=1, source_target_pairs={{3,0},{0,1},{1,2},{2,3},{7,4},{4,5},{5,6},{6,7},{11,8},{8,9},{9,10... | collective-permute-start | bytes 98312 | tf_op jit(solution)/shard_map/mode_reduce/ppermute | solution.py:25
  84.8 5.0 %collective-permute-start.5 = (f32[2,8,512]{2,1,0:T(8,128)}, f32[2,8,512]{2,1,0:T(8,128)S(1)}, u32[]{:S(2)}, u32[]{:S(2)}) collective-permute-start(f32[2,8,512]{2,1,0:T(8,128)} %get-tuple-element.47), channel_id=1, source_target_pairs={{2,0},{3,1},{0,2},{1,3},{6,4},{7,5},{4,6},{5,7},{10,8},{11,9},{8,1... | collective-permute-start | bytes 98312 | tf_op jit(solution)/shard_map/mode_reduce/ppermute | solution.py:25
  84.8 5.0 %collective-permute-start.6 = (f32[2,8,512]{2,1,0:T(8,128)}, f32[2,8,512]{2,1,0:T(8,128)S(1)}, u32[]{:S(2)}, u32[]{:S(2)}) collective-permute-start(f32[2,8,512]{2,1,0:T(8,128)} %get-tuple-element.47), channel_id=1, source_target_pairs={{1,0},{2,1},{3,2},{0,3},{5,4},{6,5},{7,6},{4,7},{9,8},{10,9},{11,1... | collective-permute-start | bytes 98312 | tf_op jit(solution)/shard_map/mode_reduce/ppermute | solution.py:25

commit v5 on v4

--- a/solution.py
+++ b/solution.py
@@ -390,12 +390,12 @@
         )
     with jax.named_scope("mode_reduce"):
         count = lax.axis_size("mode")
-        me = lax.axis_index("mode")
-        stacked = jnp.stack([sens] + [shifted(sens, "mode", k) for k in range(1, count)])
-        total = None
-        for j in range(count):
-            part = lax.dynamic_index_in_dim(stacked, (me - j) % count, axis=0, keepdims=False)
-            total = part if total is None else total + part
+        total = sens
+        span = 1
+        while span < count:
+            route = [(i, i ^ span) for i in range(count)]
+            total = total + lax.ppermute(total, "mode", route)
+            span *= 2
         sensitivity = total / (STEPS * modes_total)
     return (q2, a2, sensitivity)
 

time: 92.9 us -> 98.9 us (1.065)
  waiting for transfers between devices: 32.5 us -> 38.1 us
  starting transfers between devices: 20.2 us -> 21.4 us
    ppermute x0 -> x2, waiting for transfers between devices: none -> 7.94 us  [per_device(): total = total + lax.ppermute(total, 'mode', route)]
    ppermute x7 -> x4, waiting for transfers between devices: 32.5 us -> 30.1 us  [shifted(): return lax.ppermute(block, axis, route)]
    ppermute x0 -> x2, starting transfers between devices: none -> 1.08 us  [per_device(): total = total + lax.ppermute(total, 'mode', route)]
    ppermute x7 -> x4, starting transfers between devices: 20.2 us -> 20.3 us  [shifted(): return lax.ppermute(block, axis, route)]
  transfers between devices with their start and end apart: 7 -> 6, of which waited for: 4 -> 5; matrix products, arithmetic and copies ran while one was open for 14% -> 12% of each run, Pallas kernels for 7% -> 7%
where the time goes in v5:
time: 98.9 us; the launch traced here: 98 us
  waiting for transfers between devices  38.1 us (39%)
  starting transfers between devices  21.4 us (22%)
  Pallas kernels  17.8 us (18%)
  local copies, waits for them, and re-layouts  7.8 us (8%)
  other arithmetic  6.24 us (6%)
  matrix products  5.65 us (6%)
  between operations  1.06 us (1%)
    ppermute x4, waiting for transfers between devices, shifted(): return lax.ppermute(block, axis, route)  30.1 us
    ppermute x4, starting transfers between devices, shifted(): return lax.ppermute(block, axis, route)  20.3 us
    pallas_call x2, Pallas kernels, run_step(): pl.pallas_call(kernel, grid_spec=grid_spec, out_shape=out_shape, compiler...  14.1 us
    ppermute x2, waiting for transfers between devices, per_device(): total = total + lax.ppermute(total, 'mode', route)  7.94 us
    dot_general x4, matrix products, reverse_lanes(): jnp.dot(flat, turn, precision=lax.Precision.HIGHEST, preferred_element_ty...  5.65 us
    pallas_call x1, Pallas kernels, edge_rows(): pl.pallas_call(edge_kernel, grid=(modes,), in_specs=[state_spec, state_sp...  3.7 us
    scatter-add x2, local copies, waits for them, and re-layouts, per_device(): sens = sens.at[:, 0, :].add(s0).at[:, height - 1, :].add(s7)  2.78 us
  transfers between devices with their start and end apart: 6, of which 5 were waited for; matrix products, arithmetic and copies ran while one was open for 12% of the time, Pallas kernels for 7%

profile of v5, /device:TPU:32, one launch (start us, length us, event | category | flops | bytes accessed | tf_op | source)
XLA Modules:
  0.0 98.0 jit_solution(17218454366603544619)
XLA Ops:
  0.7 3.7 %edge_exchange_0.1 = (f32[2,4,2,10,512]{4,3,2,1,0:T(8,128)}, f32[2,4,2,10,512]{4,3,2,1,0:T(8,128)}) custom-call(f32[4,2,5,2,8,512]{5,4,3,2,1,0:T(8,128)} %x_ref.1, f32[4,2,5,2,8,512]{5,4,3,2,1,0:T(8,128)} %a_ref.1), custom_call_target="tpu_custom_call" | custom-call | tf_op jit(solution)/shard_map/edge_exchange_0/pallas_call | solution.py:348
  4.4 10.4 %collective-permute-start = (f32[2,4,2,10,512]{4,3,2,1,0:T(8,128)}, f32[2,4,2,10,512]{4,3,2,1,0:T(8,128)S(1)}, u32[]{:S(2)}, u32[]{:S(2)}) collective-permute-start(f32[2,4,2,10,512]{4,3,2,1,0:T(8,128)} %get-tuple-element.41), channel_id=1, source_target_pairs={{4,0},{8,4},{12,8},{16,12},{20,16},{24,20},{28,24},{32,28},{36,32}... | collective-permute-start | bytes 983048 | tf_op jit(solution)/shard_map/edge_exchange_0/ppermute | solution.py:25
  14.8 0.2 compare_reduce_fusion
  15.1 0.6 gather_fusion
  15.8 0.1 reshape.2389
  15.9 0.2 slice_reduce_fusion.1
  16.1 0.8 fusion.45
  17.0 0.1 stack.145
  17.1 0.1 reshape.2369
  17.2 0.8 slice_multiply_fusion.2
  18.1 0.7 pad_add_fusion.tbl
  18.7 6.6 %flow_step_0.1 = (f32[4,2,5,2,8,512]{5,4,3,2,1,0:T(8,128)}, f32[4,2,5,2,8,512]{5,4,3,2,1,0:T(8,128)}, f32[2,8,512]{2,1,0:T(8,128)}, f32[2,4,2,10,512]{4,3,2,1,0:T(8,128)}, f32[2,4,2,10,512]{4,3,2,1,0:T(8,128)}) custom-call(s32[17]{0:T(128)} %pad_add_fusion.tbl, f32[4,2,5,2,8,512]{5,4,3,2,1,0:T(8,128)} %x_ref.1, f32[4,2,5,2,8,512]{5,4,3,2,1,0:T(8,128)} %a_ref.1, ...), custom_call_target="tpu_custom_call" | custom-call | tf_op jit(solution)/shard_map/flow_step_0/pallas_call | solution.py:270
  25.4 8.6 %collective-permute-done = f32[2,4,2,10,512]{4,3,2,1,0:T(8,128)S(1)} collective-permute-done((f32[2,4,2,10,512]{4,3,2,1,0:T(8,128)}, f32[2,4,2,10,512]{4,3,2,1,0:T(8,128)S(1)}, u32[]{:S(2)}, u32[]{:S(2)}) %collective-permute-start) | collective-permute-done | bytes 327712 | tf_op jit(solution)/shard_map/edge_exchange_0/ppermute | solution.py:25
  34.0 0.6 gather_fusion.1
  34.6 1.1 %convolution_select_fusion.1 = f32[2,4,2,10,512]{4,3,1,0,2:T(8,128)S(1)} fusion(f32[2,2,4,10,512]{4,3,2,1,0:T(8,128)S(1)} %gather_fusion.1, pred[2]{0:T(512)(128)(4,1)S(1)} %compare_and_fusion.1, pred[2]{0:T(512)(128)(4,1)S(1)} %get-tuple-element.49), kind=kOutput, calls=%fused_computation.6 | convolution fusion | flops 504348672 | bytes 655364 | tf_op jit(solution)/shard_map/edge_fix_0/dot_general | solution.py:327
  35.7 0.1 copy.116
  35.9 0.1 copy.127
  36.0 3.3 %collective-permute-done.2 = f32[2,4,2,10,512]{4,3,2,1,0:T(8,128)S(1)} collective-permute-done((f32[2,4,2,10,512]{4,3,2,1,0:T(8,128)}, f32[2,4,2,10,512]{4,3,2,1,0:T(8,128)S(1)}, u32[]{:S(2)}, u32[]{:S(2)}) %collective-permute-start.2) | collective-permute-done | bytes 327712 | tf_op jit(solution)/shard_map/edge_exchange_0/ppermute | solution.py:25
  39.3 0.6 gather_fusion.2
  39.9 1.1 %convolution_select_fusion = f32[2,4,2,10,512]{4,3,1,0,2:T(8,128)S(1)} fusion(f32[2,2,4,10,512]{4,3,2,1,0:T(8,128)S(1)} %gather_fusion.2, pred[2]{0:T(512)(128)(4,1)S(1)} %compare_and_fusion, pred[2]{0:T(512)(128)(4,1)S(1)} %get-tuple-element.48), kind=kOutput, calls=%fused_computation.5 | convolution fusion | flops 504348672 | bytes 655364 | tf_op jit(solution)/shard_map/edge_fix_0/dot_general | solution.py:327
  41.0 0.1 copy.140
  41.2 0.1 copy.152
  41.3 0.1 add_bitcast_fusion.12
  41.4 0.4 add_bitcast_fusion.11
  41.8 0.3 stack.179
  42.1 0.3 stack.190
  42.4 0.1 multiply_add_fusion.1
  42.5 0.2 multiply_reduce_fusion.1
  42.7 0.1 add_bitcast_fusion.32
  42.8 0.4 add_bitcast_fusion.31
  43.2 0.3 stack.156
  43.5 0.3 stack.167
  43.7 0.1 multiply_add_fusion.3
  43.8 0.2 multiply_reduce_fusion
  44.1 9.9 %collective-permute-start.3 = (f32[2,4,2,10,512]{4,3,2,1,0:T(8,128)S(1)}, f32[2,4,2,10,512]{4,3,2,1,0:T(8,128)S(1)}, u32[]{:S(2)}, u32[]{:S(2)}) collective-permute-start(f32[2,4,2,10,512]{4,3,2,1,0:T(8,128)S(1)} %get-tuple-element.55.refs_6_), channel_id=1, source_target_pairs={{4,0},{8,4},{12,8},{16,12},{20,16},{24,20},{28,24},{32,28},{36,32}... | collective-permute-start | bytes 983048 | tf_op jit(solution)/shard_map/edge_exchange_1/ppermute | solution.py:25
  54.0 0.8 reshape_add_fusion
  54.8 1.4 %scatter-add.6 = f32[2,8,512]{2,1,0:T(8,128)} dynamic-update-slice(f32[2,8,512]{2,1,0:T(8,128)} %get-tuple-element.44, f32[2,1,512]{2,1,0:T(1,128)S(1)} %reshape_add_fusion, s32[]{:T(128)} %constant.109.clone.1, s32[]{:T(128)} %constant.109.clone.1, s32[]{:T(128)} %constant.109.clone.1) | dynamic-update-slice | bytes 8196 | tf_op jit(solution)/shard_map/edge_fix_0/scatter-add | solution.py:383
  56.2 0.8 slice_add_fusion
  56.9 1.4 %scatter-add.9.refs_11_ = f32[2,8,512]{2,1,0:T(8,128)} dynamic-update-slice(f32[2,8,512]{2,1,0:T(8,128)} %scatter-add.6, f32[2,1,512]{2,1,0:T(1,128)S(1)} %slice_add_fusion, s32[]{:T(128)} %constant.109.clone.1, s32[]{:T(128)} %constant.125.clone.1, s32[]{:T(128)} %constant.109.clone.1) | dynamic-update-slice | bytes 8196 | tf_op jit(solution)/shard_map/edge_fix_0/scatter-add | solution.py:383
  58.3 18.3 %collective-permute-done.1.refs_2_ = f32[2,4,2,10,512]{4,3,2,1,0:T(8,128)S(1)} collective-permute-done((f32[2,4,2,10,512]{4,3,2,1,0:T(8,128)S(1)}, f32[2,4,2,10,512]{4,3,2,1,0:T(8,128)S(1)}, u32[]{:S(2)}, u32[]{:S(2)}) %collective-permute-start.1) | collective-permute-done | bytes 327712 | tf_op jit(solution)/shard_map/edge_exchange_1/ppermute | solution.py:25
  76.6 1.8 %fusion.1.refs_4_ = f32[2,4,2,10,512]{4,3,2,1,0:T(8,128)} fusion(f32[2,4,2,10,512]{4,3,2,1,0:T(8,128)S(1)} %collective-permute-done.1.refs_2_), kind=kOutput, calls=%fused_computation.8 | convolution fusion | flops 504102912 | bytes 655360 | tf_op jit(solution)/shard_map/flow_step_1/dot_general | solution.py:327
  78.4 1.8 %fusion.refs_5_ = f32[2,4,2,10,512]{4,3,2,1,0:T(8,128)} fusion(f32[2,4,2,10,512]{4,3,2,1,0:T(8,128)S(1)} %collective-permute-done.3.refs_3_), kind=kOutput, calls=%fused_computation.7 | convolution fusion | flops 504102912 | bytes 655360 | tf_op jit(solution)/shard_map/flow_step_1/dot_general | solution.py:327
  80.1 7.5 %flow_step_1.1 = (f32[4,2,5,2,8,512]{5,4,3,2,1,0:T(8,128)}, f32[4,2,5,2,8,512]{5,4,3,2,1,0:T(8,128)}, f32[2,8,512]{2,1,0:T(8,128)}) custom-call(s32[17]{0:T(128)} %pad_add_fusion.tbl, f32[4,2,5,2,8,512]{5,4,3,2,1,0:T(8,128)} %get-tuple-element.38.refs_0_, f32[4,2,5,2,8,512]{5,4,3,2,1,0:T(8,128)} %get-tuple-element.39.refs_1_, ...), custom_call_target="tpu_custom_call" | custom-call | tf_op jit(solution)/shard_map/flow_step_1/pallas_call | solution.py:270
  87.6 1.1 %collective-permute-start.4 = (f32[2,8,512]{2,1,0:T(8,128)}, f32[2,8,512]{2,1,0:T(8,128)S(1)}, u32[]{:S(2)}, u32[]{:S(2)}) collective-permute-start(f32[2,8,512]{2,1,0:T(8,128)} %get-tuple-element.47), channel_id=1, source_target_pairs={{0,1},{1,0},{2,3},{3,2},{4,5},{5,4},{6,7},{7,6},{8,9},{9,8},{10,11... | collective-permute-start | bytes 98312 | tf_op jit(solution)/shard_map/mode_reduce/ppermute | solution.py:397
  88.7 3.1 %collective-permute-done.4 = f32[2,8,512]{2,1,0:T(8,128)S(1)} collective-permute-done((f32[2,8,512]{2,1,0:T(8,128)}, f32[2,8,512]{2,1,0:T(8,128)S(1)}, u32[]{:S(2)}, u32[]{:S(2)}) %collective-permute-start.4) | collective-permute-done | bytes 32800 | tf_op jit(solution)/shard_map/mode_reduce/ppermute | solution.py:397
  91.8 0.8 add.1155
  92.6 4.8 %collective-permute-done.5 = f32[2,8,512]{2,1,0:T(8,128)S(1)} collective-permute-done((f32[2,8,512]{2,1,0:T(8,128)S(1)}, f32[2,8,512]{2,1,0:T(8,128)S(1)}, u32[]{:S(2)}, u32[]{:S(2)}) %collective-permute-start.5) | collective-permute-done | bytes 32800 | tf_op jit(solution)/shard_map/mode_reduce/ppermute | solution.py:397
  97.4 0.6 add_multiply_fusion
  (52 shorter events, 0.6 us)
Async XLA Ops:
  0.6 14.5 %copy-start = (s32[128]{0:T(128)S(1)}, s32[128]{0:T(128)}, u32[]{:S(2)}) copy-start(s32[128]{0:T(128)} %param.19) | copy-start | bytes 1540
  0.6 14.1 %copy-start.9 = (s32[2,4]{1,0:T(2,128)S(1)}, s32[2,4]{1,0:T(2,128)}, u32[]{:S(2)}) copy-start(s32[2,4]{1,0:T(2,128)} %param.20) | copy-start | bytes 100
  0.7 14.1 %copy-start.8 = (s32[2,4]{1,0:T(2,128)S(1)}, s32[2,4]{1,0:T(2,128)}, u32[]{:S(2)}) copy-start(s32[2,4]{1,0:T(2,128)} %param.21) | copy-start | bytes 100
  0.7 17.4 %copy-start.7 = (f32[2,2,8,512]{3,2,1,0:T(8,128)S(1)}, f32[2,2,8,512]{3,2,1,0:T(8,128)}, u32[]{:S(2)}) copy-start(f32[2,2,8,512]{3,2,1,0:T(8,128)} %refs_9_.1) | copy-start | bytes 196612
  4.4 29.6 %collective-permute-start = (f32[2,4,2,10,512]{4,3,2,1,0:T(8,128)}, f32[2,4,2,10,512]{4,3,2,1,0:T(8,128)S(1)}, u32[]{:S(2)}, u32[]{:S(2)}) collective-permute-start(f32[2,4,2,10,512]{4,3,2,1,0:T(8,128)} %get-tuple-element.41), channel_id=1, source_target_pairs={{4,0},{8,4},{12,8},{16,12},{20,16},{24,20},{28,24},{32,28},{36,32}... | collective-permute-start | bytes 983048 | tf_op jit(solution)/shard_map/edge_exchange_0/ppermute | solution.py:25
  14.8 24.5 %collective-permute-start.2 = (f32[2,4,2,10,512]{4,3,2,1,0:T(8,128)}, f32[2,4,2,10,512]{4,3,2,1,0:T(8,128)S(1)}, u32[]{:S(2)}, u32[]{:S(2)}) collective-permute-start(f32[2,4,2,10,512]{4,3,2,1,0:T(8,128)} %get-tuple-element.43), channel_id=1, source_target_pairs={{252,0},{0,4},{4,8},{8,12},{12,16},{16,20},{20,24},{24,28},{28,32}... | collective-permute-start | bytes 983048 | tf_op jit(solution)/shard_map/edge_exchange_0/ppermute | solution.py:25
  41.1 1.2 %copy-start.4 = (f32[2,4,2,10,512]{4,3,2,1,0:T(8,128)S(1)}, f32[2,4,2,10,512]{4,3,2,1,0:T(8,128)}, u32[]{:S(2)}) copy-start(f32[2,4,2,10,512]{4,3,2,1,0:T(8,128)} %get-tuple-element.42) | copy-start | bytes 983044
  42.5 1.3 %copy-start.3 = (f32[2,4,2,10,512]{4,3,2,1,0:T(8,128)S(1)}, f32[2,4,2,10,512]{4,3,2,1,0:T(8,128)}, u32[]{:S(2)}) copy-start(f32[2,4,2,10,512]{4,3,2,1,0:T(8,128)} %get-tuple-element.40) | copy-start | bytes 983044
  42.6 1.5 %copy-start.1 = (f32[2,4,2,10,512]{4,3,2,1,0:T(8,128)}, f32[2,4,2,10,512]{4,3,2,1,0:T(8,128)S(1)}, u32[]{:S(2)}) copy-start(f32[2,4,2,10,512]{4,3,2,1,0:T(8,128)S(1)} %get-tuple-element.55.refs_6_) | copy-start | bytes 983044
  44.0 36.1 %copy-start.2 = (f32[2,4,2,10,512]{4,3,2,1,0:T(8,128)}, f32[2,4,2,10,512]{4,3,2,1,0:T(8,128)S(1)}, u32[]{:S(2)}) copy-start(f32[2,4,2,10,512]{4,3,2,1,0:T(8,128)S(1)} %get-tuple-element.53.refs_7_) | copy-start | bytes 983044
  44.0 32.5 %collective-permute-start.1 = (f32[2,4,2,10,512]{4,3,2,1,0:T(8,128)S(1)}, f32[2,4,2,10,512]{4,3,2,1,0:T(8,128)S(1)}, u32[]{:S(2)}, u32[]{:S(2)}) collective-permute-start(f32[2,4,2,10,512]{4,3,2,1,0:T(8,128)S(1)} %get-tuple-element.53.refs_7_), channel_id=1, source_target_pairs={{252,0},{0,4},{4,8},{8,12},{12,16},{16,20},{20,24},{24,28},{28,32}... | collective-permute-start | bytes 983048 | tf_op jit(solution)/shard_map/edge_exchange_1/ppermute | solution.py:25
  44.1 34.2 %collective-permute-start.3 = (f32[2,4,2,10,512]{4,3,2,1,0:T(8,128)S(1)}, f32[2,4,2,10,512]{4,3,2,1,0:T(8,128)S(1)}, u32[]{:S(2)}, u32[]{:S(2)}) collective-permute-start(f32[2,4,2,10,512]{4,3,2,1,0:T(8,128)S(1)} %get-tuple-element.55.refs_6_), channel_id=1, source_target_pairs={{4,0},{8,4},{12,8},{16,12},{20,16},{24,20},{28,24},{32,28},{36,32}... | collective-permute-start | bytes 983048 | tf_op jit(solution)/shard_map/edge_exchange_1/ppermute | solution.py:25
  76.6 3.6 %copy-start.5 = (f32[2,4,2,10,512]{4,3,2,1,0:T(8,128)}, f32[2,4,2,10,512]{4,3,2,1,0:T(8,128)S(1)}, u32[]{:S(2)}) copy-start(f32[2,4,2,10,512]{4,3,2,1,0:T(8,128)S(1)} %collective-permute-done.1.refs_2_) | copy-start | bytes 983044
  78.4 1.8 %copy-start.6 = (f32[2,4,2,10,512]{4,3,2,1,0:T(8,128)}, f32[2,4,2,10,512]{4,3,2,1,0:T(8,128)S(1)}, u32[]{:S(2)}) copy-start(f32[2,4,2,10,512]{4,3,2,1,0:T(8,128)S(1)} %collective-permute-done.3.refs_3_) | copy-start | bytes 983044
  87.6 4.2 %collective-permute-start.4 = (f32[2,8,512]{2,1,0:T(8,128)}, f32[2,8,512]{2,1,0:T(8,128)S(1)}, u32[]{:S(2)}, u32[]{:S(2)}) collective-permute-start(f32[2,8,512]{2,1,0:T(8,128)} %get-tuple-element.47), channel_id=1, source_target_pairs={{0,1},{1,0},{2,3},{3,2},{4,5},{5,4},{6,7},{7,6},{8,9},{9,8},{10,11... | collective-permute-start | bytes 98312 | tf_op jit(solution)/shard_map/mode_reduce/ppermute | solution.py:397
  92.6 4.8 %collective-permute-start.5 = (f32[2,8,512]{2,1,0:T(8,128)S(1)}, f32[2,8,512]{2,1,0:T(8,128)S(1)}, u32[]{:S(2)}, u32[]{:S(2)}) collective-permute-start(f32[2,8,512]{2,1,0:T(8,128)S(1)} %add.1155), channel_id=1, source_target_pairs={{0,2},{1,3},{2,0},{3,1},{4,6},{5,7},{6,4},{7,5},{8,10},{9,11},{10,... | collective-permute-start | bytes 98312 | tf_op jit(solution)/shard_map/mode_reduce/ppermute | solution.py:397

commit v6 on v4

--- a/solution.py
+++ b/solution.py
@@ -329,29 +329,21 @@
 
 
 def edge_kernel(x_ref, a_ref, lo_ref, hi_ref):
-    nv = x_ref.shape[2]
-    height = x_ref.shape[4]
+    modes, parts, nv, slots, height, _ = x_ref.shape
     for arr, src in enumerate((x_ref, a_ref)):
-        for p in range(x_ref.shape[1]):
-            for n in range(nv):
-                k = p * nv + n
-                for s in range(x_ref.shape[3]):
-                    lo_ref[arr, 0, s, pl.ds(k, 1), :] = src[0, p, n, s, 0:1, :]
-                    hi_ref[arr, 0, s, pl.ds(k, 1), :] = src[0, p, n, s, height - 1:height, :]
+        for m in range(modes):
+            for p in range(parts):
+                for n in range(nv):
+                    k = p * nv + n
+                    for s in range(slots):
+                        lo_ref[arr, m, s, pl.ds(k, 1), :] = src[m, p, n, s, 0:1, :]
+                        hi_ref[arr, m, s, pl.ds(k, 1), :] = src[m, p, n, s, height - 1:height, :]
 
 
 def edge_rows(x, a):
     modes, parts, nv, slots, height, width = x.shape
-    state_spec = pl.BlockSpec((1, parts, nv, slots, height, width), lambda m: (m, 0, 0, 0, 0, 0))
-    edge_spec = pl.BlockSpec((2, 1, slots, parts * nv, width), lambda m: (0, m, 0, 0, 0))
     edge_shape = jax.ShapeDtypeStruct((2, modes, slots, parts * nv, width), jnp.float32)
-    return pl.pallas_call(
-        edge_kernel,
-        grid=(modes,),
-        in_specs=[state_spec, state_spec],
-        out_specs=[edge_spec, edge_spec],
-        out_shape=[edge_shape, edge_shape],
-    )(x, a)
+    return pl.pallas_call(edge_kernel, out_shape=[edge_shape, edge_shape])(x, a)
 
 
 def per_device(direct, adjoint, density, velocity, pressure, block_home, face_nbr, face_flip):

time: 92.9 us -> 92 us (level)
  transfers between devices with their start and end apart: 7 -> 7, of which waited for: 4 -> 4; matrix products, arithmetic and copies ran while one was open for 14% -> 15% of each run, Pallas kernels for 7% -> 7%
where the time goes in v6:
time: 92 us; the launch traced here: 90.4 us
  waiting for transfers between devices  32.5 us (35%)
  starting transfers between devices  20.2 us (22%)
  Pallas kernels  17 us (18%)
  local copies, waits for them, and re-layouts  7.79 us (8%)
  other arithmetic  6.19 us (7%)
  matrix products  5.67 us (6%)
  between operations  1.05 us (1%)
    ppermute x7, waiting for transfers between devices, shifted(): return lax.ppermute(block, axis, route)  32.5 us
    ppermute x7, starting transfers between devices, shifted(): return lax.ppermute(block, axis, route)  20.2 us
    pallas_call x2, Pallas kernels, run_step(): pl.pallas_call(kernel, grid_spec=grid_spec, out_shape=out_shape, compiler...  14.1 us
    dot_general x4, matrix products, reverse_lanes(): jnp.dot(flat, turn, precision=lax.Precision.HIGHEST, preferred_element_ty...  5.67 us
    pallas_call x1, Pallas kernels, edge_rows(): return pl.pallas_call(edge_kernel, out_shape=[edge_shape, edge_shape])(x, a)  2.89 us
    scatter-add x2, local copies, waits for them, and re-layouts, per_device(): sens = sens.at[:, 0, :].add(s0).at[:, height - 1, :].add(s7)  2.78 us
  transfers between devices with their start and end apart: 7, of which 4 were waited for; matrix products, arithmetic and copies ran while one was open for 15% of the time, Pallas kernels for 7%

profile of v6, /device:TPU:32, one launch (start us, length us, event | category | flops | bytes accessed | tf_op | source)
XLA Modules:
  0.0 90.4 jit_solution(437288662139082868)
XLA Ops:
  0.7 2.9 %edge_exchange_0.1 = (f32[2,4,2,10,512]{4,3,2,1,0:T(8,128)}, f32[2,4,2,10,512]{4,3,2,1,0:T(8,128)}) custom-call(f32[4,2,5,2,8,512]{5,4,3,2,1,0:T(8,128)} %x_ref.1, f32[4,2,5,2,8,512]{5,4,3,2,1,0:T(8,128)} %a_ref.1), custom_call_target="tpu_custom_call" | custom-call | tf_op jit(solution)/shard_map/edge_exchange_0/pallas_call | solution.py:346
  3.6 10.4 %collective-permute-start = (f32[2,4,2,10,512]{4,3,2,1,0:T(8,128)}, f32[2,4,2,10,512]{4,3,2,1,0:T(8,128)S(1)}, u32[]{:S(2)}, u32[]{:S(2)}) collective-permute-start(f32[2,4,2,10,512]{4,3,2,1,0:T(8,128)} %get-tuple-element.41), channel_id=1, source_target_pairs={{4,0},{8,4},{12,8},{16,12},{20,16},{24,20},{28,24},{32,28},{36,32}... | collective-permute-start | bytes 983048 | tf_op jit(solution)/shard_map/edge_exchange_0/ppermute | solution.py:25
  14.1 0.6 gather_fusion
  14.8 0.2 slice_reduce_fusion.1
  15.0 0.8 fusion.45
  15.9 0.2 compare_reduce_fusion
  16.2 0.8 slice_multiply_fusion.2
  17.1 0.1 stack.160
  17.2 0.1 reshape.2374
  17.2 0.6 pad_add_fusion.tbl
  17.8 6.6 %flow_step_0.1 = (f32[4,2,5,2,8,512]{5,4,3,2,1,0:T(8,128)}, f32[4,2,5,2,8,512]{5,4,3,2,1,0:T(8,128)}, f32[2,8,512]{2,1,0:T(8,128)}, f32[2,4,2,10,512]{4,3,2,1,0:T(8,128)}, f32[2,4,2,10,512]{4,3,2,1,0:T(8,128)}) custom-call(s32[17]{0:T(128)} %pad_add_fusion.tbl, f32[4,2,5,2,8,512]{5,4,3,2,1,0:T(8,128)} %x_ref.1, f32[4,2,5,2,8,512]{5,4,3,2,1,0:T(8,128)} %a_ref.1, ...), custom_call_target="tpu_custom_call" | custom-call | tf_op jit(solution)/shard_map/flow_step_0/pallas_call | solution.py:270
  24.5 10.5 %collective-permute-done.2 = f32[2,4,2,10,512]{4,3,2,1,0:T(8,128)S(1)} collective-permute-done((f32[2,4,2,10,512]{4,3,2,1,0:T(8,128)}, f32[2,4,2,10,512]{4,3,2,1,0:T(8,128)S(1)}, u32[]{:S(2)}, u32[]{:S(2)}) %collective-permute-start.2) | collective-permute-done | bytes 327712 | tf_op jit(solution)/shard_map/edge_exchange_0/ppermute | solution.py:25
  35.0 0.6 gather_fusion.2
  35.6 1.1 %convolution_select_fusion = f32[2,4,2,10,512]{4,3,1,0,2:T(8,128)S(1)} fusion(f32[2,2,4,10,512]{4,3,2,1,0:T(8,128)S(1)} %gather_fusion.2, pred[2]{0:T(512)(128)(4,1)S(1)} %compare_and_fusion, pred[2]{0:T(512)(128)(4,1)S(1)} %get-tuple-element.48), kind=kOutput, calls=%fused_computation.5 | convolution fusion | flops 504348672 | bytes 655364 | tf_op jit(solution)/shard_map/edge_fix_0/dot_general | solution.py:327
  36.7 0.1 copy.140
  36.8 0.1 copy.152
  37.0 0.1 add_bitcast_fusion.12
  37.1 0.4 add_bitcast_fusion.11
  37.5 0.3 stack.205
  37.8 0.3 stack.194
  38.0 0.1 multiply_add_fusion.1
  38.1 0.2 multiply_reduce_fusion.1
  38.4 0.6 gather_fusion.1
  39.0 1.1 %convolution_select_fusion.1 = f32[2,4,2,10,512]{4,3,1,0,2:T(8,128)S(1)} fusion(f32[2,2,4,10,512]{4,3,2,1,0:T(8,128)S(1)} %gather_fusion.1, pred[2]{0:T(512)(128)(4,1)S(1)} %compare_and_fusion.1, pred[2]{0:T(512)(128)(4,1)S(1)} %get-tuple-element.49), kind=kOutput, calls=%fused_computation.6 | convolution fusion | flops 504348672 | bytes 655364 | tf_op jit(solution)/shard_map/edge_fix_0/dot_general | solution.py:327
  40.1 0.1 copy.127
  40.2 0.1 copy.116
  40.4 0.1 add_bitcast_fusion.32
  40.5 0.4 add_bitcast_fusion.31
  40.9 0.3 stack.182
  41.2 0.3 stack.171
  41.4 0.1 multiply_add_fusion.3
  41.5 0.2 multiply_reduce_fusion
  41.7 0.5 collective-permute-start.3
  42.2 0.1 collective-permute-start.1
  42.3 0.8 reshape_add_fusion
  43.1 1.4 %scatter-add.6 = f32[2,8,512]{2,1,0:T(8,128)} dynamic-update-slice(f32[2,8,512]{2,1,0:T(8,128)} %get-tuple-element.44, f32[2,1,512]{2,1,0:T(1,128)S(1)} %reshape_add_fusion, s32[]{:T(128)} %constant.145.clone.1, s32[]{:T(128)} %constant.145.clone.1, s32[]{:T(128)} %constant.145.clone.1) | dynamic-update-slice | bytes 8196 | tf_op jit(solution)/shard_map/edge_fix_0/scatter-add | solution.py:375
  44.5 0.8 slice_add_fusion
  45.3 1.4 %scatter-add.9.refs_11_ = f32[2,8,512]{2,1,0:T(8,128)} dynamic-update-slice(f32[2,8,512]{2,1,0:T(8,128)} %scatter-add.6, f32[2,1,512]{2,1,0:T(1,128)S(1)} %slice_add_fusion, s32[]{:T(128)} %constant.145.clone.1, s32[]{:T(128)} %constant.161.clone.1, s32[]{:T(128)} %constant.145.clone.1) | dynamic-update-slice | bytes 8196 | tf_op jit(solution)/shard_map/edge_fix_0/scatter-add | solution.py:375
  46.7 18.5 %collective-permute-done.3.refs_3_ = f32[2,4,2,10,512]{4,3,2,1,0:T(8,128)S(1)} collective-permute-done((f32[2,4,2,10,512]{4,3,2,1,0:T(8,128)S(1)}, f32[2,4,2,10,512]{4,3,2,1,0:T(8,128)S(1)}, u32[]{:S(2)}, u32[]{:S(2)}) %collective-permute-start.3) | collective-permute-done | bytes 327712 | tf_op jit(solution)/shard_map/edge_exchange_1/ppermute | solution.py:25
  65.2 1.8 %fusion.refs_5_ = f32[2,4,2,10,512]{4,3,2,1,0:T(8,128)} fusion(f32[2,4,2,10,512]{4,3,2,1,0:T(8,128)S(1)} %collective-permute-done.3.refs_3_), kind=kOutput, calls=%fused_computation.7 | convolution fusion | flops 504102912 | bytes 655360 | tf_op jit(solution)/shard_map/flow_step_1/dot_general | solution.py:327
  67.0 1.8 %fusion.1.refs_4_ = f32[2,4,2,10,512]{4,3,2,1,0:T(8,128)} fusion(f32[2,4,2,10,512]{4,3,2,1,0:T(8,128)S(1)} %collective-permute-done.1.refs_2_), kind=kOutput, calls=%fused_computation.8 | convolution fusion | flops 504102912 | bytes 655360 | tf_op jit(solution)/shard_map/flow_step_1/dot_general | solution.py:327
  68.8 7.5 %flow_step_1.1 = (f32[4,2,5,2,8,512]{5,4,3,2,1,0:T(8,128)}, f32[4,2,5,2,8,512]{5,4,3,2,1,0:T(8,128)}, f32[2,8,512]{2,1,0:T(8,128)}) custom-call(s32[17]{0:T(128)} %pad_add_fusion.tbl, f32[4,2,5,2,8,512]{5,4,3,2,1,0:T(8,128)} %get-tuple-element.38.refs_0_, f32[4,2,5,2,8,512]{5,4,3,2,1,0:T(8,128)} %get-tuple-element.39.refs_1_, ...), custom_call_target="tpu_custom_call" | custom-call | tf_op jit(solution)/shard_map/flow_step_1/pallas_call | solution.py:270
  76.3 7.7 %collective-permute-start.4 = (f32[2,8,512]{2,1,0:T(8,128)}, f32[2,8,512]{2,1,0:T(8,128)S(1)}, u32[]{:S(2)}, u32[]{:S(2)}) collective-permute-start(f32[2,8,512]{2,1,0:T(8,128)} %get-tuple-element.47), channel_id=1, source_target_pairs={{3,0},{0,1},{1,2},{2,3},{7,4},{4,5},{5,6},{6,7},{11,8},{8,9},{9,10... | collective-permute-start | bytes 98312 | tf_op jit(solution)/shard_map/mode_reduce/ppermute | solution.py:25
  83.9 1.6 %collective-permute-start.6 = (f32[2,8,512]{2,1,0:T(8,128)}, f32[2,8,512]{2,1,0:T(8,128)S(1)}, u32[]{:S(2)}, u32[]{:S(2)}) collective-permute-start(f32[2,8,512]{2,1,0:T(8,128)} %get-tuple-element.47), channel_id=1, source_target_pairs={{1,0},{2,1},{3,2},{0,3},{5,4},{6,5},{7,6},{4,7},{9,8},{10,9},{11,1... | collective-permute-start | bytes 98312 | tf_op jit(solution)/shard_map/mode_reduce/ppermute | solution.py:25
  85.5 0.4 collective-permute-done.4
  85.8 3.1 %collective-permute-done.5 = f32[2,8,512]{2,1,0:T(8,128)S(1)} collective-permute-done((f32[2,8,512]{2,1,0:T(8,128)}, f32[2,8,512]{2,1,0:T(8,128)S(1)}, u32[]{:S(2)}, u32[]{:S(2)}) %collective-permute-start.5) | collective-permute-done | bytes 32800 | tf_op jit(solution)/shard_map/mode_reduce/ppermute | solution.py:25
  88.9 0.8 pad_maximum_fusion.2
  89.7 0.6 multiply_bitcast_fusion
  (54 shorter events, 0.6 us)
Async XLA Ops:
  0.6 13.4 %copy-start = (s32[128]{0:T(128)S(1)}, s32[128]{0:T(128)}, u32[]{:S(2)}) copy-start(s32[128]{0:T(128)} %param.19) | copy-start | bytes 1540
  0.6 13.3 %copy-start.9 = (s32[2,4]{1,0:T(2,128)S(1)}, s32[2,4]{1,0:T(2,128)}, u32[]{:S(2)}) copy-start(s32[2,4]{1,0:T(2,128)} %param.20) | copy-start | bytes 100
  0.7 15.2 %copy-start.8 = (s32[2,4]{1,0:T(2,128)S(1)}, s32[2,4]{1,0:T(2,128)}, u32[]{:S(2)}) copy-start(s32[2,4]{1,0:T(2,128)} %param.21) | copy-start | bytes 100
  0.7 15.5 %copy-start.7 = (f32[2,2,8,512]{3,2,1,0:T(8,128)S(1)}, f32[2,2,8,512]{3,2,1,0:T(8,128)}, u32[]{:S(2)}) copy-start(f32[2,2,8,512]{3,2,1,0:T(8,128)} %refs_9_.1) | copy-start | bytes 196612
  3.6 31.4 %collective-permute-start.2 = (f32[2,4,2,10,512]{4,3,2,1,0:T(8,128)}, f32[2,4,2,10,512]{4,3,2,1,0:T(8,128)S(1)}, u32[]{:S(2)}, u32[]{:S(2)}) collective-permute-start(f32[2,4,2,10,512]{4,3,2,1,0:T(8,128)} %get-tuple-element.43), channel_id=1, source_target_pairs={{252,0},{0,4},{4,8},{8,12},{12,16},{16,20},{20,24},{24,28},{28,32}... | collective-permute-start | bytes 983048 | tf_op jit(solution)/shard_map/edge_exchange_0/ppermute | solution.py:25
  3.6 34.8 %collective-permute-start = (f32[2,4,2,10,512]{4,3,2,1,0:T(8,128)}, f32[2,4,2,10,512]{4,3,2,1,0:T(8,128)S(1)}, u32[]{:S(2)}, u32[]{:S(2)}) collective-permute-start(f32[2,4,2,10,512]{4,3,2,1,0:T(8,128)} %get-tuple-element.41), channel_id=1, source_target_pairs={{4,0},{8,4},{12,8},{16,12},{20,16},{24,20},{28,24},{32,28},{36,32}... | collective-permute-start | bytes 983048 | tf_op jit(solution)/shard_map/edge_exchange_0/ppermute | solution.py:25
  36.8 1.2 %copy-start.4 = (f32[2,4,2,10,512]{4,3,2,1,0:T(8,128)S(1)}, f32[2,4,2,10,512]{4,3,2,1,0:T(8,128)}, u32[]{:S(2)}) copy-start(f32[2,4,2,10,512]{4,3,2,1,0:T(8,128)} %get-tuple-element.42) | copy-start | bytes 983044
  38.3 3.4 %copy-start.1 = (f32[2,4,2,10,512]{4,3,2,1,0:T(8,128)}, f32[2,4,2,10,512]{4,3,2,1,0:T(8,128)S(1)}, u32[]{:S(2)}) copy-start(f32[2,4,2,10,512]{4,3,2,1,0:T(8,128)S(1)} %get-tuple-element.55.refs_6_) | copy-start | bytes 983044
  40.2 1.2 %copy-start.3 = (f32[2,4,2,10,512]{4,3,2,1,0:T(8,128)S(1)}, f32[2,4,2,10,512]{4,3,2,1,0:T(8,128)}, u32[]{:S(2)}) copy-start(f32[2,4,2,10,512]{4,3,2,1,0:T(8,128)} %get-tuple-element.40) | copy-start | bytes 983044
  41.7 27.1 %copy-start.2 = (f32[2,4,2,10,512]{4,3,2,1,0:T(8,128)}, f32[2,4,2,10,512]{4,3,2,1,0:T(8,128)S(1)}, u32[]{:S(2)}) copy-start(f32[2,4,2,10,512]{4,3,2,1,0:T(8,128)S(1)} %get-tuple-element.53.refs_7_) | copy-start | bytes 983044
  41.7 23.5 %collective-permute-start.3 = (f32[2,4,2,10,512]{4,3,2,1,0:T(8,128)S(1)}, f32[2,4,2,10,512]{4,3,2,1,0:T(8,128)S(1)}, u32[]{:S(2)}, u32[]{:S(2)}) collective-permute-start(f32[2,4,2,10,512]{4,3,2,1,0:T(8,128)S(1)} %get-tuple-element.55.refs_6_), channel_id=1, source_target_pairs={{4,0},{8,4},{12,8},{16,12},{20,16},{24,20},{28,24},{32,28},{36,32}... | collective-permute-start | bytes 983048 | tf_op jit(solution)/shard_map/edge_exchange_1/ppermute | solution.py:25
  42.2 24.8 %collective-permute-start.1 = (f32[2,4,2,10,512]{4,3,2,1,0:T(8,128)S(1)}, f32[2,4,2,10,512]{4,3,2,1,0:T(8,128)S(1)}, u32[]{:S(2)}, u32[]{:S(2)}) collective-permute-start(f32[2,4,2,10,512]{4,3,2,1,0:T(8,128)S(1)} %get-tuple-element.53.refs_7_), channel_id=1, source_target_pairs={{252,0},{0,4},{4,8},{8,12},{12,16},{16,20},{20,24},{24,28},{28,32}... | collective-permute-start | bytes 983048 | tf_op jit(solution)/shard_map/edge_exchange_1/ppermute | solution.py:25
  65.2 3.6 %copy-start.5 = (f32[2,4,2,10,512]{4,3,2,1,0:T(8,128)}, f32[2,4,2,10,512]{4,3,2,1,0:T(8,128)S(1)}, u32[]{:S(2)}) copy-start(f32[2,4,2,10,512]{4,3,2,1,0:T(8,128)S(1)} %collective-permute-done.3.refs_3_) | copy-start | bytes 983044
  67.0 1.8 %copy-start.6 = (f32[2,4,2,10,512]{4,3,2,1,0:T(8,128)}, f32[2,4,2,10,512]{4,3,2,1,0:T(8,128)S(1)}, u32[]{:S(2)}) copy-start(f32[2,4,2,10,512]{4,3,2,1,0:T(8,128)S(1)} %collective-permute-done.1.refs_2_) | copy-start | bytes 983044
  76.3 9.6 %collective-permute-start.4 = (f32[2,8,512]{2,1,0:T(8,128)}, f32[2,8,512]{2,1,0:T(8,128)S(1)}, u32[]{:S(2)}, u32[]{:S(2)}) collective-permute-start(f32[2,8,512]{2,1,0:T(8,128)} %get-tuple-element.47), channel_id=1, source_target_pairs={{3,0},{0,1},{1,2},{2,3},{7,4},{4,5},{5,6},{6,7},{11,8},{8,9},{9,10... | collective-permute-start | bytes 98312 | tf_op jit(solution)/shard_map/mode_reduce/ppermute | solution.py:25
  83.9 5.0 %collective-permute-start.5 = (f32[2,8,512]{2,1,0:T(8,128)}, f32[2,8,512]{2,1,0:T(8,128)S(1)}, u32[]{:S(2)}, u32[]{:S(2)}) collective-permute-start(f32[2,8,512]{2,1,0:T(8,128)} %get-tuple-element.47), channel_id=1, source_target_pairs={{2,0},{3,1},{0,2},{1,3},{6,4},{7,5},{4,6},{5,7},{10,8},{11,9},{8,1... | collective-permute-start | bytes 98312 | tf_op jit(solution)/shard_map/mode_reduce/ppermute | solution.py:25
  83.9 5.0 %collective-permute-start.6 = (f32[2,8,512]{2,1,0:T(8,128)}, f32[2,8,512]{2,1,0:T(8,128)S(1)}, u32[]{:S(2)}, u32[]{:S(2)}) collective-permute-start(f32[2,8,512]{2,1,0:T(8,128)} %get-tuple-element.47), channel_id=1, source_target_pairs={{1,0},{2,1},{3,2},{0,3},{5,4},{6,5},{7,6},{4,7},{9,8},{10,9},{11,1... | collective-permute-start | bytes 98312 | tf_op jit(solution)/shard_map/mode_reduce/ppermute | solution.py:25

commit v7 on v6

--- a/solution.py
+++ b/solution.py
@@ -382,12 +382,11 @@
         )
     with jax.named_scope("mode_reduce"):
         count = lax.axis_size("mode")
-        me = lax.axis_index("mode")
-        stacked = jnp.stack([sens] + [shifted(sens, "mode", k) for k in range(1, count)])
-        total = None
-        for j in range(count):
-            part = lax.dynamic_index_in_dim(stacked, (me - j) % count, axis=0, keepdims=False)
-            total = part if total is None else total + part
+        copies = jnp.broadcast_to(sens[None], (count,) + sens.shape)
+        gathered = lax.all_to_all(copies, "mode", 0, 0)
+        total = gathered[0]
+        for j in range(1, count):
+            total = total + gathered[j]
         sensitivity = total / (STEPS * modes_total)
     return (q2, a2, sensitivity)
 

time: 92 us -> 97.5 us (1.060)
  blocking collectives: 0 us -> 8.41 us
  waiting for transfers between devices: 32.5 us -> 30.3 us
    all_to_all x0 -> x1, blocking collectives: none -> 8.41 us  [per_device(): gathered = lax.all_to_all(copies, 'mode', 0, 0)]
    ppermute x7 -> x4, waiting for transfers between devices: 32.5 us -> 30.3 us  [shifted(): return lax.ppermute(block, axis, route)]
    ppermute x7 -> x4, starting transfers between devices: 20.2 us -> 20.3 us  [shifted(): return lax.ppermute(block, axis, route)]
  transfers between devices with their start and end apart: 7 -> 4, of which waited for: 4 -> 3; matrix products, arithmetic and copies ran while one was open for 15% -> 12% of each run, Pallas kernels for 7% -> 7%
where the time goes in v7:
time: 97.5 us; the launch traced here: 96.7 us
  waiting for transfers between devices  30.3 us (31%)
  starting transfers between devices  20.3 us (21%)
  Pallas kernels  17 us (17%)
  local copies, waits for them, and re-layouts  8.57 us (9%)
  blocking collectives  8.41 us (9%)
  matrix products  5.67 us (6%)
  other arithmetic  5.42 us (6%)
  between operations  1.06 us (1%)
    ppermute x4, waiting for transfers between devices, shifted(): return lax.ppermute(block, axis, route)  30.3 us
    ppermute x4, starting transfers between devices, shifted(): return lax.ppermute(block, axis, route)  20.3 us
    pallas_call x2, Pallas kernels, run_step(): pl.pallas_call(kernel, grid_spec=grid_spec, out_shape=out_shape, compiler...  14.1 us
    all_to_all x1, blocking collectives, per_device(): gathered = lax.all_to_all(copies, 'mode', 0, 0)  8.41 us
    dot_general x4, matrix products, reverse_lanes(): jnp.dot(flat, turn, precision=lax.Precision.HIGHEST, preferred_element_ty...  5.67 us
    pallas_call x1, Pallas kernels, edge_rows(): return pl.pallas_call(edge_kernel, out_shape=[edge_shape, edge_shape])(x, a)  2.88 us
    scatter-add x2, local copies, waits for them, and re-layouts, per_device(): sens = sens.at[:, 0, :].add(s0).at[:, height - 1, :].add(s7)  2.78 us
  transfers between devices with their start and end apart: 4, of which 3 were waited for; matrix products, arithmetic and copies ran while one was open for 12% of the time, Pallas kernels for 7%

profile of v7, /device:TPU:32, one launch (start us, length us, event | category | flops | bytes accessed | tf_op | source)
XLA Modules:
  0.0 96.7 jit_solution(16589338546264715557)
XLA Ops:
  0.7 2.9 %edge_exchange_0.1 = (f32[2,4,2,10,512]{4,3,2,1,0:T(8,128)}, f32[2,4,2,10,512]{4,3,2,1,0:T(8,128)}) custom-call(f32[4,2,5,2,8,512]{5,4,3,2,1,0:T(8,128)} %x_ref.1, f32[4,2,5,2,8,512]{5,4,3,2,1,0:T(8,128)} %a_ref.1), custom_call_target="tpu_custom_call" | custom-call | tf_op jit(solution)/shard_map/edge_exchange_0/pallas_call | solution.py:346
  3.6 10.4 %collective-permute-start = (f32[2,4,2,10,512]{4,3,2,1,0:T(8,128)}, f32[2,4,2,10,512]{4,3,2,1,0:T(8,128)S(1)}, u32[]{:S(2)}, u32[]{:S(2)}) collective-permute-start(f32[2,4,2,10,512]{4,3,2,1,0:T(8,128)} %get-tuple-element.41), channel_id=1, source_target_pairs={{4,0},{8,4},{12,8},{16,12},{20,16},{24,20},{28,24},{32,28},{36,32}... | collective-permute-start | bytes 983048 | tf_op jit(solution)/shard_map/edge_exchange_0/ppermute | solution.py:25
  14.0 0.2 compare_reduce_fusion
  14.2 0.1 reshape.2396
  14.3 0.6 gather_fusion
  15.0 0.1 reshape.2395
  15.1 0.2 slice_reduce_fusion.1
  15.3 0.8 fusion.47
  16.2 0.1 stack.145
  16.3 0.1 reshape.2375
  16.4 0.8 slice_multiply_fusion.2
  17.3 0.6 pad_add_fusion.tbl
  17.9 6.6 %flow_step_0.1 = (f32[4,2,5,2,8,512]{5,4,3,2,1,0:T(8,128)}, f32[4,2,5,2,8,512]{5,4,3,2,1,0:T(8,128)}, f32[2,8,512]{2,1,0:T(8,128)}, f32[2,4,2,10,512]{4,3,2,1,0:T(8,128)}, f32[2,4,2,10,512]{4,3,2,1,0:T(8,128)}) custom-call(s32[17]{0:T(128)} %pad_add_fusion.tbl, f32[4,2,5,2,8,512]{5,4,3,2,1,0:T(8,128)} %x_ref.1, f32[4,2,5,2,8,512]{5,4,3,2,1,0:T(8,128)} %a_ref.1, ...), custom_call_target="tpu_custom_call" | custom-call | tf_op jit(solution)/shard_map/flow_step_0/pallas_call | solution.py:270
  24.5 8.6 %collective-permute-done = f32[2,4,2,10,512]{4,3,2,1,0:T(8,128)S(1)} collective-permute-done((f32[2,4,2,10,512]{4,3,2,1,0:T(8,128)}, f32[2,4,2,10,512]{4,3,2,1,0:T(8,128)S(1)}, u32[]{:S(2)}, u32[]{:S(2)}) %collective-permute-start) | collective-permute-done | bytes 327712 | tf_op jit(solution)/shard_map/edge_exchange_0/ppermute | solution.py:25
  33.1 0.6 gather_fusion.1
  33.7 1.1 %convolution_select_fusion.1 = f32[2,4,2,10,512]{4,3,1,0,2:T(8,128)S(1)} fusion(f32[2,2,4,10,512]{4,3,2,1,0:T(8,128)S(1)} %gather_fusion.1, pred[2]{0:T(512)(128)(4,1)S(1)} %compare_and_fusion.1, pred[2]{0:T(512)(128)(4,1)S(1)} %get-tuple-element.49), kind=kOutput, calls=%fused_computation.6 | convolution fusion | flops 504348672 | bytes 655364 | tf_op jit(solution)/shard_map/edge_fix_0/dot_general | solution.py:327
  34.9 0.1 copy.116
  35.0 0.1 copy.127
  35.2 3.3 %collective-permute-done.2 = f32[2,4,2,10,512]{4,3,2,1,0:T(8,128)S(1)} collective-permute-done((f32[2,4,2,10,512]{4,3,2,1,0:T(8,128)}, f32[2,4,2,10,512]{4,3,2,1,0:T(8,128)S(1)}, u32[]{:S(2)}, u32[]{:S(2)}) %collective-permute-start.2) | collective-permute-done | bytes 327712 | tf_op jit(solution)/shard_map/edge_exchange_0/ppermute | solution.py:25
  38.5 0.6 gather_fusion.2
  39.1 1.1 %convolution_select_fusion = f32[2,4,2,10,512]{4,3,1,0,2:T(8,128)S(1)} fusion(f32[2,2,4,10,512]{4,3,2,1,0:T(8,128)S(1)} %gather_fusion.2, pred[2]{0:T(512)(128)(4,1)S(1)} %compare_and_fusion, pred[2]{0:T(512)(128)(4,1)S(1)} %get-tuple-element.48), kind=kOutput, calls=%fused_computation.5 | convolution fusion | flops 504348672 | bytes 655364 | tf_op jit(solution)/shard_map/edge_fix_0/dot_general | solution.py:327
  40.2 0.1 copy.140
  40.4 0.1 copy.152
  40.5 0.1 add_bitcast_fusion.12
  40.6 0.4 add_bitcast_fusion.11
  41.0 0.3 stack.179
  41.3 0.3 stack.190
  41.6 0.1 multiply_add_fusion.1
  41.7 0.2 multiply_reduce_fusion.1
  41.9 0.1 add_bitcast_fusion.32
  42.0 0.4 add_bitcast_fusion.31
  42.4 0.3 stack.156
  42.7 0.3 stack.167
  42.9 0.1 multiply_add_fusion.3
  43.0 0.2 multiply_reduce_fusion
  43.2 0.1 collective-permute-start.1
  43.3 9.9 %collective-permute-start.3 = (f32[2,4,2,10,512]{4,3,2,1,0:T(8,128)S(1)}, f32[2,4,2,10,512]{4,3,2,1,0:T(8,128)S(1)}, u32[]{:S(2)}, u32[]{:S(2)}) collective-permute-start(f32[2,4,2,10,512]{4,3,2,1,0:T(8,128)S(1)} %get-tuple-element.55.refs_6_), channel_id=1, source_target_pairs={{4,0},{8,4},{12,8},{16,12},{20,16},{24,20},{28,24},{32,28},{36,32}... | collective-permute-start | bytes 983048 | tf_op jit(solution)/shard_map/edge_exchange_1/ppermute | solution.py:25
  53.2 0.8 reshape_add_fusion
  53.9 1.4 %scatter-add.6 = f32[2,8,512]{2,1,0:T(8,128)} dynamic-update-slice(f32[2,8,512]{2,1,0:T(8,128)} %get-tuple-element.44, f32[2,1,512]{2,1,0:T(1,128)S(1)} %reshape_add_fusion, s32[]{:T(128)} %constant.109.clone.1, s32[]{:T(128)} %constant.109.clone.1, s32[]{:T(128)} %constant.109.clone.1) | dynamic-update-slice | bytes 8196 | tf_op jit(solution)/shard_map/edge_fix_0/scatter-add | solution.py:375
  55.4 0.8 slice_add_fusion.3
  56.1 1.4 %scatter-add.9.refs_11_ = f32[2,8,512]{2,1,0:T(8,128)} dynamic-update-slice(f32[2,8,512]{2,1,0:T(8,128)} %scatter-add.6, f32[2,1,512]{2,1,0:T(1,128)S(1)} %slice_add_fusion.3, s32[]{:T(128)} %constant.109.clone.1, s32[]{:T(128)} %constant.125.clone.1, s32[]{:T(128)} %constant.109.clone.1) | dynamic-update-slice | bytes 8196 | tf_op jit(solution)/shard_map/edge_fix_0/scatter-add | solution.py:375
  57.5 18.3 %collective-permute-done.1.refs_2_ = f32[2,4,2,10,512]{4,3,2,1,0:T(8,128)S(1)} collective-permute-done((f32[2,4,2,10,512]{4,3,2,1,0:T(8,128)S(1)}, f32[2,4,2,10,512]{4,3,2,1,0:T(8,128)S(1)}, u32[]{:S(2)}, u32[]{:S(2)}) %collective-permute-start.1) | collective-permute-done | bytes 327712 | tf_op jit(solution)/shard_map/edge_exchange_1/ppermute | solution.py:25
  75.8 1.8 %fusion.1.refs_4_ = f32[2,4,2,10,512]{4,3,2,1,0:T(8,128)} fusion(f32[2,4,2,10,512]{4,3,2,1,0:T(8,128)S(1)} %collective-permute-done.1.refs_2_), kind=kOutput, calls=%fused_computation.8 | convolution fusion | flops 504102912 | bytes 655360 | tf_op jit(solution)/shard_map/flow_step_1/dot_general | solution.py:327
  77.6 1.8 %fusion.refs_5_ = f32[2,4,2,10,512]{4,3,2,1,0:T(8,128)} fusion(f32[2,4,2,10,512]{4,3,2,1,0:T(8,128)S(1)} %collective-permute-done.3.refs_3_), kind=kOutput, calls=%fused_computation.7 | convolution fusion | flops 504102912 | bytes 655360 | tf_op jit(solution)/shard_map/flow_step_1/dot_general | solution.py:327
  79.4 7.5 %flow_step_1.1 = (f32[4,2,5,2,8,512]{5,4,3,2,1,0:T(8,128)}, f32[4,2,5,2,8,512]{5,4,3,2,1,0:T(8,128)}, f32[2,8,512]{2,1,0:T(8,128)}) custom-call(s32[17]{0:T(128)} %pad_add_fusion.tbl, f32[4,2,5,2,8,512]{5,4,3,2,1,0:T(8,128)} %get-tuple-element.38.refs_0_, f32[4,2,5,2,8,512]{5,4,3,2,1,0:T(8,128)} %get-tuple-element.39.refs_1_, ...), custom_call_target="tpu_custom_call" | custom-call | tf_op jit(solution)/shard_map/flow_step_1/pallas_call | solution.py:270
  86.9 0.8 broadcast_in_dim.73
  87.6 8.4 %all_to_all.5 = f32[4,2,8,512]{3,2,1,0:T(8,128)S(1)} all-to-all(f32[4,2,8,512]{3,2,1,0:T(8,128)S(1)} %broadcast_in_dim.73), channel_id=1, replica_groups=mesh['blk'=64,'mode'=4] {'mode'}, dimensions={0} | all-to-all | bytes 262144 | tf_op jit(solution)/shard_map/mode_reduce/all_to_all | solution.py:386
  96.0 0.6 fusion.23
  (49 shorter events, 0.5 us)
Async XLA Ops:
  0.6 13.7 %copy-start = (s32[128]{0:T(128)S(1)}, s32[128]{0:T(128)}, u32[]{:S(2)}) copy-start(s32[128]{0:T(128)} %param.19) | copy-start | bytes 1540
  0.6 13.3 %copy-start.9 = (s32[2,4]{1,0:T(2,128)S(1)}, s32[2,4]{1,0:T(2,128)}, u32[]{:S(2)}) copy-start(s32[2,4]{1,0:T(2,128)} %param.20) | copy-start | bytes 100
  0.7 13.3 %copy-start.8 = (s32[2,4]{1,0:T(2,128)S(1)}, s32[2,4]{1,0:T(2,128)}, u32[]{:S(2)}) copy-start(s32[2,4]{1,0:T(2,128)} %param.21) | copy-start | bytes 100
  0.7 16.6 %copy-start.7 = (f32[2,2,8,512]{3,2,1,0:T(8,128)S(1)}, f32[2,2,8,512]{3,2,1,0:T(8,128)}, u32[]{:S(2)}) copy-start(f32[2,2,8,512]{3,2,1,0:T(8,128)} %refs_9_.1) | copy-start | bytes 196612
  3.6 29.6 %collective-permute-start = (f32[2,4,2,10,512]{4,3,2,1,0:T(8,128)}, f32[2,4,2,10,512]{4,3,2,1,0:T(8,128)S(1)}, u32[]{:S(2)}, u32[]{:S(2)}) collective-permute-start(f32[2,4,2,10,512]{4,3,2,1,0:T(8,128)} %get-tuple-element.41), channel_id=1, source_target_pairs={{4,0},{8,4},{12,8},{16,12},{20,16},{24,20},{28,24},{32,28},{36,32}... | collective-permute-start | bytes 983048 | tf_op jit(solution)/shard_map/edge_exchange_0/ppermute | solution.py:25
  13.9 24.6 %collective-permute-start.2 = (f32[2,4,2,10,512]{4,3,2,1,0:T(8,128)}, f32[2,4,2,10,512]{4,3,2,1,0:T(8,128)S(1)}, u32[]{:S(2)}, u32[]{:S(2)}) collective-permute-start(f32[2,4,2,10,512]{4,3,2,1,0:T(8,128)} %get-tuple-element.43), channel_id=1, source_target_pairs={{252,0},{0,4},{4,8},{8,12},{12,16},{16,20},{20,24},{24,28},{28,32}... | collective-permute-start | bytes 983048 | tf_op jit(solution)/shard_map/edge_exchange_0/ppermute | solution.py:25
  40.3 1.2 %copy-start.4 = (f32[2,4,2,10,512]{4,3,2,1,0:T(8,128)S(1)}, f32[2,4,2,10,512]{4,3,2,1,0:T(8,128)}, u32[]{:S(2)}) copy-start(f32[2,4,2,10,512]{4,3,2,1,0:T(8,128)} %get-tuple-element.42) | copy-start | bytes 983044
  41.7 1.3 %copy-start.3 = (f32[2,4,2,10,512]{4,3,2,1,0:T(8,128)S(1)}, f32[2,4,2,10,512]{4,3,2,1,0:T(8,128)}, u32[]{:S(2)}) copy-start(f32[2,4,2,10,512]{4,3,2,1,0:T(8,128)} %get-tuple-element.40) | copy-start | bytes 983044
  41.8 1.5 %copy-start.1 = (f32[2,4,2,10,512]{4,3,2,1,0:T(8,128)}, f32[2,4,2,10,512]{4,3,2,1,0:T(8,128)S(1)}, u32[]{:S(2)}) copy-start(f32[2,4,2,10,512]{4,3,2,1,0:T(8,128)S(1)} %get-tuple-element.55.refs_6_) | copy-start | bytes 983044
  43.2 36.2 %copy-start.2 = (f32[2,4,2,10,512]{4,3,2,1,0:T(8,128)}, f32[2,4,2,10,512]{4,3,2,1,0:T(8,128)S(1)}, u32[]{:S(2)}) copy-start(f32[2,4,2,10,512]{4,3,2,1,0:T(8,128)S(1)} %get-tuple-element.53.refs_7_) | copy-start | bytes 983044
  43.2 32.6 %collective-permute-start.1 = (f32[2,4,2,10,512]{4,3,2,1,0:T(8,128)S(1)}, f32[2,4,2,10,512]{4,3,2,1,0:T(8,128)S(1)}, u32[]{:S(2)}, u32[]{:S(2)}) collective-permute-start(f32[2,4,2,10,512]{4,3,2,1,0:T(8,128)S(1)} %get-tuple-element.53.refs_7_), channel_id=1, source_target_pairs={{252,0},{0,4},{4,8},{8,12},{12,16},{16,20},{20,24},{24,28},{28,32}... | collective-permute-start | bytes 983048 | tf_op jit(solution)/shard_map/edge_exchange_1/ppermute | solution.py:25
  43.3 34.3 %collective-permute-start.3 = (f32[2,4,2,10,512]{4,3,2,1,0:T(8,128)S(1)}, f32[2,4,2,10,512]{4,3,2,1,0:T(8,128)S(1)}, u32[]{:S(2)}, u32[]{:S(2)}) collective-permute-start(f32[2,4,2,10,512]{4,3,2,1,0:T(8,128)S(1)} %get-tuple-element.55.refs_6_), channel_id=1, source_target_pairs={{4,0},{8,4},{12,8},{16,12},{20,16},{24,20},{28,24},{32,28},{36,32}... | collective-permute-start | bytes 983048 | tf_op jit(solution)/shard_map/edge_exchange_1/ppermute | solution.py:25
  75.8 3.6 %copy-start.5 = (f32[2,4,2,10,512]{4,3,2,1,0:T(8,128)}, f32[2,4,2,10,512]{4,3,2,1,0:T(8,128)S(1)}, u32[]{:S(2)}) copy-start(f32[2,4,2,10,512]{4,3,2,1,0:T(8,128)S(1)} %collective-permute-done.1.refs_2_) | copy-start | bytes 983044
  77.6 1.8 %copy-start.6 = (f32[2,4,2,10,512]{4,3,2,1,0:T(8,128)}, f32[2,4,2,10,512]{4,3,2,1,0:T(8,128)S(1)}, u32[]{:S(2)}) copy-start(f32[2,4,2,10,512]{4,3,2,1,0:T(8,128)S(1)} %collective-permute-done.3.refs_3_) | copy-start | bytes 983044

commit v8 on v6

--- a/solution.py
+++ b/solution.py
@@ -98,6 +98,15 @@
 
 
 LANES = 128
+
+
+def pick_rows(ref, arr, slot, slots):
+    rows = NV * 2
+    out = ref[0, pl.ds(arr * slots * rows, rows), :]
+    for other in range(1, slots):
+        cand = ref[0, pl.ds((arr * slots + other) * rows, rows), :]
+        out = jnp.where((jnp.zeros(out.shape, jnp.int32) + slot) == other, cand, out)
+    return out
 
 
 def step_kernel(tbl, *refs, modes_total, first, ghosts, patched):
@@ -139,8 +148,8 @@
             for arr in range(2):
                 if ghosts:
                     recv_ref, turn_ref = ((rlo_ref, tlo_ref), (rhi_ref, thi_ref))[side]
-                    plain = recv_ref[arr, 0, t]
-                    turned = turn_ref[arr, 0, t]
+                    plain = pick_rows(recv_ref, arr, t, slots)
+                    turned = pick_rows(turn_ref, arr, t, slots)
                     flag = (jnp.zeros(plain.shape, jnp.int32) + f) != 0
                     gh_ref[arr, side, s] = jnp.where(flag, turned, plain)
                 else:
@@ -155,11 +164,20 @@
     last_row = row == height - 1
     first_lane = lane == 0
     last_lane = lane == LANES - 1
+    def edge_row(ref, arr, slot, k, cols):
+        if isinstance(slot, int):
+            return ref[0, pl.ds((arr * slots + slot) * 2 * NV + k, 1), cols]
+        out = ref[0, pl.ds(arr * slots * 2 * NV + k, 1), cols]
+        for other in range(1, slots):
+            cand = ref[0, pl.ds((arr * slots + other) * 2 * NV + k, 1), cols]
+            out = jnp.where((jnp.zeros(out.shape, jnp.int32) + slot) == other, cand, out)
+        return out
+
     def load(src, arr, p, n, slot, k, cols):
         g = src[0, p, n, slot, :, cols]
         if patched:
-            top = jnp.broadcast_to(c0_ref[arr, 0, slot, pl.ds(k, 1), cols], shape)
-            bottom = jnp.broadcast_to(c7_ref[arr, 0, slot, pl.ds(k, 1), cols], shape)
+            top = jnp.broadcast_to(edge_row(c0_ref, arr, slot, k, cols), shape)
+            bottom = jnp.broadcast_to(edge_row(c7_ref, arr, slot, k, cols), shape)
             g = jnp.where(first_row, top, jnp.where(last_row, bottom, g))
         return g
 
@@ -213,8 +231,9 @@
                         nv = vals[k] + TIME_STEP * rate[n]
                         dst[0, p, n, s, :, cs] = nv
                         if first:
-                            elo_ref[arr, 0, s, pl.ds(k, 1), cs] = nv[0:1, :]
-                            ehi_ref[arr, 0, s, pl.ds(k, 1), cs] = nv[height - 1:height, :]
+                            at = (arr * slots + s) * 2 * NV + k
+                            elo_ref[0, pl.ds(at, 1), cs] = nv[0:1, :]
+                            ehi_ref[0, pl.ds(at, 1), cs] = nv[height - 1:height, :]
                         sq = nv * nv
                         total = sq if total is None else total + sq
                 means.append(total / 10.0)
@@ -227,9 +246,9 @@
 def run_step(tbl, x, a, rlo, rhi, patch, density, velocity, pressure, sens_in, modes_total, first):
     modes, parts, nv, slots, height, width = x.shape
     state_block = (1, parts, nv, slots, height, width)
-    edge_block = (2, 1, slots, parts * nv, width)
+    edge_block = (1, 2 * slots * parts * nv, width)
     state_spec = pl.BlockSpec(state_block, lambda m, t: (m, 0, 0, 0, 0, 0))
-    edge_spec = pl.BlockSpec(edge_block, lambda m, t: (0, m, 0, 0, 0))
+    edge_spec = pl.BlockSpec(edge_block, lambda m, t: (m, 0, 0))
     flow_spec = pl.BlockSpec((slots, height, width), lambda m, t: (0, 0, 0))
     vel_spec = pl.BlockSpec((2, slots, height, width), lambda m, t: (0, 0, 0, 0))
     ghosts = rlo is not None
@@ -254,7 +273,7 @@
     ]
     out_specs = [state_spec, state_spec, flow_spec]
     if first:
-        edge_shape = jax.ShapeDtypeStruct((2, modes, slots, parts * nv, width), jnp.float32)
+        edge_shape = jax.ShapeDtypeStruct((modes, 2 * slots * parts * nv, width), jnp.float32)
         out_shape += [edge_shape, edge_shape]
         out_specs += [edge_spec, edge_spec]
     grid_spec = pltpu.PrefetchScalarGridSpec(
@@ -281,7 +300,19 @@
     return [u * f[0] + r * f[1], u * f[1] + f[4] * ir, u * f[2], u * f[3], kp * f[1] + u * f[4]]
 
 
+def unflat(e, slots):
+    modes, _, width = e.shape
+    return jnp.transpose(e.reshape(modes, 2, slots, 2 * NV, width), (1, 0, 2, 3, 4))
+
+
+def flat(e):
+    _, modes, slots, rows, width = e.shape
+    return jnp.transpose(e, (1, 0, 2, 3, 4)).reshape(modes, 2 * slots * rows, width)
+
+
 def fix_rows(partial0, partial7, rlo, rhi, slot_of, face_flip, density, velocity, pressure):
+    slots = density.shape[0]
+    partial0, partial7, rlo, rhi = (unflat(e, slots) for e in (partial0, partial7, rlo, rhi))
     _, modes, slots, rows, width = partial0.shape
     height = density.shape[1]
 
@@ -315,7 +346,7 @@
         fixed[row] = jnp.stack(out)
         means = jnp.sum(fixed[row] * fixed[row], axis=3) / 10.0
         sens_rows[row] = jnp.sum(means[0] * means[1], axis=0)
-    return fixed[0], fixed[height - 1], sens_rows[0], sens_rows[height - 1]
+    return flat(fixed[0]), flat(fixed[height - 1]), sens_rows[0], sens_rows[height - 1]
 
 
 def reverse_lanes(rows):
@@ -336,13 +367,14 @@
                 for n in range(nv):
                     k = p * nv + n
                     for s in range(slots):
-                        lo_ref[arr, m, s, pl.ds(k, 1), :] = src[m, p, n, s, 0:1, :]
-                        hi_ref[arr, m, s, pl.ds(k, 1), :] = src[m, p, n, s, height - 1:height, :]
+                        at = (arr * slots + s) * parts * nv + k
+                        lo_ref[m, pl.ds(at, 1), :] = src[m, p, n, s, 0:1, :]
+                        hi_ref[m, pl.ds(at, 1), :] = src[m, p, n, s, height - 1:height, :]
 
 
 def edge_rows(x, a):
     modes, parts, nv, slots, height, width = x.shape
-    edge_shape = jax.ShapeDtypeStruct((2, modes, slots, parts * nv, width), jnp.float32)
+    edge_shape = jax.ShapeDtypeStruct((modes, 2 * slots * parts * nv, width), jnp.float32)
     return pl.pallas_call(edge_kernel, out_shape=[edge_shape, edge_shape])(x, a)
 
 

time: 92 us -> 76.3 us (0.83)
  waiting for transfers between devices: 32.5 us -> 14 us
  local copies, waits for them, and re-layouts: 7.79 us -> 10.1 us
  starting transfers between devices: 20.2 us -> 22.2 us
    ppermute x7, waiting for transfers between devices: 32.5 us -> 14 us  [shifted(): return lax.ppermute(block, axis, route)]
    pallas_call x0 -> x2, local copies, waits for them, and re-layouts: none -> 2.38 us  [run_step(): pl.pallas_call(kernel, grid_spec=grid_spec, out_shape=out_shape, compiler...]
    ppermute x7, starting transfers between devices: 20.2 us -> 22.2 us  [shifted(): return lax.ppermute(block, axis, route)]
    another operation x4 -> x0, local copies, waits for them, and re-layouts: 1.02 us -> none  [fix_rows(): delta = jnp.stack(res, axis=2)]
  transfers between devices with their start and end apart: 7 -> 7, of which waited for: 4 -> 4; matrix products, arithmetic and copies ran while one was open for 15% -> 20% of each run, Pallas kernels for 7% -> 9%
where the time goes in v8:
time: 76.3 us; the launch traced here: 75.3 us
  starting transfers between devices  22.2 us (29%)
  Pallas kernels  16.9 us (22%)
  waiting for transfers between devices  14 us (18%)
  local copies, waits for them, and re-layouts  10.1 us (13%)
  other arithmetic  5.96 us (8%)
  matrix products  5.02 us (7%)
  between operations  1.17 us (2%)
    ppermute x7, starting transfers between devices, shifted(): return lax.ppermute(block, axis, route)  22.2 us
    pallas_call x2, Pallas kernels, run_step(): pl.pallas_call(kernel, grid_spec=grid_spec, out_shape=out_shape, compiler...  14.1 us
    ppermute x7, waiting for transfers between devices, shifted(): return lax.ppermute(block, axis, route)  14 us
    dot_general x4, matrix products, reverse_lanes(): jnp.dot(flat, turn, precision=lax.Precision.HIGHEST, preferred_element_ty...  5.02 us
    scatter-add x2, local copies, waits for them, and re-layouts, per_device(): sens = sens.at[:, 0, :].add(s0).at[:, height - 1, :].add(s7)  2.78 us
    pallas_call x1, Pallas kernels, edge_rows(): return pl.pallas_call(edge_kernel, out_shape=[edge_shape, edge_shape])(x, a)  2.77 us
    pallas_call x2, local copies, waits for them, and re-layouts, run_step(): pl.pallas_call(kernel, grid_spec=grid_spec, out_shape=out_shape, compiler...  2.38 us
    add x2, other arithmetic, per_device(): sens = sens.at[:, 0, :].add(s0).at[:, height - 1, :].add(s7)  1.53 us
  transfers between devices with their start and end apart: 7, of which 4 were waited for; matrix products, arithmetic and copies ran while one was open for 20% of the time, Pallas kernels for 9%

profile of v8, /device:TPU:32, one launch (start us, length us, event | category | flops | bytes accessed | tf_op | source)
XLA Modules:
  0.0 75.3 jit_solution(8143557939777129860)
XLA Ops:
  0.7 2.8 %edge_exchange_0.1 = (f32[4,40,512]{2,1,0:T(8,128)}, f32[4,40,512]{2,1,0:T(8,128)}) custom-call(f32[4,2,5,2,8,512]{5,4,3,2,1,0:T(8,128)} %x_ref.1, f32[4,2,5,2,8,512]{5,4,3,2,1,0:T(8,128)} %a_ref.1), custom_call_target="tpu_custom_call" | custom-call | tf_op jit(solution)/shard_map/edge_exchange_0/pallas_call | solution.py:378
  3.4 10.4 %collective-permute-start = (f32[4,40,512]{2,1,0:T(8,128)}, f32[4,40,512]{2,1,0:T(8,128)S(1)}, u32[]{:S(2)}, u32[]{:S(2)}) collective-permute-start(f32[4,40,512]{2,1,0:T(8,128)} %get-tuple-element.41), channel_id=1, source_target_pairs={{4,0},{8,4},{12,8},{16,12},{20,16},{24,20},{28,24},{32,28},{36,32}... | collective-permute-start | bytes 983048 | tf_op jit(solution)/shard_map/edge_exchange_0/ppermute | solution.py:25
  13.8 0.8 %fusion.43 = (f32[2,1,512]{2,1,0:T(1,128)S(1)}, f32[2,1,512]{2,1,0:T(1,128)S(1)}) fusion(f32[2,8,512]{2,1,0:T(8,128)} %refs_8_.1), kind=kLoop, calls=%fused_computation.181 | loop fusion | bytes 16384 | tf_op jit(solution)/shard_map/edge_fix_0/slice | solution.py:330
  14.8 0.6 gather_fusion
  15.5 0.1 reshape.2418
  15.6 0.2 slice_reduce_fusion.1
  15.8 0.2 compare_reduce_fusion
  16.0 0.8 %slice_multiply_fusion.2 = (f32[2,1,512]{2,1,0:T(1,128)S(1)}, f32[2,1,512]{2,1,0:T(1,128)S(1)}) fusion(f32[2,8,512]{2,1,0:T(8,128)} %refs_10_.1), kind=kLoop, calls=%fused_computation.141 | loop fusion | flops 2048 | bytes 16384 | tf_op jit(solution)/shard_map/edge_fix_0/mul | solution.py:333
  17.0 0.1 stack.160
  17.1 0.1 reshape.2392
  17.1 0.6 pad_add_fusion.tbl
  17.7 6.5 %flow_step_0.1 = (f32[4,2,5,2,8,512]{5,4,3,2,1,0:T(8,128)}, f32[4,2,5,2,8,512]{5,4,3,2,1,0:T(8,128)}, f32[2,8,512]{2,1,0:T(8,128)}, f32[4,40,512]{2,1,0:T(8,128)}, f32[4,40,512]{2,1,0:T(8,128)}) custom-call(s32[17]{0:T(128)} %pad_add_fusion.tbl, f32[4,2,5,2,8,512]{5,4,3,2,1,0:T(8,128)} %x_ref.1, f32[4,2,5,2,8,512]{5,4,3,2,1,0:T(8,128)} %a_ref.1, ...), custom_call_target="tpu_custom_call" | custom-call | tf_op jit(solution)/shard_map/flow_step_0/pallas_call | solution.py:289
  24.2 1.2 %copy.164 = f32[4,40,512]{2,0,1:T(4,128)S(1)} copy(f32[4,40,512]{2,1,0:T(8,128)} %get-tuple-element.42) | data formatting | bytes 655360 | tf_op jit(solution)/shard_map/flow_step_0/pallas_call | solution.py:289
  25.4 1.2 %copy.135 = f32[4,40,512]{2,0,1:T(4,128)S(1)} copy(f32[4,40,512]{2,1,0:T(8,128)} %get-tuple-element.40) | data formatting | bytes 655360 | tf_op jit(solution)/shard_map/flow_step_0/pallas_call | solution.py:289
  26.7 0.2 copy.165
  26.9 0.7 gather_fusion.2
  27.7 1.1 %convolution_select_fusion = f32[2,4,2,10,512]{4,3,2,1,0:T(8,128)S(1)} fusion(f32[2,2,4,10,512]{4,2,3,1,0:T(4,128)S(1)} %gather_fusion.2, pred[2]{0:T(512)(128)(4,1)S(1)} %get-tuple-element.122, pred[2]{0:T(512)(128)(4,1)S(1)} %get-tuple-element.48), kind=kOutput, calls=%fused_computation.5 | convolution fusion | flops 504348672 | bytes 655364 | tf_op jit(solution)/shard_map/edge_fix_0/dot_general | solution.py:358
  28.8 0.1 copy.188
  29.2 0.1 copy.167
  29.6 0.1 slice_add_fusion.1
  29.7 0.1 multiply_reduce_fusion.1
  29.9 0.2 copy.136
  30.1 0.7 gather_fusion.1
  30.9 1.1 %convolution_select_fusion.1 = f32[2,4,2,10,512]{4,3,2,1,0:T(8,128)S(1)} fusion(f32[2,2,4,10,512]{4,2,3,1,0:T(4,128)S(1)} %gather_fusion.1, pred[2]{0:T(512)(128)(4,1)S(1)} %get-tuple-element.123, pred[2]{0:T(512)(128)(4,1)S(1)} %get-tuple-element.49), kind=kOutput, calls=%fused_computation.6 | convolution fusion | flops 504348672 | bytes 655364 | tf_op jit(solution)/shard_map/edge_fix_0/dot_general | solution.py:358
  32.0 0.1 copy.138
  32.2 0.1 copy.150
  32.8 0.1 slice_add_fusion.3
  33.0 0.1 multiply_reduce_fusion
  33.1 0.1 copy.200.refs_6_
  33.2 2.3 %collective-permute-start.3 = (f32[4,40,512]{2,1,0:T(8,128)S(1)}, f32[4,40,512]{2,1,0:T(8,128)S(1)}, u32[]{:S(2)}, u32[]{:S(2)}) collective-permute-start(f32[4,40,512]{2,1,0:T(8,128)S(1)} %copy.200.refs_6_), channel_id=1, source_target_pairs={{4,0},{8,4},{12,8},{16,12},{20,16},{24,20},{28,24},{32,28},{36,32}... | collective-permute-start | bytes 983048 | tf_op jit(solution)/shard_map/edge_exchange_1/ppermute | solution.py:25
  35.5 0.1 copy.163.refs_7_
  35.6 0.3 collective-permute-start.1
  35.9 0.8 %reshape_add_fusion = f32[2,1,512]{2,1,0:T(1,128)S(1)} fusion(f32[2,512]{1,0:T(2,128)S(1)} %fusion.21, f32[2,8,512]{2,1,0:T(8,128)} %get-tuple-element.44), kind=kLoop, calls=%fused_computation.140 | loop fusion | flops 1024 | bytes 12288 | tf_op jit(solution)/shard_map/edge_fix_0/add | solution.py:407
  36.7 1.4 %scatter-add.6 = f32[2,8,512]{2,1,0:T(8,128)} dynamic-update-slice(f32[2,8,512]{2,1,0:T(8,128)} %get-tuple-element.44, f32[2,1,512]{2,1,0:T(1,128)S(1)} %reshape_add_fusion, s32[]{:T(128)} %constant.145.clone.1, s32[]{:T(128)} %constant.145.clone.1, s32[]{:T(128)} %constant.145.clone.1) | dynamic-update-slice | bytes 8196 | tf_op jit(solution)/shard_map/edge_fix_0/scatter-add | solution.py:407
  38.1 0.8 %slice_add_fusion.4 = f32[2,1,512]{2,1,0:T(1,128)S(1)} fusion(f32[2,8,512]{2,1,0:T(8,128)} %scatter-add.6, f32[2,512]{1,0:T(2,128)S(1)} %fusion.20), kind=kLoop, calls=%fused_computation.130 | loop fusion | flops 1024 | bytes 12288 | tf_op jit(solution)/shard_map/edge_fix_0/add | solution.py:407
  38.8 1.4 %scatter-add.9.refs_11_ = f32[2,8,512]{2,1,0:T(8,128)} dynamic-update-slice(f32[2,8,512]{2,1,0:T(8,128)} %scatter-add.6, f32[2,1,512]{2,1,0:T(1,128)S(1)} %slice_add_fusion.4, s32[]{:T(128)} %constant.145.clone.1, s32[]{:T(128)} %constant.161.clone.1, s32[]{:T(128)} %constant.145.clone.1) | dynamic-update-slice | bytes 8196 | tf_op jit(solution)/shard_map/edge_fix_0/scatter-add | solution.py:407
  40.2 8.3 %collective-permute-done.3.refs_3_ = f32[4,40,512]{2,1,0:T(8,128)S(1)} collective-permute-done((f32[4,40,512]{2,1,0:T(8,128)S(1)}, f32[4,40,512]{2,1,0:T(8,128)S(1)}, u32[]{:S(2)}, u32[]{:S(2)}) %collective-permute-start.3) | collective-permute-done | bytes 327712 | tf_op jit(solution)/shard_map/edge_exchange_1/ppermute | solution.py:25
  48.6 1.4 %fusion.refs_5_ = f32[4,40,512]{2,1,0:T(8,128)} fusion(f32[4,40,512]{2,1,0:T(8,128)S(1)} %collective-permute-done.3.refs_3_), kind=kOutput, calls=%fused_computation.7 | convolution fusion | flops 504102912 | bytes 655360 | tf_op jit(solution)/shard_map/flow_step_1/dot_general | solution.py:358
  50.0 3.4 %collective-permute-done.1.refs_2_ = f32[4,40,512]{2,1,0:T(8,128)S(1)} collective-permute-done((f32[4,40,512]{2,1,0:T(8,128)S(1)}, f32[4,40,512]{2,1,0:T(8,128)S(1)}, u32[]{:S(2)}, u32[]{:S(2)}) %collective-permute-start.1) | collective-permute-done | bytes 327712 | tf_op jit(solution)/shard_map/edge_exchange_1/ppermute | solution.py:25
  53.4 1.4 %fusion.1.refs_4_ = f32[4,40,512]{2,1,0:T(8,128)} fusion(f32[4,40,512]{2,1,0:T(8,128)S(1)} %collective-permute-done.1.refs_2_), kind=kOutput, calls=%fused_computation.8 | convolution fusion | flops 504102912 | bytes 655360 | tf_op jit(solution)/shard_map/flow_step_1/dot_general | solution.py:358
  54.9 7.6 %flow_step_1.1 = (f32[4,2,5,2,8,512]{5,4,3,2,1,0:T(8,128)}, f32[4,2,5,2,8,512]{5,4,3,2,1,0:T(8,128)}, f32[2,8,512]{2,1,0:T(8,128)}) custom-call(s32[17]{0:T(128)} %pad_add_fusion.tbl, f32[4,2,5,2,8,512]{5,4,3,2,1,0:T(8,128)} %get-tuple-element.38.refs_0_, f32[4,2,5,2,8,512]{5,4,3,2,1,0:T(8,128)} %get-tuple-element.39.refs_1_, f32[4,40,512]{2,1,0:T(8,128)} %copy-done.5, ...), custom_call_target="tpu_custom_call" | custom-call | tf_op jit(solution)/shard_map/flow_step_1/pallas_call | solution.py:289
  62.4 0.7 collective-permute-start.4
  63.1 6.6 %collective-permute-start.5 = (f32[2,8,512]{2,1,0:T(8,128)}, f32[2,8,512]{2,1,0:T(8,128)S(1)}, u32[]{:S(2)}, u32[]{:S(2)}) collective-permute-start(f32[2,8,512]{2,1,0:T(8,128)} %get-tuple-element.47), channel_id=1, source_target_pairs={{2,0},{3,1},{0,2},{1,3},{6,4},{7,5},{4,6},{5,7},{10,8},{11,9},{8,1... | collective-permute-start | bytes 98312 | tf_op jit(solution)/shard_map/mode_reduce/ppermute | solution.py:25
  69.7 1.9 %collective-permute-start.6 = (f32[2,8,512]{2,1,0:T(8,128)}, f32[2,8,512]{2,1,0:T(8,128)S(1)}, u32[]{:S(2)}, u32[]{:S(2)}) collective-permute-start(f32[2,8,512]{2,1,0:T(8,128)} %get-tuple-element.47), channel_id=1, source_target_pairs={{1,0},{2,1},{3,2},{0,3},{5,4},{6,5},{7,6},{4,7},{9,8},{10,9},{11,1... | collective-permute-start | bytes 98312 | tf_op jit(solution)/shard_map/mode_reduce/ppermute | solution.py:25
  71.7 0.5 collective-permute-done.5
  72.2 1.7 %collective-permute-done.6 = f32[2,8,512]{2,1,0:T(8,128)S(1)} collective-permute-done((f32[2,8,512]{2,1,0:T(8,128)}, f32[2,8,512]{2,1,0:T(8,128)S(1)}, u32[]{:S(2)}, u32[]{:S(2)}) %collective-permute-start.6) | collective-permute-done | bytes 32800 | tf_op jit(solution)/shard_map/mode_reduce/ppermute | solution.py:25
  73.9 0.8 %pad_maximum_fusion.2 = f32[4,2,8,512]{3,2,1,0:T(8,128)S(1)} fusion(f32[1,2,8,512]{3,2,1,0:T(8,128)S(1)} %bitcast.384, f32[1,2,8,512]{3,2,1,0:T(8,128)S(1)} %bitcast.383, f32[1,2,8,512]{3,2,1,0:T(8,128)S(1)} %bitcast.382, f32[1,2,8,512]{3,2,1,0:T(8,128)} %bitcast.381), kind=kLoop, calls=%fused_computation.40 | loop fusion | flops 98304 | bytes 262144 | tf_op jit(solution)/shard_map/mode_reduce/stack | solution.py:418
  74.6 0.6 multiply_bitcast_fusion
  (85 shorter events, 1.4 us)
Async XLA Ops:
  0.6 14.2 %copy-start = (s32[128]{0:T(128)S(1)}, s32[128]{0:T(128)}, u32[]{:S(2)}) copy-start(s32[128]{0:T(128)} %param.19) | copy-start | bytes 1540
  0.6 14.0 %copy-start.7 = (s32[2,4]{1,0:T(2,128)S(1)}, s32[2,4]{1,0:T(2,128)}, u32[]{:S(2)}) copy-start(s32[2,4]{1,0:T(2,128)} %param.20) | copy-start | bytes 100
  0.7 15.2 %copy-start.6 = (s32[2,4]{1,0:T(2,128)S(1)}, s32[2,4]{1,0:T(2,128)}, u32[]{:S(2)}) copy-start(s32[2,4]{1,0:T(2,128)} %param.21) | copy-start | bytes 100
  0.7 15.3 %copy-start.3 = (f32[2,2,8,512]{3,2,1,0:T(8,128)S(1)}, f32[2,2,8,512]{3,2,1,0:T(8,128)}, u32[]{:S(2)}) copy-start(f32[2,2,8,512]{3,2,1,0:T(8,128)} %refs_9_.1) | copy-start | bytes 196612
  3.4 23.2 %collective-permute-start.2 = (f32[4,40,512]{2,1,0:T(8,128)}, f32[4,40,512]{2,1,0:T(8,128)S(1)}, u32[]{:S(2)}, u32[]{:S(2)}) collective-permute-start(f32[4,40,512]{2,1,0:T(8,128)} %get-tuple-element.43), channel_id=1, source_target_pairs={{252,0},{0,4},{4,8},{8,12},{12,16},{16,20},{20,24},{24,28},{28,32}... | collective-permute-start | bytes 983048 | tf_op jit(solution)/shard_map/edge_exchange_0/ppermute | solution.py:25
  3.4 26.4 %collective-permute-start = (f32[4,40,512]{2,1,0:T(8,128)}, f32[4,40,512]{2,1,0:T(8,128)S(1)}, u32[]{:S(2)}, u32[]{:S(2)}) collective-permute-start(f32[4,40,512]{2,1,0:T(8,128)} %get-tuple-element.41), channel_id=1, source_target_pairs={{4,0},{8,4},{12,8},{16,12},{20,16},{24,20},{28,24},{32,28},{36,32}... | collective-permute-start | bytes 983048 | tf_op jit(solution)/shard_map/edge_exchange_0/ppermute | solution.py:25
  33.2 21.6 %copy-start.1 = (f32[4,40,512]{2,1,0:T(8,128)}, f32[4,40,512]{2,1,0:T(8,128)S(1)}, u32[]{:S(2)}) copy-start(f32[4,40,512]{2,1,0:T(8,128)S(1)} %copy.200.refs_6_) | copy-start | bytes 983044
  33.2 15.4 %collective-permute-start.3 = (f32[4,40,512]{2,1,0:T(8,128)S(1)}, f32[4,40,512]{2,1,0:T(8,128)S(1)}, u32[]{:S(2)}, u32[]{:S(2)}) collective-permute-start(f32[4,40,512]{2,1,0:T(8,128)S(1)} %copy.200.refs_6_), channel_id=1, source_target_pairs={{4,0},{8,4},{12,8},{16,12},{20,16},{24,20},{28,24},{32,28},{36,32}... | collective-permute-start | bytes 983048 | tf_op jit(solution)/shard_map/edge_exchange_1/ppermute | solution.py:25
  35.6 19.2 %copy-start.2 = (f32[4,40,512]{2,1,0:T(8,128)}, f32[4,40,512]{2,1,0:T(8,128)S(1)}, u32[]{:S(2)}) copy-start(f32[4,40,512]{2,1,0:T(8,128)S(1)} %copy.163.refs_7_) | copy-start | bytes 983044
  35.6 17.8 %collective-permute-start.1 = (f32[4,40,512]{2,1,0:T(8,128)S(1)}, f32[4,40,512]{2,1,0:T(8,128)S(1)}, u32[]{:S(2)}, u32[]{:S(2)}) collective-permute-start(f32[4,40,512]{2,1,0:T(8,128)S(1)} %copy.163.refs_7_), channel_id=1, source_target_pairs={{252,0},{0,4},{4,8},{8,12},{12,16},{16,20},{20,24},{24,28},{28,32}... | collective-permute-start | bytes 983048 | tf_op jit(solution)/shard_map/edge_exchange_1/ppermute | solution.py:25
  48.6 6.3 %copy-start.4 = (f32[4,40,512]{2,1,0:T(8,128)}, f32[4,40,512]{2,1,0:T(8,128)S(1)}, u32[]{:S(2)}) copy-start(f32[4,40,512]{2,1,0:T(8,128)S(1)} %collective-permute-done.3.refs_3_) | copy-start | bytes 983044
  53.4 1.4 %copy-start.5 = (f32[4,40,512]{2,1,0:T(8,128)}, f32[4,40,512]{2,1,0:T(8,128)S(1)}, u32[]{:S(2)}) copy-start(f32[4,40,512]{2,1,0:T(8,128)S(1)} %collective-permute-done.1.refs_2_) | copy-start | bytes 983044
  62.4 9.2 %collective-permute-start.4 = (f32[2,8,512]{2,1,0:T(8,128)}, f32[2,8,512]{2,1,0:T(8,128)S(1)}, u32[]{:S(2)}, u32[]{:S(2)}) collective-permute-start(f32[2,8,512]{2,1,0:T(8,128)} %get-tuple-element.47), channel_id=1, source_target_pairs={{3,0},{0,1},{1,2},{2,3},{7,4},{4,5},{5,6},{6,7},{11,8},{8,9},{9,10... | collective-permute-start | bytes 98312 | tf_op jit(solution)/shard_map/mode_reduce/ppermute | solution.py:25
  63.1 9.1 %collective-permute-start.5 = (f32[2,8,512]{2,1,0:T(8,128)}, f32[2,8,512]{2,1,0:T(8,128)S(1)}, u32[]{:S(2)}, u32[]{:S(2)}) collective-permute-start(f32[2,8,512]{2,1,0:T(8,128)} %get-tuple-element.47), channel_id=1, source_target_pairs={{2,0},{3,1},{0,2},{1,3},{6,4},{7,5},{4,6},{5,7},{10,8},{11,9},{8,1... | collective-permute-start | bytes 98312 | tf_op jit(solution)/shard_map/mode_reduce/ppermute | solution.py:25
  69.7 4.1 %collective-permute-start.6 = (f32[2,8,512]{2,1,0:T(8,128)}, f32[2,8,512]{2,1,0:T(8,128)S(1)}, u32[]{:S(2)}, u32[]{:S(2)}) collective-permute-start(f32[2,8,512]{2,1,0:T(8,128)} %get-tuple-element.47), channel_id=1, source_target_pairs={{1,0},{2,1},{3,2},{0,3},{5,4},{6,5},{7,6},{4,7},{9,8},{10,9},{11,1... | collective-permute-start | bytes 98312 | tf_op jit(solution)/shard_map/mode_reduce/ppermute | solution.py:25

commit v9 on v8

--- a/solution.py
+++ b/solution.py
@@ -300,53 +300,47 @@
     return [u * f[0] + r * f[1], u * f[1] + f[4] * ir, u * f[2], u * f[3], kp * f[1] + u * f[4]]
 
 
-def unflat(e, slots):
-    modes, _, width = e.shape
-    return jnp.transpose(e.reshape(modes, 2, slots, 2 * NV, width), (1, 0, 2, 3, 4))
-
-
-def flat(e):
-    _, modes, slots, rows, width = e.shape
-    return jnp.transpose(e, (1, 0, 2, 3, 4)).reshape(modes, 2 * slots * rows, width)
-
-
 def fix_rows(partial0, partial7, rlo, rhi, slot_of, face_flip, density, velocity, pressure):
-    slots = density.shape[0]
-    partial0, partial7, rlo, rhi = (unflat(e, slots) for e in (partial0, partial7, rlo, rhi))
-    _, modes, slots, rows, width = partial0.shape
-    height = density.shape[1]
-
-    def picked(recv, side):
-        plain = jnp.take(recv, slot_of[:, side], axis=2)
-        turned = reverse_lanes(plain)
-        flag = (face_flip[:, side] != 0)[None, None, :, None, None]
-        return jnp.where(flag, turned, plain)
-
-    ghost = {0: picked(rlo, 0), height - 1: picked(rhi, 1)}
+    slots, height, width = density.shape
+    rows = 2 * NV
+    received = {0: (rlo, reverse_lanes(rlo)), height - 1: (rhi, reverse_lanes(rhi))}
     partial = {0: partial0, height - 1: partial7}
-    fixed = {}
-    sens_rows = {}
-    for row in (0, height - 1):
-        r = density[:, row, :]
-        ir = 1.0 / r
-        u = velocity[0][:, row, :]
-        kp = HEAT_RATIO * pressure[:, row, :]
+    fixed, sens_rows = {}, {}
+    for side, row in enumerate((0, height - 1)):
+        plain_all, turned_all = received[row]
+        r_all = density[:, row, :]
+        u_all = velocity[0][:, row, :]
+        kp_all = HEAT_RATIO * pressure[:, row, :]
         half = 0.5 if row == 0 else -0.5
-        out = []
+        pieces, means = [], {}
         for arr, sign in ((0, 1.0), (1, -1.0)):
-            g = ghost[row][arr].reshape(modes, slots, 2, NV, width)
-            res = []
-            for p in range(2):
-                f = [g[:, :, p, n, :] for n in range(NV)]
-                conv = ghost_term(f, r, ir, u, kp, arr == 1)
-                for n in range(NV):
-                    res.append(sign * half * conv[n] + VISCOSITY * f[n])
-            delta = jnp.stack(res, axis=2)
-            out.append(partial[row][arr] + TIME_STEP * delta)
-        fixed[row] = jnp.stack(out)
-        means = jnp.sum(fixed[row] * fixed[row], axis=3) / 10.0
-        sens_rows[row] = jnp.sum(means[0] * means[1], axis=0)
-    return flat(fixed[0]), flat(fixed[height - 1]), sens_rows[0], sens_rows[height - 1]
+            for s in range(slots):
+                t = slot_of[s, side]
+
+                def rows_of(block, slot):
+                    return block[:, (arr * slots + slot) * rows:(arr * slots + slot + 1) * rows, :]
+
+                plain, turned = rows_of(plain_all, 0), rows_of(turned_all, 0)
+                for other in range(1, slots):
+                    plain = jnp.where(t == other, rows_of(plain_all, other), plain)
+                    turned = jnp.where(t == other, rows_of(turned_all, other), turned)
+                g = jnp.where(face_flip[s, side] != 0, turned, plain)
+                r = r_all[s]
+                ir = 1.0 / r
+                u = u_all[s]
+                kp = kp_all[s]
+                res = []
+                for p in range(2):
+                    f = [g[:, p * NV + n, :] for n in range(NV)]
+                    conv = ghost_term(f, r, ir, u, kp, arr == 1)
+                    for n in range(NV):
+                        res.append(sign * half * conv[n] + VISCOSITY * f[n])
+                piece = rows_of(partial[row], s) + TIME_STEP * jnp.stack(res, axis=1)
+                pieces.append(piece)
+                means[arr, s] = jnp.sum(piece * piece, axis=1) / 10.0
+        fixed[row] = jnp.concatenate(pieces, axis=1)
+        sens_rows[row] = jnp.stack([jnp.sum(means[0, s] * means[1, s], axis=0) for s in range(slots)])
+    return fixed[0], fixed[height - 1], sens_rows[0], sens_rows[height - 1]
 
 
 def reverse_lanes(rows):

time: 76.3 us -> 82.2 us (1.077)
  starting transfers between devices: 22.2 us -> 27.6 us
  between operations: 1.17 us -> 6.22 us
  local copies, waits for them, and re-layouts: 10.1 us -> 7.21 us
  waiting for transfers between devices: 14 us -> 12.6 us
  matrix products: 5.02 us -> 4.17 us
    ppermute x7, starting transfers between devices: 22.2 us -> 27.6 us  [shifted(): return lax.ppermute(block, axis, route)]
    pallas_call x2 -> x0, local copies, waits for them, and re-layouts: 2.38 us -> none  [run_step(): pl.pallas_call(kernel, grid_spec=grid_spec, out_shape=out_shape, compiler...]
    gather x2 -> x0, local copies, waits for them, and re-layouts: 1.49 us -> none  [picked(): plain = jnp.take(recv, slot_of[:, side], axis=2)]
    ppermute x7, waiting for transfers between devices: 14 us -> 12.6 us  [shifted(): return lax.ppermute(block, axis, route)]
    another operation x0 -> x8, local copies, waits for them, and re-layouts: none -> 1.16 us  [fix_rows(): piece = rows_of(partial[row], s) + TIME_STEP * jnp.stack(res, axis=1)]
    add x2 -> x10, other arithmetic: 0.27 us -> 1.23 us  [fix_rows(): res.append(sign * half * conv[n] + VISCOSITY * f[n])]
    dot_general x4, matrix products: 5.02 us -> 4.17 us  [reverse_lanes(): jnp.dot(flat, turn, precision=lax.Precision.HIGHEST, preferred_element_ty...]
    slice x13 -> x6, local copies, waits for them, and re-layouts: 1.69 us -> 2.15 us  [the longest x1 0.81 us: fix_rows(): r = r_all[s]]
  transfers between devices with their start and end apart: 7 -> 7, of which waited for: 4 -> 4; matrix products, arithmetic and copies ran while one was open for 20% -> 16% of each run, Pallas kernels for 9% -> 8%
where the time goes in v9:
time: 82.2 us; the launch traced here: 81.3 us
  starting transfers between devices  27.6 us (34%)
  Pallas kernels  16.8 us (20%)
  waiting for transfers between devices  12.6 us (15%)
  local copies, waits for them, and re-layouts  7.21 us (9%)
  other arithmetic  6.64 us (8%)
  between operations  6.22 us (8%)
  matrix products  4.17 us (5%)
    ppermute x7, starting transfers between devices, shifted(): return lax.ppermute(block, axis, route)  27.6 us
    pallas_call x2, Pallas kernels, run_step(): pl.pallas_call(kernel, grid_spec=grid_spec, out_shape=out_shape, compiler...  14.1 us
    ppermute x7, waiting for transfers between devices, shifted(): return lax.ppermute(block, axis, route)  12.6 us
    dot_general x4, matrix products, reverse_lanes(): jnp.dot(flat, turn, precision=lax.Precision.HIGHEST, preferred_element_ty...  4.17 us
    scatter-add x2, local copies, waits for them, and re-layouts, per_device(): sens = sens.at[:, 0, :].add(s0).at[:, height - 1, :].add(s7)  2.78 us
    pallas_call x1, Pallas kernels, edge_rows(): return pl.pallas_call(edge_kernel, out_shape=[edge_shape, edge_shape])(x, a)  2.75 us
  transfers between devices with their start and end apart: 7, of which 4 were waited for; matrix products, arithmetic and copies ran while one was open for 16% of the time, Pallas kernels for 8%

profile of v9, /device:TPU:32, one launch (start us, length us, event | category | flops | bytes accessed | tf_op | source)
XLA Modules:
  0.0 81.3 jit_solution(8270517874252125096)
XLA Ops:
  0.7 2.8 %edge_exchange_0.1 = (f32[4,40,512]{2,1,0:T(8,128)}, f32[4,40,512]{2,1,0:T(8,128)}) custom-call(f32[4,2,5,2,8,512]{5,4,3,2,1,0:T(8,128)} %x_ref.1, f32[4,2,5,2,8,512]{5,4,3,2,1,0:T(8,128)} %a_ref.1), custom_call_target="tpu_custom_call" | custom-call | tf_op jit(solution)/shard_map/edge_exchange_0/pallas_call | solution.py:372
  3.4 10.4 %collective-permute-start = (f32[4,40,512]{2,1,0:T(8,128)}, f32[4,40,512]{2,1,0:T(8,128)S(1)}, u32[]{:S(2)}, u32[]{:S(2)}) collective-permute-start(f32[4,40,512]{2,1,0:T(8,128)} %get-tuple-element.40), channel_id=1, source_target_pairs={{4,0},{8,4},{12,8},{16,12},{20,16},{24,20},{28,24},{32,28},{36,32}... | collective-permute-start | bytes 983048 | tf_op jit(solution)/shard_map/edge_exchange_0/ppermute | solution.py:25
  13.8 0.7 fusion.41
  14.7 0.6 gather_fusion
  15.4 0.6 fusion.42
  18.7 0.8 %slice_multiply_fusion = (f32[2,1,512]{2,1,0:T(1,128)S(1)}, f32[2,1,512]{2,1,0:T(1,128)S(1)}) fusion(f32[2,8,512]{2,1,0:T(8,128)} %refs_10_.1), kind=kLoop, calls=%fused_computation.144 | loop fusion | flops 2048 | bytes 16384 | tf_op jit(solution)/shard_map/edge_fix_0/mul | solution.py:313
  19.5 0.8 fusion.37
  20.6 0.7 pad_add_fusion.tbl
  21.3 6.5 %flow_step_0.1 = (f32[4,2,5,2,8,512]{5,4,3,2,1,0:T(8,128)}, f32[4,2,5,2,8,512]{5,4,3,2,1,0:T(8,128)}, f32[2,8,512]{2,1,0:T(8,128)}, f32[4,40,512]{2,1,0:T(8,128)}, f32[4,40,512]{2,1,0:T(8,128)}) custom-call(s32[17]{0:T(128)} %pad_add_fusion.tbl, f32[4,2,5,2,8,512]{5,4,3,2,1,0:T(8,128)} %x_ref.1, f32[4,2,5,2,8,512]{5,4,3,2,1,0:T(8,128)} %a_ref.1, ...), custom_call_target="tpu_custom_call" | custom-call | tf_op jit(solution)/shard_map/flow_step_0/pallas_call | solution.py:289
  30.4 0.7 fusion.6
  31.2 0.1 multiply_add_fusion.68
  31.3 0.1 select_select_fusion.7
  31.4 0.1 multiply_add_fusion.48
  31.6 0.1 multiply_add_fusion.58
  31.7 0.1 multiply_add_fusion.78
  31.9 0.7 fusion.4
  32.7 0.1 multiply_add_fusion.28
  32.8 0.1 select_select_fusion.3
  32.9 0.1 multiply_add_fusion.8
  33.2 0.1 multiply_add_fusion.18
  33.3 0.1 multiply_add_fusion.38
  33.5 0.1 stack.46
  33.6 0.1 stack.47
  33.7 0.1 stack.48
  33.9 0.1 stack.45
  34.1 0.2 multiply_reduce_fusion.7
  34.3 9.9 %collective-permute-start.3 = (f32[4,40,512]{2,1,0:T(8,128)S(1)}, f32[4,40,512]{2,1,0:T(8,128)S(1)}, u32[]{:S(2)}, u32[]{:S(2)}) collective-permute-start(f32[4,40,512]{2,1,0:T(8,128)S(1)} %pad_maximum_fusion.1.refs_6_), channel_id=1, source_target_pairs={{4,0},{8,4},{12,8},{16,12},{20,16},{24,20},{28,24},{32,28},{36,32}... | collective-permute-start | bytes 983048 | tf_op jit(solution)/shard_map/edge_exchange_1/ppermute | solution.py:25
  44.3 0.1 stack.42
  44.4 0.1 stack.43
  44.6 0.1 stack.44
  44.7 0.1 stack.41
  44.9 0.2 multiply_reduce_fusion.3
  45.4 0.8 reshape_add_fusion
  46.1 1.4 %scatter-add.6 = f32[2,8,512]{2,1,0:T(8,128)} dynamic-update-slice(f32[2,8,512]{2,1,0:T(8,128)} %get-tuple-element.43, f32[2,1,512]{2,1,0:T(1,128)S(1)} %reshape_add_fusion, s32[]{:T(128)} %constant.149.clone.1, s32[]{:T(128)} %constant.149.clone.1, s32[]{:T(128)} %constant.149.clone.1) | dynamic-update-slice | bytes 8196 | tf_op jit(solution)/shard_map/edge_fix_0/scatter-add | solution.py:401
  47.5 0.8 slice_add_fusion
  48.3 1.4 %scatter-add.9.refs_11_ = f32[2,8,512]{2,1,0:T(8,128)} dynamic-update-slice(f32[2,8,512]{2,1,0:T(8,128)} %scatter-add.6, f32[2,1,512]{2,1,0:T(1,128)S(1)} %slice_add_fusion, s32[]{:T(128)} %constant.149.clone.1, s32[]{:T(128)} %constant.167.clone.1, s32[]{:T(128)} %constant.149.clone.1) | dynamic-update-slice | bytes 8196 | tf_op jit(solution)/shard_map/edge_fix_0/scatter-add | solution.py:401
  49.7 1.7 %collective-permute-done.3.refs_3_ = f32[4,40,512]{2,1,0:T(8,128)S(1)} collective-permute-done((f32[4,40,512]{2,1,0:T(8,128)S(1)}, f32[4,40,512]{2,1,0:T(8,128)S(1)}, u32[]{:S(2)}, u32[]{:S(2)}) %collective-permute-start.3) | collective-permute-done | bytes 327712 | tf_op jit(solution)/shard_map/edge_exchange_1/ppermute | solution.py:25
  51.4 1.4 %fusion.refs_5_ = f32[4,40,512]{2,1,0:T(8,128)} fusion(f32[4,40,512]{2,1,0:T(8,128)S(1)} %collective-permute-done.3.refs_3_), kind=kOutput, calls=%fused_computation.1 | convolution fusion | flops 504102912 | bytes 655360 | tf_op jit(solution)/shard_map/flow_step_1/dot_general | solution.py:352
  52.8 7.6 %collective-permute-done.1.refs_2_ = f32[4,40,512]{2,1,0:T(8,128)S(1)} collective-permute-done((f32[4,40,512]{2,1,0:T(8,128)S(1)}, f32[4,40,512]{2,1,0:T(8,128)S(1)}, u32[]{:S(2)}, u32[]{:S(2)}) %collective-permute-start.1) | collective-permute-done | bytes 327712 | tf_op jit(solution)/shard_map/edge_exchange_1/ppermute | solution.py:25
  60.5 1.4 %fusion.2.refs_4_ = f32[4,40,512]{2,1,0:T(8,128)} fusion(f32[4,40,512]{2,1,0:T(8,128)S(1)} %collective-permute-done.1.refs_2_), kind=kOutput, calls=%fused_computation.3 | convolution fusion | flops 504102912 | bytes 655360 | tf_op jit(solution)/shard_map/flow_step_1/dot_general | solution.py:352
  61.9 7.6 %flow_step_1.1 = (f32[4,2,5,2,8,512]{5,4,3,2,1,0:T(8,128)}, f32[4,2,5,2,8,512]{5,4,3,2,1,0:T(8,128)}, f32[2,8,512]{2,1,0:T(8,128)}) custom-call(s32[17]{0:T(128)} %pad_add_fusion.tbl, f32[4,2,5,2,8,512]{5,4,3,2,1,0:T(8,128)} %get-tuple-element.37.refs_0_, f32[4,2,5,2,8,512]{5,4,3,2,1,0:T(8,128)} %get-tuple-element.38.refs_1_, f32[4,40,512]{2,1,0:T(8,128)} %copy-done.7, ...), custom_call_target="tpu_custom_call" | custom-call | tf_op jit(solution)/shard_map/flow_step_1/pallas_call | solution.py:289
  69.4 1.9 %collective-permute-start.4 = (f32[2,8,512]{2,1,0:T(8,128)}, f32[2,8,512]{2,1,0:T(8,128)S(1)}, u32[]{:S(2)}, u32[]{:S(2)}) collective-permute-start(f32[2,8,512]{2,1,0:T(8,128)} %get-tuple-element.46), channel_id=1, source_target_pairs={{3,0},{0,1},{1,2},{2,3},{7,4},{4,5},{5,6},{6,7},{11,8},{8,9},{9,10... | collective-permute-start | bytes 98312 | tf_op jit(solution)/shard_map/mode_reduce/ppermute | solution.py:25
  71.3 4.5 %collective-permute-start.5 = (f32[2,8,512]{2,1,0:T(8,128)}, f32[2,8,512]{2,1,0:T(8,128)S(1)}, u32[]{:S(2)}, u32[]{:S(2)}) collective-permute-start(f32[2,8,512]{2,1,0:T(8,128)} %get-tuple-element.46), channel_id=1, source_target_pairs={{2,0},{3,1},{0,2},{1,3},{6,4},{7,5},{4,6},{5,7},{10,8},{11,9},{8,1... | collective-permute-start | bytes 98312 | tf_op jit(solution)/shard_map/mode_reduce/ppermute | solution.py:25
  75.8 0.8 %collective-permute-start.6 = (f32[2,8,512]{2,1,0:T(8,128)}, f32[2,8,512]{2,1,0:T(8,128)S(1)}, u32[]{:S(2)}, u32[]{:S(2)}) collective-permute-start(f32[2,8,512]{2,1,0:T(8,128)} %get-tuple-element.46), channel_id=1, source_target_pairs={{1,0},{2,1},{3,2},{0,3},{5,4},{6,5},{7,6},{4,7},{9,8},{10,9},{11,1... | collective-permute-start | bytes 98312 | tf_op jit(solution)/shard_map/mode_reduce/ppermute | solution.py:25
  76.6 1.6 %collective-permute-done.5 = f32[2,8,512]{2,1,0:T(8,128)S(1)} collective-permute-done((f32[2,8,512]{2,1,0:T(8,128)}, f32[2,8,512]{2,1,0:T(8,128)S(1)}, u32[]{:S(2)}, u32[]{:S(2)}) %collective-permute-start.5) | collective-permute-done | bytes 32800 | tf_op jit(solution)/shard_map/mode_reduce/ppermute | solution.py:25
  78.3 1.7 %collective-permute-done.6 = f32[2,8,512]{2,1,0:T(8,128)S(1)} collective-permute-done((f32[2,8,512]{2,1,0:T(8,128)}, f32[2,8,512]{2,1,0:T(8,128)S(1)}, u32[]{:S(2)}, u32[]{:S(2)}) %collective-permute-start.6) | collective-permute-done | bytes 32800 | tf_op jit(solution)/shard_map/mode_reduce/ppermute | solution.py:25
  79.9 0.8 pad_maximum_fusion.2
  80.7 0.6 multiply_bitcast_fusion
  (54 shorter events, 1.1 us)
Async XLA Ops:
  0.6 14.0 %copy-start = (s32[128]{0:T(128)S(1)}, s32[128]{0:T(128)}, u32[]{:S(2)}) copy-start(s32[128]{0:T(128)} %param.17) | copy-start | bytes 1540
  0.6 13.2 %copy-start.9 = (s32[2,4]{1,0:T(2,128)S(1)}, s32[2,4]{1,0:T(2,128)}, u32[]{:S(2)}) copy-start(s32[2,4]{1,0:T(2,128)} %param.18) | copy-start | bytes 100
  0.7 13.2 %copy-start.8 = (s32[2,4]{1,0:T(2,128)S(1)}, s32[2,4]{1,0:T(2,128)}, u32[]{:S(2)}) copy-start(s32[2,4]{1,0:T(2,128)} %param.19) | copy-start | bytes 100
  0.7 18.0 %copy-start.5 = (f32[2,2,8,512]{3,2,1,0:T(8,128)S(1)}, f32[2,2,8,512]{3,2,1,0:T(8,128)}, u32[]{:S(2)}) copy-start(f32[2,2,8,512]{3,2,1,0:T(8,128)} %refs_9_.1) | copy-start | bytes 196612
  3.4 27.0 %collective-permute-start = (f32[4,40,512]{2,1,0:T(8,128)}, f32[4,40,512]{2,1,0:T(8,128)S(1)}, u32[]{:S(2)}, u32[]{:S(2)}) collective-permute-start(f32[4,40,512]{2,1,0:T(8,128)} %get-tuple-element.40), channel_id=1, source_target_pairs={{4,0},{8,4},{12,8},{16,12},{20,16},{24,20},{28,24},{32,28},{36,32}... | collective-permute-start | bytes 983048 | tf_op jit(solution)/shard_map/edge_exchange_0/ppermute | solution.py:25
  13.8 18.1 %collective-permute-start.2 = (f32[4,40,512]{2,1,0:T(8,128)}, f32[4,40,512]{2,1,0:T(8,128)S(1)}, u32[]{:S(2)}, u32[]{:S(2)}) collective-permute-start(f32[4,40,512]{2,1,0:T(8,128)} %get-tuple-element.42), channel_id=1, source_target_pairs={{252,0},{0,4},{4,8},{8,12},{12,16},{16,20},{20,24},{24,28},{28,32}... | collective-permute-start | bytes 983048 | tf_op jit(solution)/shard_map/edge_exchange_0/ppermute | solution.py:25
  32.8 1.2 %copy-start.4 = (f32[4,40,512]{2,1,0:T(8,128)S(1)}, f32[4,40,512]{2,1,0:T(8,128)}, u32[]{:S(2)}) copy-start(f32[4,40,512]{2,1,0:T(8,128)} %get-tuple-element.41) | copy-start | bytes 983044
  34.1 10.8 %copy-start.3 = (f32[4,40,512]{2,1,0:T(8,128)S(1)}, f32[4,40,512]{2,1,0:T(8,128)}, u32[]{:S(2)}) copy-start(f32[4,40,512]{2,1,0:T(8,128)} %get-tuple-element.39) | copy-start | bytes 983044
  34.3 10.8 %copy-start.1 = (f32[4,40,512]{2,1,0:T(8,128)}, f32[4,40,512]{2,1,0:T(8,128)S(1)}, u32[]{:S(2)}) copy-start(f32[4,40,512]{2,1,0:T(8,128)S(1)} %pad_maximum_fusion.1.refs_6_) | copy-start | bytes 983044
  34.3 17.1 %collective-permute-start.3 = (f32[4,40,512]{2,1,0:T(8,128)S(1)}, f32[4,40,512]{2,1,0:T(8,128)S(1)}, u32[]{:S(2)}, u32[]{:S(2)}) collective-permute-start(f32[4,40,512]{2,1,0:T(8,128)S(1)} %pad_maximum_fusion.1.refs_6_), channel_id=1, source_target_pairs={{4,0},{8,4},{12,8},{16,12},{20,16},{24,20},{28,24},{32,28},{36,32}... | collective-permute-start | bytes 983048 | tf_op jit(solution)/shard_map/edge_exchange_1/ppermute | solution.py:25
  45.2 16.7 %copy-start.2 = (f32[4,40,512]{2,1,0:T(8,128)}, f32[4,40,512]{2,1,0:T(8,128)S(1)}, u32[]{:S(2)}) copy-start(f32[4,40,512]{2,1,0:T(8,128)S(1)} %pad_maximum_fusion.refs_7_) | copy-start | bytes 983044
  45.2 15.3 %collective-permute-start.1 = (f32[4,40,512]{2,1,0:T(8,128)S(1)}, f32[4,40,512]{2,1,0:T(8,128)S(1)}, u32[]{:S(2)}, u32[]{:S(2)}) collective-permute-start(f32[4,40,512]{2,1,0:T(8,128)S(1)} %pad_maximum_fusion.refs_7_), channel_id=1, source_target_pairs={{252,0},{0,4},{4,8},{8,12},{12,16},{16,20},{20,24},{24,28},{28,32}... | collective-permute-start | bytes 983048 | tf_op jit(solution)/shard_map/edge_exchange_1/ppermute | solution.py:25
  51.4 10.4 %copy-start.6 = (f32[4,40,512]{2,1,0:T(8,128)}, f32[4,40,512]{2,1,0:T(8,128)S(1)}, u32[]{:S(2)}) copy-start(f32[4,40,512]{2,1,0:T(8,128)S(1)} %collective-permute-done.3.refs_3_) | copy-start | bytes 983044
  60.4 1.4 %copy-start.7 = (f32[4,40,512]{2,1,0:T(8,128)}, f32[4,40,512]{2,1,0:T(8,128)S(1)}, u32[]{:S(2)}) copy-start(f32[4,40,512]{2,1,0:T(8,128)S(1)} %collective-permute-done.1.refs_2_) | copy-start | bytes 983044
  69.4 7.2 %collective-permute-start.4 = (f32[2,8,512]{2,1,0:T(8,128)}, f32[2,8,512]{2,1,0:T(8,128)S(1)}, u32[]{:S(2)}, u32[]{:S(2)}) collective-permute-start(f32[2,8,512]{2,1,0:T(8,128)} %get-tuple-element.46), channel_id=1, source_target_pairs={{3,0},{0,1},{1,2},{2,3},{7,4},{4,5},{5,6},{6,7},{11,8},{8,9},{9,10... | collective-permute-start | bytes 98312 | tf_op jit(solution)/shard_map/mode_reduce/ppermute | solution.py:25
  71.3 7.0 %collective-permute-start.5 = (f32[2,8,512]{2,1,0:T(8,128)}, f32[2,8,512]{2,1,0:T(8,128)S(1)}, u32[]{:S(2)}, u32[]{:S(2)}) collective-permute-start(f32[2,8,512]{2,1,0:T(8,128)} %get-tuple-element.46), channel_id=1, source_target_pairs={{2,0},{3,1},{0,2},{1,3},{6,4},{7,5},{4,6},{5,7},{10,8},{11,9},{8,1... | collective-permute-start | bytes 98312 | tf_op jit(solution)/shard_map/mode_reduce/ppermute | solution.py:25
  75.8 4.1 %collective-permute-start.6 = (f32[2,8,512]{2,1,0:T(8,128)}, f32[2,8,512]{2,1,0:T(8,128)S(1)}, u32[]{:S(2)}, u32[]{:S(2)}) collective-permute-start(f32[2,8,512]{2,1,0:T(8,128)} %get-tuple-element.46), channel_id=1, source_target_pairs={{1,0},{2,1},{3,2},{0,3},{5,4},{6,5},{7,6},{4,7},{9,8},{10,9},{11,1... | collective-permute-start | bytes 98312 | tf_op jit(solution)/shard_map/mode_reduce/ppermute | solution.py:25

commit v10 on v8

--- a/solution.py
+++ b/solution.py
@@ -231,9 +231,8 @@
                         nv = vals[k] + TIME_STEP * rate[n]
                         dst[0, p, n, s, :, cs] = nv
                         if first:
-                            at = (arr * slots + s) * 2 * NV + k
-                            elo_ref[0, pl.ds(at, 1), cs] = nv[0:1, :]
-                            ehi_ref[0, pl.ds(at, 1), cs] = nv[height - 1:height, :]
+                            elo_ref[arr, 0, s, pl.ds(k, 1), cs] = nv[0:1, :]
+                            ehi_ref[arr, 0, s, pl.ds(k, 1), cs] = nv[height - 1:height, :]
                         sq = nv * nv
                         total = sq if total is None else total + sq
                 means.append(total / 10.0)
@@ -273,9 +272,10 @@
     ]
     out_specs = [state_spec, state_spec, flow_spec]
     if first:
-        edge_shape = jax.ShapeDtypeStruct((modes, 2 * slots * parts * nv, width), jnp.float32)
-        out_shape += [edge_shape, edge_shape]
-        out_specs += [edge_spec, edge_spec]
+        part_shape = jax.ShapeDtypeStruct((2, modes, slots, parts * nv, width), jnp.float32)
+        part_spec = pl.BlockSpec((2, 1, slots, parts * nv, width), lambda m, t: (0, m, 0, 0, 0))
+        out_shape += [part_shape, part_shape]
+        out_specs += [part_spec, part_spec]
     grid_spec = pltpu.PrefetchScalarGridSpec(
         num_scalar_prefetch=1,
         grid=(modes,),
@@ -312,7 +312,7 @@
 
 def fix_rows(partial0, partial7, rlo, rhi, slot_of, face_flip, density, velocity, pressure):
     slots = density.shape[0]
-    partial0, partial7, rlo, rhi = (unflat(e, slots) for e in (partial0, partial7, rlo, rhi))
+    rlo, rhi = (unflat(e, slots) for e in (rlo, rhi))
     _, modes, slots, rows, width = partial0.shape
     height = density.shape[1]
 

time: 76.3 us -> 77 us (level)
  starting transfers between devices: 22.2 us -> 23.5 us
  local copies, waits for them, and re-layouts: 10.1 us -> 9.19 us
    pallas_call x2 -> x0, local copies, waits for them, and re-layouts: 2.38 us -> none  [run_step(): pl.pallas_call(kernel, grid_spec=grid_spec, out_shape=out_shape, compiler...]
    ppermute x7, starting transfers between devices: 22.2 us -> 23.5 us  [shifted(): return lax.ppermute(block, axis, route)]
    another operation x0 -> x4, local copies, waits for them, and re-layouts: none -> 1.02 us  [fix_rows(): delta = jnp.stack(res, axis=2)]
    another operation x4, other arithmetic: 0.11 us -> 0.98 us  [fix_rows(): delta = jnp.stack(res, axis=2)]
  transfers between devices with their start and end apart: 7 -> 7, of which waited for: 4 -> 5; matrix products, arithmetic and copies ran while one was open for 20% -> 18% of each run, Pallas kernels for 9% -> 9%
where the time goes in v10:
time: 77 us; the launch traced here: 76.2 us
  starting transfers between devices  23.5 us (31%)
  Pallas kernels  16.9 us (22%)
  waiting for transfers between devices  14.3 us (19%)
  local copies, waits for them, and re-layouts  9.19 us (12%)
  other arithmetic  6.19 us (8%)
  matrix products  4.99 us (6%)
  between operations  1.11 us (1%)
    ppermute x7, starting transfers between devices, shifted(): return lax.ppermute(block, axis, route)  23.5 us
    ppermute x7, waiting for transfers between devices, shifted(): return lax.ppermute(block, axis, route)  14.3 us
    pallas_call x2, Pallas kernels, run_step(): pl.pallas_call(kernel, grid_spec=grid_spec, out_shape=out_shape, compiler...  14.2 us
    dot_general x4, matrix products, reverse_lanes(): jnp.dot(flat, turn, precision=lax.Precision.HIGHEST, preferred_element_ty...  4.99 us
    scatter-add x2, local copies, waits for them, and re-layouts, per_device(): sens = sens.at[:, 0, :].add(s0).at[:, height - 1, :].add(s7)  2.78 us
    pallas_call x1, Pallas kernels, edge_rows(): return pl.pallas_call(edge_kernel, out_shape=[edge_shape, edge_shape])(x, a)  2.75 us
  transfers between devices with their start and end apart: 7, of which 5 were waited for; matrix products, arithmetic and copies ran while one was open for 18% of the time, Pallas kernels for 9%

profile of v10, /device:TPU:32, one launch (start us, length us, event | category | flops | bytes accessed | tf_op | source)
XLA Modules:
  0.0 76.2 jit_solution(11365590078157341327)
XLA Ops:
  0.7 2.8 %edge_exchange_0.1 = (f32[4,40,512]{2,1,0:T(8,128)}, f32[4,40,512]{2,1,0:T(8,128)}) custom-call(f32[4,2,5,2,8,512]{5,4,3,2,1,0:T(8,128)} %x_ref.1, f32[4,2,5,2,8,512]{5,4,3,2,1,0:T(8,128)} %a_ref.1), custom_call_target="tpu_custom_call" | custom-call | tf_op jit(solution)/shard_map/edge_exchange_0/pallas_call | solution.py:378
  3.4 10.4 %collective-permute-start = (f32[4,40,512]{2,1,0:T(8,128)}, f32[4,40,512]{2,1,0:T(8,128)S(1)}, u32[]{:S(2)}, u32[]{:S(2)}) collective-permute-start(f32[4,40,512]{2,1,0:T(8,128)} %get-tuple-element.41), channel_id=1, source_target_pairs={{4,0},{8,4},{12,8},{16,12},{20,16},{24,20},{28,24},{32,28},{36,32}... | collective-permute-start | bytes 983048 | tf_op jit(solution)/shard_map/edge_exchange_0/ppermute | solution.py:25
  13.8 0.8 %fusion.45 = (f32[2,1,512]{2,1,0:T(1,128)S(1)}, f32[2,1,512]{2,1,0:T(1,128)S(1)}) fusion(f32[2,8,512]{2,1,0:T(8,128)} %refs_8_.1), kind=kLoop, calls=%fused_computation.180 | loop fusion | bytes 16384 | tf_op jit(solution)/shard_map/edge_fix_0/slice | solution.py:330
  14.8 0.6 gather_fusion
  15.6 0.2 slice_reduce_fusion.1
  15.8 0.2 compare_reduce_fusion
  16.0 0.8 %slice_multiply_fusion.2 = (f32[2,1,512]{2,1,0:T(1,128)S(1)}, f32[2,1,512]{2,1,0:T(1,128)S(1)}) fusion(f32[2,8,512]{2,1,0:T(8,128)} %refs_10_.1), kind=kLoop, calls=%fused_computation.140 | loop fusion | flops 2048 | bytes 16384 | tf_op jit(solution)/shard_map/edge_fix_0/mul | solution.py:333
  17.1 0.6 pad_add_fusion.tbl
  17.7 6.6 %flow_step_0.1 = (f32[4,2,5,2,8,512]{5,4,3,2,1,0:T(8,128)}, f32[4,2,5,2,8,512]{5,4,3,2,1,0:T(8,128)}, f32[2,8,512]{2,1,0:T(8,128)}, f32[2,4,2,10,512]{4,3,2,1,0:T(8,128)}, f32[2,4,2,10,512]{4,3,2,1,0:T(8,128)}) custom-call(s32[17]{0:T(128)} %pad_add_fusion.tbl, f32[4,2,5,2,8,512]{5,4,3,2,1,0:T(8,128)} %x_ref.1, f32[4,2,5,2,8,512]{5,4,3,2,1,0:T(8,128)} %a_ref.1, ...), custom_call_target="tpu_custom_call" | custom-call | tf_op jit(solution)/shard_map/flow_step_0/pallas_call | solution.py:289
  24.4 2.0 %collective-permute-done.2 = f32[4,40,512]{2,1,0:T(8,128)S(1)} collective-permute-done((f32[4,40,512]{2,1,0:T(8,128)}, f32[4,40,512]{2,1,0:T(8,128)S(1)}, u32[]{:S(2)}, u32[]{:S(2)}) %collective-permute-start.2) | collective-permute-done | bytes 327712 | tf_op jit(solution)/shard_map/edge_exchange_0/ppermute | solution.py:25
  26.4 0.2 copy.150
  26.6 0.7 gather_fusion.2
  27.4 1.1 %convolution_select_fusion = f32[2,4,2,10,512]{4,3,2,1,0:T(8,128)S(1)} fusion(f32[2,2,4,10,512]{4,2,3,1,0:T(4,128)S(1)} %gather_fusion.2, pred[2]{0:T(512)(128)(4,1)S(1)} %get-tuple-element.200, pred[2]{0:T(512)(128)(4,1)S(1)} %get-tuple-element.48), kind=kOutput, calls=%fused_computation.5 | convolution fusion | flops 504348672 | bytes 655364 | tf_op jit(solution)/shard_map/edge_fix_0/dot_general | solution.py:358
  28.5 0.1 copy.152
  28.7 0.1 copy.164
  29.0 0.4 add_bitcast_fusion.11
  29.4 0.3 stack.205
  29.6 0.3 stack.194
  30.0 0.2 multiply_reduce_fusion.1
  30.2 0.2 copy.124
  30.4 0.7 gather_fusion.1
  31.2 1.1 %convolution_select_fusion.1 = f32[2,4,2,10,512]{4,3,2,1,0:T(8,128)S(1)} fusion(f32[2,2,4,10,512]{4,2,3,1,0:T(4,128)S(1)} %gather_fusion.1, pred[2]{0:T(512)(128)(4,1)S(1)} %get-tuple-element.201, pred[2]{0:T(512)(128)(4,1)S(1)} %get-tuple-element.49), kind=kOutput, calls=%fused_computation.6 | convolution fusion | flops 504348672 | bytes 655364 | tf_op jit(solution)/shard_map/edge_fix_0/dot_general | solution.py:358
  32.3 0.1 copy.137
  32.5 0.1 copy.126
  32.8 0.4 add_bitcast_fusion.31
  33.2 0.3 stack.182
  33.4 0.3 stack.171
  33.8 0.2 multiply_reduce_fusion
  34.0 0.2 copy.175
  34.3 2.0 %collective-permute-start.3 = (f32[4,40,512]{2,1,0:T(8,128)S(1)}, f32[4,40,512]{2,1,0:T(8,128)S(1)}, u32[]{:S(2)}, u32[]{:S(2)}) collective-permute-start(f32[4,40,512]{2,1,0:T(8,128)S(1)} %copy.176.refs_6_), channel_id=1, source_target_pairs={{4,0},{8,4},{12,8},{16,12},{20,16},{24,20},{28,24},{32,28},{36,32}... | collective-permute-start | bytes 983048 | tf_op jit(solution)/shard_map/edge_exchange_1/ppermute | solution.py:25
  36.3 0.2 copy.148
  36.6 0.3 collective-permute-start.1
  36.9 0.8 %reshape_add_fusion = f32[2,1,512]{2,1,0:T(1,128)S(1)} fusion(f32[2,512]{1,0:T(2,128)S(1)} %fusion.23, f32[2,8,512]{2,1,0:T(8,128)} %get-tuple-element.44), kind=kLoop, calls=%fused_computation.139 | loop fusion | flops 1024 | bytes 12288 | tf_op jit(solution)/shard_map/edge_fix_0/add | solution.py:407
  37.7 1.4 %scatter-add.6 = f32[2,8,512]{2,1,0:T(8,128)} dynamic-update-slice(f32[2,8,512]{2,1,0:T(8,128)} %get-tuple-element.44, f32[2,1,512]{2,1,0:T(1,128)S(1)} %reshape_add_fusion, s32[]{:T(128)} %constant.145.clone.1, s32[]{:T(128)} %constant.145.clone.1, s32[]{:T(128)} %constant.145.clone.1) | dynamic-update-slice | bytes 8196 | tf_op jit(solution)/shard_map/edge_fix_0/scatter-add | solution.py:407
  39.1 0.8 %slice_add_fusion = f32[2,1,512]{2,1,0:T(1,128)S(1)} fusion(f32[2,8,512]{2,1,0:T(8,128)} %scatter-add.6, f32[2,512]{1,0:T(2,128)S(1)} %fusion.22), kind=kLoop, calls=%fused_computation.129 | loop fusion | flops 1024 | bytes 12288 | tf_op jit(solution)/shard_map/edge_fix_0/add | solution.py:407
  39.9 1.4 %scatter-add.9.refs_11_ = f32[2,8,512]{2,1,0:T(8,128)} dynamic-update-slice(f32[2,8,512]{2,1,0:T(8,128)} %scatter-add.6, f32[2,1,512]{2,1,0:T(1,128)S(1)} %slice_add_fusion, s32[]{:T(128)} %constant.145.clone.1, s32[]{:T(128)} %constant.161.clone.1, s32[]{:T(128)} %constant.145.clone.1) | dynamic-update-slice | bytes 8196 | tf_op jit(solution)/shard_map/edge_fix_0/scatter-add | solution.py:407
  41.3 8.8 %collective-permute-done.3.refs_3_ = f32[4,40,512]{2,1,0:T(8,128)S(1)} collective-permute-done((f32[4,40,512]{2,1,0:T(8,128)S(1)}, f32[4,40,512]{2,1,0:T(8,128)S(1)}, u32[]{:S(2)}, u32[]{:S(2)}) %collective-permute-start.3) | collective-permute-done | bytes 327712 | tf_op jit(solution)/shard_map/edge_exchange_1/ppermute | solution.py:25
  50.0 1.4 %fusion.refs_5_ = f32[4,40,512]{2,1,0:T(8,128)} fusion(f32[4,40,512]{2,1,0:T(8,128)S(1)} %collective-permute-done.3.refs_3_), kind=kOutput, calls=%fused_computation.7 | convolution fusion | flops 504102912 | bytes 655360 | tf_op jit(solution)/shard_map/flow_step_1/dot_general | solution.py:358
  51.4 0.4 collective-permute-done.1.refs_2_
  51.8 1.4 %fusion.1.refs_4_ = f32[4,40,512]{2,1,0:T(8,128)} fusion(f32[4,40,512]{2,1,0:T(8,128)S(1)} %collective-permute-done.1.refs_2_), kind=kOutput, calls=%fused_computation.8 | convolution fusion | flops 504102912 | bytes 655360 | tf_op jit(solution)/shard_map/flow_step_1/dot_general | solution.py:358
  53.2 7.6 %flow_step_1.1 = (f32[4,2,5,2,8,512]{5,4,3,2,1,0:T(8,128)}, f32[4,2,5,2,8,512]{5,4,3,2,1,0:T(8,128)}, f32[2,8,512]{2,1,0:T(8,128)}) custom-call(s32[17]{0:T(128)} %pad_add_fusion.tbl, f32[4,2,5,2,8,512]{5,4,3,2,1,0:T(8,128)} %get-tuple-element.38.refs_0_, f32[4,2,5,2,8,512]{5,4,3,2,1,0:T(8,128)} %get-tuple-element.39.refs_1_, f32[4,40,512]{2,1,0:T(8,128)} %copy-done.7, ...), custom_call_target="tpu_custom_call" | custom-call | tf_op jit(solution)/shard_map/flow_step_1/pallas_call | solution.py:289
  60.7 3.9 %collective-permute-start.4 = (f32[2,8,512]{2,1,0:T(8,128)}, f32[2,8,512]{2,1,0:T(8,128)S(1)}, u32[]{:S(2)}, u32[]{:S(2)}) collective-permute-start(f32[2,8,512]{2,1,0:T(8,128)} %get-tuple-element.47), channel_id=1, source_target_pairs={{3,0},{0,1},{1,2},{2,3},{7,4},{4,5},{5,6},{6,7},{11,8},{8,9},{9,10... | collective-permute-start | bytes 98312 | tf_op jit(solution)/shard_map/mode_reduce/ppermute | solution.py:25
  64.7 6.0 %collective-permute-start.5 = (f32[2,8,512]{2,1,0:T(8,128)}, f32[2,8,512]{2,1,0:T(8,128)S(1)}, u32[]{:S(2)}, u32[]{:S(2)}) collective-permute-start(f32[2,8,512]{2,1,0:T(8,128)} %get-tuple-element.47), channel_id=1, source_target_pairs={{2,0},{3,1},{0,2},{1,3},{6,4},{7,5},{4,6},{5,7},{10,8},{11,9},{8,1... | collective-permute-start | bytes 98312 | tf_op jit(solution)/shard_map/mode_reduce/ppermute | solution.py:25
  70.7 1.0 %collective-permute-start.6 = (f32[2,8,512]{2,1,0:T(8,128)}, f32[2,8,512]{2,1,0:T(8,128)S(1)}, u32[]{:S(2)}, u32[]{:S(2)}) collective-permute-start(f32[2,8,512]{2,1,0:T(8,128)} %get-tuple-element.47), channel_id=1, source_target_pairs={{1,0},{2,1},{3,2},{0,3},{5,4},{6,5},{7,6},{4,7},{9,8},{10,9},{11,1... | collective-permute-start | bytes 98312 | tf_op jit(solution)/shard_map/mode_reduce/ppermute | solution.py:25
  71.7 1.5 %collective-permute-done.5 = f32[2,8,512]{2,1,0:T(8,128)S(1)} collective-permute-done((f32[2,8,512]{2,1,0:T(8,128)}, f32[2,8,512]{2,1,0:T(8,128)S(1)}, u32[]{:S(2)}, u32[]{:S(2)}) %collective-permute-start.5) | collective-permute-done | bytes 32800 | tf_op jit(solution)/shard_map/mode_reduce/ppermute | solution.py:25
  73.1 1.7 %collective-permute-done.6 = f32[2,8,512]{2,1,0:T(8,128)S(1)} collective-permute-done((f32[2,8,512]{2,1,0:T(8,128)}, f32[2,8,512]{2,1,0:T(8,128)S(1)}, u32[]{:S(2)}, u32[]{:S(2)}) %collective-permute-start.6) | collective-permute-done | bytes 32800 | tf_op jit(solution)/shard_map/mode_reduce/ppermute | solution.py:25
  74.8 0.8 %pad_maximum_fusion.2 = f32[4,2,8,512]{3,2,1,0:T(8,128)S(1)} fusion(f32[1,2,8,512]{3,2,1,0:T(8,128)S(1)} %bitcast.358, f32[1,2,8,512]{3,2,1,0:T(8,128)S(1)} %bitcast.357, f32[1,2,8,512]{3,2,1,0:T(8,128)S(1)} %bitcast.356, f32[1,2,8,512]{3,2,1,0:T(8,128)} %bitcast.355), kind=kLoop, calls=%fused_computation.40 | loop fusion | flops 98304 | bytes 262144 | tf_op jit(solution)/shard_map/mode_reduce/stack | solution.py:418
  75.6 0.6 multiply_bitcast_fusion
  (59 shorter events, 1.4 us)
Async XLA Ops:
  0.6 14.2 %copy-start = (s32[128]{0:T(128)S(1)}, s32[128]{0:T(128)}, u32[]{:S(2)}) copy-start(s32[128]{0:T(128)} %param.19) | copy-start | bytes 1540
  0.6 14.0 %copy-start.9 = (s32[2,4]{1,0:T(2,128)S(1)}, s32[2,4]{1,0:T(2,128)}, u32[]{:S(2)}) copy-start(s32[2,4]{1,0:T(2,128)} %param.20) | copy-start | bytes 100
  0.7 15.1 %copy-start.8 = (s32[2,4]{1,0:T(2,128)S(1)}, s32[2,4]{1,0:T(2,128)}, u32[]{:S(2)}) copy-start(s32[2,4]{1,0:T(2,128)} %param.21) | copy-start | bytes 100
  0.7 15.3 %copy-start.5 = (f32[2,2,8,512]{3,2,1,0:T(8,128)S(1)}, f32[2,2,8,512]{3,2,1,0:T(8,128)}, u32[]{:S(2)}) copy-start(f32[2,2,8,512]{3,2,1,0:T(8,128)} %refs_9_.1) | copy-start | bytes 196612
  3.4 23.0 %collective-permute-start.2 = (f32[4,40,512]{2,1,0:T(8,128)}, f32[4,40,512]{2,1,0:T(8,128)S(1)}, u32[]{:S(2)}, u32[]{:S(2)}) collective-permute-start(f32[4,40,512]{2,1,0:T(8,128)} %get-tuple-element.43), channel_id=1, source_target_pairs={{252,0},{0,4},{4,8},{8,12},{12,16},{16,20},{20,24},{24,28},{28,32}... | collective-permute-start | bytes 983048 | tf_op jit(solution)/shard_map/edge_exchange_0/ppermute | solution.py:25
  3.4 26.8 %collective-permute-start = (f32[4,40,512]{2,1,0:T(8,128)}, f32[4,40,512]{2,1,0:T(8,128)S(1)}, u32[]{:S(2)}, u32[]{:S(2)}) collective-permute-start(f32[4,40,512]{2,1,0:T(8,128)} %get-tuple-element.41), channel_id=1, source_target_pairs={{4,0},{8,4},{12,8},{16,12},{20,16},{24,20},{28,24},{32,28},{36,32}... | collective-permute-start | bytes 983048 | tf_op jit(solution)/shard_map/edge_exchange_0/ppermute | solution.py:25
  28.6 1.2 %copy-start.4 = (f32[2,4,2,10,512]{4,3,2,1,0:T(8,128)S(1)}, f32[2,4,2,10,512]{4,3,2,1,0:T(8,128)}, u32[]{:S(2)}) copy-start(f32[2,4,2,10,512]{4,3,2,1,0:T(8,128)} %get-tuple-element.42) | copy-start | bytes 983044
  32.5 1.2 %copy-start.3 = (f32[2,4,2,10,512]{4,3,2,1,0:T(8,128)S(1)}, f32[2,4,2,10,512]{4,3,2,1,0:T(8,128)}, u32[]{:S(2)}) copy-start(f32[2,4,2,10,512]{4,3,2,1,0:T(8,128)} %get-tuple-element.40) | copy-start | bytes 983044
  34.3 17.1 %copy-start.1 = (f32[4,40,512]{2,1,0:T(8,128)}, f32[4,40,512]{2,1,0:T(8,128)S(1)}, u32[]{:S(2)}) copy-start(f32[4,40,512]{2,1,0:T(8,128)S(1)} %copy.176.refs_6_) | copy-start | bytes 983044
  34.3 15.7 %collective-permute-start.3 = (f32[4,40,512]{2,1,0:T(8,128)S(1)}, f32[4,40,512]{2,1,0:T(8,128)S(1)}, u32[]{:S(2)}, u32[]{:S(2)}) collective-permute-start(f32[4,40,512]{2,1,0:T(8,128)S(1)} %copy.176.refs_6_), channel_id=1, source_target_pairs={{4,0},{8,4},{12,8},{16,12},{20,16},{24,20},{28,24},{32,28},{36,32}... | collective-permute-start | bytes 983048 | tf_op jit(solution)/shard_map/edge_exchange_1/ppermute | solution.py:25
  36.6 16.5 %copy-start.2 = (f32[4,40,512]{2,1,0:T(8,128)}, f32[4,40,512]{2,1,0:T(8,128)S(1)}, u32[]{:S(2)}) copy-start(f32[4,40,512]{2,1,0:T(8,128)S(1)} %copy.149.refs_7_) | copy-start | bytes 983044
  36.6 15.1 %collective-permute-start.1 = (f32[4,40,512]{2,1,0:T(8,128)S(1)}, f32[4,40,512]{2,1,0:T(8,128)S(1)}, u32[]{:S(2)}, u32[]{:S(2)}) collective-permute-start(f32[4,40,512]{2,1,0:T(8,128)S(1)} %copy.149.refs_7_), channel_id=1, source_target_pairs={{252,0},{0,4},{4,8},{8,12},{12,16},{16,20},{20,24},{24,28},{28,32}... | collective-permute-start | bytes 983048 | tf_op jit(solution)/shard_map/edge_exchange_1/ppermute | solution.py:25
  50.0 3.2 %copy-start.6 = (f32[4,40,512]{2,1,0:T(8,128)}, f32[4,40,512]{2,1,0:T(8,128)S(1)}, u32[]{:S(2)}) copy-start(f32[4,40,512]{2,1,0:T(8,128)S(1)} %collective-permute-done.3.refs_3_) | copy-start | bytes 983044
  51.8 1.4 %copy-start.7 = (f32[4,40,512]{2,1,0:T(8,128)}, f32[4,40,512]{2,1,0:T(8,128)S(1)}, u32[]{:S(2)}) copy-start(f32[4,40,512]{2,1,0:T(8,128)S(1)} %collective-permute-done.1.refs_2_) | copy-start | bytes 983044
  60.7 10.9 %collective-permute-start.4 = (f32[2,8,512]{2,1,0:T(8,128)}, f32[2,8,512]{2,1,0:T(8,128)S(1)}, u32[]{:S(2)}, u32[]{:S(2)}) collective-permute-start(f32[2,8,512]{2,1,0:T(8,128)} %get-tuple-element.47), channel_id=1, source_target_pairs={{3,0},{0,1},{1,2},{2,3},{7,4},{4,5},{5,6},{6,7},{11,8},{8,9},{9,10... | collective-permute-start | bytes 98312 | tf_op jit(solution)/shard_map/mode_reduce/ppermute | solution.py:25
  64.7 8.4 %collective-permute-start.5 = (f32[2,8,512]{2,1,0:T(8,128)}, f32[2,8,512]{2,1,0:T(8,128)S(1)}, u32[]{:S(2)}, u32[]{:S(2)}) collective-permute-start(f32[2,8,512]{2,1,0:T(8,128)} %get-tuple-element.47), channel_id=1, source_target_pairs={{2,0},{3,1},{0,2},{1,3},{6,4},{7,5},{4,6},{5,7},{10,8},{11,9},{8,1... | collective-permute-start | bytes 98312 | tf_op jit(solution)/shard_map/mode_reduce/ppermute | solution.py:25
  70.7 4.1 %collective-permute-start.6 = (f32[2,8,512]{2,1,0:T(8,128)}, f32[2,8,512]{2,1,0:T(8,128)S(1)}, u32[]{:S(2)}, u32[]{:S(2)}) collective-permute-start(f32[2,8,512]{2,1,0:T(8,128)} %get-tuple-element.47), channel_id=1, source_target_pairs={{1,0},{2,1},{3,2},{0,3},{5,4},{6,5},{7,6},{4,7},{9,8},{10,9},{11,1... | collective-permute-start | bytes 98312 | tf_op jit(solution)/shard_map/mode_reduce/ppermute | solution.py:25

commit v11 on v8

--- a/solution.py
+++ b/solution.py
@@ -396,12 +396,14 @@
 
     with jax.named_scope("edge_exchange_0"):
         down, up = edge_rows(direct, adjoint)
-        rlo = shifted(up, "blk", 1)
-        rhi = shifted(down, "blk", -1)
     with jax.named_scope("flow_step_0"):
         q1, a1, sens, elo, ehi = run_step(
             table, direct, adjoint, None, None, None, density, velocity, pressure, None, modes_total, True
         )
+    with jax.named_scope("edge_exchange_0"):
+        up, down, sens = lax.optimization_barrier((up, down, sens))
+        rlo = shifted(up, "blk", 1)
+        rhi = shifted(down, "blk", -1)
     with jax.named_scope("edge_fix_0"):
         c0, c7, s0, s7 = fix_rows(elo, ehi, rlo, rhi, slot_of, face_flip, density, velocity, pressure)
         sens = sens.at[:, 0, :].add(s0).at[:, height - 1, :].add(s7)

time: 76.3 us -> 88.1 us (1.15)
  waiting for transfers between devices: 14 us -> 21 us
  other arithmetic: 5.96 us -> 8.11 us
  starting transfers between devices: 22.2 us -> 24.1 us
    ppermute x7, waiting for transfers between devices: 14 us -> 21 us  [shifted(): return lax.ppermute(block, axis, route)]
    ppermute x7, starting transfers between devices: 22.2 us -> 24.1 us  [shifted(): return lax.ppermute(block, axis, route)]
  transfers between devices with their start and end apart: 7 -> 7, of which waited for: 4 -> 5; matrix products, arithmetic and copies ran while one was open for 20% -> 15% of each run, Pallas kernels for 9% -> 0%
where the time goes in v11:
time: 88.1 us; the launch traced here: 87.2 us
  starting transfers between devices  24.1 us (27%)
  waiting for transfers between devices  21 us (24%)
  Pallas kernels  17 us (19%)
  local copies, waits for them, and re-layouts  10.9 us (12%)
  other arithmetic  8.11 us (9%)
  matrix products  5.01 us (6%)
  between operations  1.14 us (1%)
    ppermute x7, starting transfers between devices, shifted(): return lax.ppermute(block, axis, route)  24.1 us
    ppermute x7, waiting for transfers between devices, shifted(): return lax.ppermute(block, axis, route)  21 us
    pallas_call x2, Pallas kernels, run_step(): pl.pallas_call(kernel, grid_spec=grid_spec, out_shape=out_shape, compiler...  14.3 us
    dot_general x4, matrix products, reverse_lanes(): jnp.dot(flat, turn, precision=lax.Precision.HIGHEST, preferred_element_ty...  5.01 us
    scatter-add x2, local copies, waits for them, and re-layouts, per_device(): sens = sens.at[:, 0, :].add(s0).at[:, height - 1, :].add(s7)  2.78 us
    pallas_call x1, Pallas kernels, edge_rows(): return pl.pallas_call(edge_kernel, out_shape=[edge_shape, edge_shape])(x, a)  2.73 us
    pallas_call x2, local copies, waits for them, and re-layouts, run_step(): pl.pallas_call(kernel, grid_spec=grid_spec, out_shape=out_shape, compiler...  2.38 us
  transfers between devices with their start and end apart: 7, of which 5 were waited for; matrix products, arithmetic and copies ran while one was open for 15% of the time, Pallas kernels for 0%

profile of v11, /device:TPU:32, one launch (start us, length us, event | category | flops | bytes accessed | tf_op | source)
XLA Modules:
  0.0 87.2 jit_solution(10737690312336764927)
XLA Ops:
  0.6 0.7 broadcast_maximum_fusion
  1.3 0.7 compare_convert_fusion
  2.1 0.6 gather_fusion
  2.8 0.7 and_select_fusion
  3.5 0.2 slice_reduce_fusion.1
  3.7 0.8 fusion.45
  4.7 0.7 pad_add_fusion.tbl
  5.4 2.7 %edge_exchange_0.1 = (f32[4,40,512]{2,1,0:T(8,128)}, f32[4,40,512]{2,1,0:T(8,128)}) custom-call(f32[4,2,5,2,8,512]{5,4,3,2,1,0:T(8,128)} %x_ref.1, f32[4,2,5,2,8,512]{5,4,3,2,1,0:T(8,128)} %a_ref.1), custom_call_target="tpu_custom_call" | custom-call | tf_op jit(solution)/shard_map/edge_exchange_0/pallas_call | solution.py:378
  8.1 6.7 %flow_step_0.1 = (f32[4,2,5,2,8,512]{5,4,3,2,1,0:T(8,128)}, f32[4,2,5,2,8,512]{5,4,3,2,1,0:T(8,128)}, f32[2,8,512]{2,1,0:T(8,128)}, f32[4,40,512]{2,1,0:T(8,128)}, f32[4,40,512]{2,1,0:T(8,128)}) custom-call(s32[17]{0:T(128)} %pad_add_fusion.tbl, f32[4,2,5,2,8,512]{5,4,3,2,1,0:T(8,128)} %x_ref.1, f32[4,2,5,2,8,512]{5,4,3,2,1,0:T(8,128)} %a_ref.1, ...), custom_call_target="tpu_custom_call" | custom-call | tf_op jit(solution)/shard_map/flow_step_0/pallas_call | solution.py:289
  15.0 10.5 %collective-permute-start = (f32[4,40,512]{2,1,0:T(8,128)S(1)}, f32[4,40,512]{2,1,0:T(8,128)S(1)}, u32[]{:S(2)}, u32[]{:S(2)}) collective-permute-start(f32[4,40,512]{2,1,0:T(8,128)S(1)} %copy-done.7), channel_id=1, source_target_pairs={{4,0},{8,4},{12,8},{16,12},{20,16},{24,20},{28,24},{32,28},{36,32}... | collective-permute-start | bytes 983048 | tf_op jit(solution)/shard_map/edge_exchange_0/ppermute | solution.py:25
  25.4 0.2 compare_reduce_fusion
  25.6 0.8 fusion.43
  26.5 0.8 slice_multiply_fusion.2
  27.4 1.2 %copy.164 = f32[4,40,512]{2,0,1:T(4,128)S(1)} copy(f32[4,40,512]{2,1,0:T(8,128)} %get-tuple-element.48) | data formatting | bytes 655360 | tf_op jit(solution)/shard_map/flow_step_0/pallas_call | solution.py:289
  28.6 1.2 %copy.135 = f32[4,40,512]{2,0,1:T(4,128)S(1)} copy(f32[4,40,512]{2,1,0:T(8,128)} %get-tuple-element.43) | data formatting | bytes 655360 | tf_op jit(solution)/shard_map/flow_step_0/pallas_call | solution.py:289
  29.8 7.9 %collective-permute-done.2 = f32[4,40,512]{2,1,0:T(8,128)S(1)} collective-permute-done((f32[4,40,512]{2,1,0:T(8,128)S(1)}, f32[4,40,512]{2,1,0:T(8,128)S(1)}, u32[]{:S(2)}, u32[]{:S(2)}) %collective-permute-start.2) | collective-permute-done | bytes 327712 | tf_op jit(solution)/shard_map/edge_exchange_0/ppermute | solution.py:25
  37.7 0.2 copy.165
  37.9 0.7 gather_fusion.2
  38.7 1.1 %convolution_select_fusion = f32[2,4,2,10,512]{4,3,2,1,0:T(8,128)S(1)} fusion(f32[2,2,4,10,512]{4,2,3,1,0:T(4,128)S(1)} %gather_fusion.2, pred[2]{0:T(512)(128)(4,1)S(1)} %get-tuple-element.128, pred[2]{0:T(512)(128)(4,1)S(1)} %get-tuple-element.54), kind=kOutput, calls=%fused_computation.5 | convolution fusion | flops 504348672 | bytes 655364 | tf_op jit(solution)/shard_map/edge_fix_0/dot_general | solution.py:358
  39.8 0.1 copy.188
  40.2 0.1 copy.167
  40.6 0.1 slice_add_fusion.1
  40.8 0.1 multiply_reduce_fusion.1
  40.9 0.2 copy.136
  41.1 0.7 gather_fusion.1
  41.9 1.1 %convolution_select_fusion.1 = f32[2,4,2,10,512]{4,3,2,1,0:T(8,128)S(1)} fusion(f32[2,2,4,10,512]{4,2,3,1,0:T(4,128)S(1)} %gather_fusion.1, pred[2]{0:T(512)(128)(4,1)S(1)} %get-tuple-element.129, pred[2]{0:T(512)(128)(4,1)S(1)} %get-tuple-element.55), kind=kOutput, calls=%fused_computation.6 | convolution fusion | flops 504348672 | bytes 655364 | tf_op jit(solution)/shard_map/edge_fix_0/dot_general | solution.py:358
  43.0 0.1 copy.138
  43.2 0.1 copy.150
  43.8 0.1 slice_add_fusion.3
  44.1 0.1 copy.200.refs_6_
  44.2 2.6 %collective-permute-start.3 = (f32[4,40,512]{2,1,0:T(8,128)S(1)}, f32[4,40,512]{2,1,0:T(8,128)S(1)}, u32[]{:S(2)}, u32[]{:S(2)}) collective-permute-start(f32[4,40,512]{2,1,0:T(8,128)S(1)} %copy.200.refs_6_), channel_id=1, source_target_pairs={{4,0},{8,4},{12,8},{16,12},{20,16},{24,20},{28,24},{32,28},{36,32}... | collective-permute-start | bytes 983048 | tf_op jit(solution)/shard_map/edge_exchange_1/ppermute | solution.py:25
  46.8 0.1 copy.163.refs_7_
  46.9 0.3 collective-permute-start.1
  47.2 0.8 reshape_add_fusion
  47.9 1.4 %scatter-add.6 = f32[2,8,512]{2,1,0:T(8,128)} dynamic-update-slice(f32[2,8,512]{2,1,0:T(8,128)} %get-tuple-element.50, f32[2,1,512]{2,1,0:T(1,128)S(1)} %reshape_add_fusion, s32[]{:T(128)} %constant.145.clone.1, s32[]{:T(128)} %constant.145.clone.1, s32[]{:T(128)} %constant.145.clone.1) | dynamic-update-slice | bytes 8196 | tf_op jit(solution)/shard_map/edge_fix_0/scatter-add | solution.py:409
  49.4 0.8 slice_add_fusion.4
  50.1 1.4 %scatter-add.9.refs_11_ = f32[2,8,512]{2,1,0:T(8,128)} dynamic-update-slice(f32[2,8,512]{2,1,0:T(8,128)} %scatter-add.6, f32[2,1,512]{2,1,0:T(1,128)S(1)} %slice_add_fusion.4, s32[]{:T(128)} %constant.145.clone.1, s32[]{:T(128)} %constant.161.clone.1, s32[]{:T(128)} %constant.145.clone.1) | dynamic-update-slice | bytes 8196 | tf_op jit(solution)/shard_map/edge_fix_0/scatter-add | solution.py:409
  51.5 2.7 %collective-permute-done.3.refs_3_ = f32[4,40,512]{2,1,0:T(8,128)S(1)} collective-permute-done((f32[4,40,512]{2,1,0:T(8,128)S(1)}, f32[4,40,512]{2,1,0:T(8,128)S(1)}, u32[]{:S(2)}, u32[]{:S(2)}) %collective-permute-start.3) | collective-permute-done | bytes 327712 | tf_op jit(solution)/shard_map/edge_exchange_1/ppermute | solution.py:25
  54.2 1.4 %fusion.refs_5_ = f32[4,40,512]{2,1,0:T(8,128)} fusion(f32[4,40,512]{2,1,0:T(8,128)S(1)} %collective-permute-done.3.refs_3_), kind=kOutput, calls=%fused_computation.7 | convolution fusion | flops 504102912 | bytes 655360 | tf_op jit(solution)/shard_map/flow_step_1/dot_general | solution.py:358
  55.6 6.3 %collective-permute-done.1.refs_2_ = f32[4,40,512]{2,1,0:T(8,128)S(1)} collective-permute-done((f32[4,40,512]{2,1,0:T(8,128)S(1)}, f32[4,40,512]{2,1,0:T(8,128)S(1)}, u32[]{:S(2)}, u32[]{:S(2)}) %collective-permute-start.1) | collective-permute-done | bytes 327712 | tf_op jit(solution)/shard_map/edge_exchange_1/ppermute | solution.py:25
  61.9 1.4 %fusion.1.refs_4_ = f32[4,40,512]{2,1,0:T(8,128)} fusion(f32[4,40,512]{2,1,0:T(8,128)S(1)} %collective-permute-done.1.refs_2_), kind=kOutput, calls=%fused_computation.8 | convolution fusion | flops 504102912 | bytes 655360 | tf_op jit(solution)/shard_map/flow_step_1/dot_general | solution.py:358
  63.4 7.6 %flow_step_1.1 = (f32[4,2,5,2,8,512]{5,4,3,2,1,0:T(8,128)}, f32[4,2,5,2,8,512]{5,4,3,2,1,0:T(8,128)}, f32[2,8,512]{2,1,0:T(8,128)}) custom-call(s32[17]{0:T(128)} %pad_add_fusion.tbl, f32[4,2,5,2,8,512]{5,4,3,2,1,0:T(8,128)} %get-tuple-element.41.refs_0_, f32[4,2,5,2,8,512]{5,4,3,2,1,0:T(8,128)} %get-tuple-element.42.refs_1_, f32[4,40,512]{2,1,0:T(8,128)} %copy-done.5, ...), custom_call_target="tpu_custom_call" | custom-call | tf_op jit(solution)/shard_map/flow_step_1/pallas_call | solution.py:289
  70.9 3.4 %collective-permute-start.4 = (f32[2,8,512]{2,1,0:T(8,128)}, f32[2,8,512]{2,1,0:T(8,128)S(1)}, u32[]{:S(2)}, u32[]{:S(2)}) collective-permute-start(f32[2,8,512]{2,1,0:T(8,128)} %get-tuple-element.53), channel_id=1, source_target_pairs={{3,0},{0,1},{1,2},{2,3},{7,4},{4,5},{5,6},{6,7},{11,8},{8,9},{9,10... | collective-permute-start | bytes 98312 | tf_op jit(solution)/shard_map/mode_reduce/ppermute | solution.py:25
  74.3 7.3 %collective-permute-start.5 = (f32[2,8,512]{2,1,0:T(8,128)}, f32[2,8,512]{2,1,0:T(8,128)S(1)}, u32[]{:S(2)}, u32[]{:S(2)}) collective-permute-start(f32[2,8,512]{2,1,0:T(8,128)} %get-tuple-element.53), channel_id=1, source_target_pairs={{2,0},{3,1},{0,2},{1,3},{6,4},{7,5},{4,6},{5,7},{10,8},{11,9},{8,1... | collective-permute-start | bytes 98312 | tf_op jit(solution)/shard_map/mode_reduce/ppermute | solution.py:25
  81.6 2.4 %collective-permute-done.5 = f32[2,8,512]{2,1,0:T(8,128)S(1)} collective-permute-done((f32[2,8,512]{2,1,0:T(8,128)}, f32[2,8,512]{2,1,0:T(8,128)S(1)}, u32[]{:S(2)}, u32[]{:S(2)}) %collective-permute-start.5) | collective-permute-done | bytes 32800 | tf_op jit(solution)/shard_map/mode_reduce/ppermute | solution.py:25
  84.1 1.7 %collective-permute-done.6 = f32[2,8,512]{2,1,0:T(8,128)S(1)} collective-permute-done((f32[2,8,512]{2,1,0:T(8,128)}, f32[2,8,512]{2,1,0:T(8,128)S(1)}, u32[]{:S(2)}, u32[]{:S(2)}) %collective-permute-start.6) | collective-permute-done | bytes 32800 | tf_op jit(solution)/shard_map/mode_reduce/ppermute | solution.py:25
  85.8 0.8 pad_maximum_fusion.2
  86.5 0.6 multiply_bitcast_fusion
  (87 shorter events, 1.7 us)
Async XLA Ops:
  0.6 1.5 %copy-start = (s32[128]{0:T(128)S(1)}, s32[128]{0:T(128)}, u32[]{:S(2)}) copy-start(s32[128]{0:T(128)} %param.19) | copy-start | bytes 1540
  8.1 6.7 %copy-start.8 = (f32[4,40,512]{2,1,0:T(8,128)S(1)}, f32[4,40,512]{2,1,0:T(8,128)}, u32[]{:S(2)}) copy-start(f32[4,40,512]{2,1,0:T(8,128)} %get-tuple-element.49) | copy-start | bytes 983044
  8.1 6.8 %copy-start.7 = (f32[4,40,512]{2,1,0:T(8,128)S(1)}, f32[4,40,512]{2,1,0:T(8,128)}, u32[]{:S(2)}) copy-start(f32[4,40,512]{2,1,0:T(8,128)} %get-tuple-element.47) | copy-start | bytes 983044
  8.1 17.3 %copy-start.6 = (s32[2,4]{1,0:T(2,128)S(1)}, s32[2,4]{1,0:T(2,128)}, u32[]{:S(2)}) copy-start(s32[2,4]{1,0:T(2,128)} %param.21) | copy-start | bytes 100
  8.1 17.5 %copy-start.3 = (f32[2,2,8,512]{3,2,1,0:T(8,128)S(1)}, f32[2,2,8,512]{3,2,1,0:T(8,128)}, u32[]{:S(2)}) copy-start(f32[2,2,8,512]{3,2,1,0:T(8,128)} %refs_9_.1) | copy-start | bytes 196612
  14.9 22.8 %collective-permute-start.2 = (f32[4,40,512]{2,1,0:T(8,128)S(1)}, f32[4,40,512]{2,1,0:T(8,128)S(1)}, u32[]{:S(2)}, u32[]{:S(2)}) collective-permute-start(f32[4,40,512]{2,1,0:T(8,128)S(1)} %copy-done.8), channel_id=1, source_target_pairs={{252,0},{0,4},{4,8},{8,12},{12,16},{16,20},{20,24},{24,28},{28,32}... | collective-permute-start | bytes 983048 | tf_op jit(solution)/shard_map/edge_exchange_0/ppermute | solution.py:25
  15.0 25.9 %collective-permute-start = (f32[4,40,512]{2,1,0:T(8,128)S(1)}, f32[4,40,512]{2,1,0:T(8,128)S(1)}, u32[]{:S(2)}, u32[]{:S(2)}) collective-permute-start(f32[4,40,512]{2,1,0:T(8,128)S(1)} %copy-done.7), channel_id=1, source_target_pairs={{4,0},{8,4},{12,8},{16,12},{20,16},{24,20},{28,24},{32,28},{36,32}... | collective-permute-start | bytes 983048 | tf_op jit(solution)/shard_map/edge_exchange_0/ppermute | solution.py:25
  44.2 19.1 %copy-start.1 = (f32[4,40,512]{2,1,0:T(8,128)}, f32[4,40,512]{2,1,0:T(8,128)S(1)}, u32[]{:S(2)}) copy-start(f32[4,40,512]{2,1,0:T(8,128)S(1)} %copy.200.refs_6_) | copy-start | bytes 983044
  44.2 10.0 %collective-permute-start.3 = (f32[4,40,512]{2,1,0:T(8,128)S(1)}, f32[4,40,512]{2,1,0:T(8,128)S(1)}, u32[]{:S(2)}, u32[]{:S(2)}) collective-permute-start(f32[4,40,512]{2,1,0:T(8,128)S(1)} %copy.200.refs_6_), channel_id=1, source_target_pairs={{4,0},{8,4},{12,8},{16,12},{20,16},{24,20},{28,24},{32,28},{36,32}... | collective-permute-start | bytes 983048 | tf_op jit(solution)/shard_map/edge_exchange_1/ppermute | solution.py:25
  46.9 16.5 %copy-start.2 = (f32[4,40,512]{2,1,0:T(8,128)}, f32[4,40,512]{2,1,0:T(8,128)S(1)}, u32[]{:S(2)}) copy-start(f32[4,40,512]{2,1,0:T(8,128)S(1)} %copy.163.refs_7_) | copy-start | bytes 983044
  46.9 15.0 %collective-permute-start.1 = (f32[4,40,512]{2,1,0:T(8,128)S(1)}, f32[4,40,512]{2,1,0:T(8,128)S(1)}, u32[]{:S(2)}, u32[]{:S(2)}) collective-permute-start(f32[4,40,512]{2,1,0:T(8,128)S(1)} %copy.163.refs_7_), channel_id=1, source_target_pairs={{252,0},{0,4},{4,8},{8,12},{12,16},{16,20},{20,24},{24,28},{28,32}... | collective-permute-start | bytes 983048 | tf_op jit(solution)/shard_map/edge_exchange_1/ppermute | solution.py:25
  54.2 9.1 %copy-start.4 = (f32[4,40,512]{2,1,0:T(8,128)}, f32[4,40,512]{2,1,0:T(8,128)S(1)}, u32[]{:S(2)}) copy-start(f32[4,40,512]{2,1,0:T(8,128)S(1)} %collective-permute-done.3.refs_3_) | copy-start | bytes 983044
  61.9 1.4 %copy-start.5 = (f32[4,40,512]{2,1,0:T(8,128)}, f32[4,40,512]{2,1,0:T(8,128)S(1)}, u32[]{:S(2)}) copy-start(f32[4,40,512]{2,1,0:T(8,128)S(1)} %collective-permute-done.1.refs_2_) | copy-start | bytes 983044
  70.9 10.7 %collective-permute-start.4 = (f32[2,8,512]{2,1,0:T(8,128)}, f32[2,8,512]{2,1,0:T(8,128)S(1)}, u32[]{:S(2)}, u32[]{:S(2)}) collective-permute-start(f32[2,8,512]{2,1,0:T(8,128)} %get-tuple-element.53), channel_id=1, source_target_pairs={{3,0},{0,1},{1,2},{2,3},{7,4},{4,5},{5,6},{6,7},{11,8},{8,9},{9,10... | collective-permute-start | bytes 98312 | tf_op jit(solution)/shard_map/mode_reduce/ppermute | solution.py:25
  74.3 9.7 %collective-permute-start.5 = (f32[2,8,512]{2,1,0:T(8,128)}, f32[2,8,512]{2,1,0:T(8,128)S(1)}, u32[]{:S(2)}, u32[]{:S(2)}) collective-permute-start(f32[2,8,512]{2,1,0:T(8,128)} %get-tuple-element.53), channel_id=1, source_target_pairs={{2,0},{3,1},{0,2},{1,3},{6,4},{7,5},{4,6},{5,7},{10,8},{11,9},{8,1... | collective-permute-start | bytes 98312 | tf_op jit(solution)/shard_map/mode_reduce/ppermute | solution.py:25
  81.6 4.1 %collective-permute-start.6 = (f32[2,8,512]{2,1,0:T(8,128)}, f32[2,8,512]{2,1,0:T(8,128)S(1)}, u32[]{:S(2)}, u32[]{:S(2)}) collective-permute-start(f32[2,8,512]{2,1,0:T(8,128)} %get-tuple-element.53), channel_id=1, source_target_pairs={{1,0},{2,1},{3,2},{0,3},{5,4},{6,5},{7,6},{4,7},{9,8},{10,9},{11,1... | collective-permute-start | bytes 98312 | tf_op jit(solution)/shard_map/mode_reduce/ppermute | solution.py:25

commit v12 on v8

--- a/solution.py
+++ b/solution.py
@@ -382,7 +382,8 @@
     modes, parts, nv, slots, height, width = direct.shape
     modes_total = modes * lax.axis_size("mode")
     live = (face_nbr >= 0).astype(jnp.int32)
-    positions = jnp.take(block_home, jnp.maximum(face_nbr, 0), axis=0)
+    hits = face_nbr[:, :, None] == lax.broadcasted_iota(jnp.int32, (1, 1, block_home.shape[0]), 2)
+    positions = jnp.sum(jnp.where(hits, block_home[None, None, :], 0), axis=2)
     slot_of = positions % slots
     table = jnp.stack(
         [

time: 76.3 us -> 76.3 us (level)
  starting transfers between devices: 22.2 us -> 23.4 us
  local copies, waits for them, and re-layouts: 10.1 us -> 9.29 us
    ppermute x7, starting transfers between devices: 22.2 us -> 23.4 us  [shifted(): return lax.ppermute(block, axis, route)]
  transfers between devices with their start and end apart: 7 -> 7, of which waited for: 4 -> 5; matrix products, arithmetic and copies ran while one was open for 20% -> 19% of each run, Pallas kernels for 9% -> 9%
where the time goes in v12:
time: 76.3 us; the launch traced here: 75.3 us
  starting transfers between devices  23.4 us (31%)
  Pallas kernels  16.9 us (22%)
  waiting for transfers between devices  13.3 us (17%)
  local copies, waits for them, and re-layouts  9.29 us (12%)
  other arithmetic  6.23 us (8%)
  matrix products  5.09 us (7%)
  between operations  1.17 us (2%)
    ppermute x7, starting transfers between devices, shifted(): return lax.ppermute(block, axis, route)  23.4 us
    pallas_call x2, Pallas kernels, run_step(): pl.pallas_call(kernel, grid_spec=grid_spec, out_shape=out_shape, compiler...  14.1 us
    ppermute x7, waiting for transfers between devices, shifted(): return lax.ppermute(block, axis, route)  13.3 us
    dot_general x4, matrix products, reverse_lanes(): jnp.dot(flat, turn, precision=lax.Precision.HIGHEST, preferred_element_ty...  5.09 us
    scatter-add x2, local copies, waits for them, and re-layouts, per_device(): sens = sens.at[:, 0, :].add(s0).at[:, height - 1, :].add(s7)  2.78 us
    pallas_call x1, Pallas kernels, edge_rows(): return pl.pallas_call(edge_kernel, out_shape=[edge_shape, edge_shape])(x, a)  2.76 us
    pallas_call x2, local copies, waits for them, and re-layouts, run_step(): pl.pallas_call(kernel, grid_spec=grid_spec, out_shape=out_shape, compiler...  2.38 us
    add x2, other arithmetic, per_device(): sens = sens.at[:, 0, :].add(s0).at[:, height - 1, :].add(s7)  1.54 us
  transfers between devices with their start and end apart: 7, of which 5 were waited for; matrix products, arithmetic and copies ran while one was open for 19% of the time, Pallas kernels for 9%

profile of v12, /device:TPU:32, one launch (start us, length us, event | category | flops | bytes accessed | tf_op | source)
XLA Modules:
  0.0 75.3 jit_solution(1895436792661117310)
XLA Ops:
  0.7 2.8 %edge_exchange_0.1 = (f32[4,40,512]{2,1,0:T(8,128)}, f32[4,40,512]{2,1,0:T(8,128)}) custom-call(f32[4,2,5,2,8,512]{5,4,3,2,1,0:T(8,128)} %x_ref.1, f32[4,2,5,2,8,512]{5,4,3,2,1,0:T(8,128)} %a_ref.1), custom_call_target="tpu_custom_call" | custom-call | tf_op jit(solution)/shard_map/edge_exchange_0/pallas_call | solution.py:378
  3.4 10.4 %collective-permute-start = (f32[4,40,512]{2,1,0:T(8,128)}, f32[4,40,512]{2,1,0:T(8,128)S(1)}, u32[]{:S(2)}, u32[]{:S(2)}) collective-permute-start(f32[4,40,512]{2,1,0:T(8,128)} %get-tuple-element.41), channel_id=1, source_target_pairs={{4,0},{8,4},{12,8},{16,12},{20,16},{24,20},{28,24},{32,28},{36,32}... | collective-permute-start | bytes 983048 | tf_op jit(solution)/shard_map/edge_exchange_0/ppermute | solution.py:25
  13.8 0.8 %fusion.43 = (f32[2,1,512]{2,1,0:T(1,128)S(1)}, f32[2,1,512]{2,1,0:T(1,128)S(1)}) fusion(f32[2,8,512]{2,1,0:T(8,128)} %refs_8_.1), kind=kLoop, calls=%fused_computation.179 | loop fusion | bytes 16384 | tf_op jit(solution)/shard_map/edge_fix_0/slice | solution.py:330
  14.7 0.2 select_reduce_fusion
  14.9 0.2 slice_reduce_fusion.1
  15.2 0.2 compare_reduce_fusion
  15.4 0.8 %slice_multiply_fusion.2 = (f32[2,1,512]{2,1,0:T(1,128)S(1)}, f32[2,1,512]{2,1,0:T(1,128)S(1)}) fusion(f32[2,8,512]{2,1,0:T(8,128)} %refs_10_.1), kind=kLoop, calls=%fused_computation.139 | loop fusion | flops 2048 | bytes 16384 | tf_op jit(solution)/shard_map/edge_fix_0/mul | solution.py:333
  16.3 0.1 stack.160
  16.4 0.1 reshape.2389
  16.5 0.7 pad_add_fusion.tbl
  17.2 6.5 %flow_step_0.1 = (f32[4,2,5,2,8,512]{5,4,3,2,1,0:T(8,128)}, f32[4,2,5,2,8,512]{5,4,3,2,1,0:T(8,128)}, f32[2,8,512]{2,1,0:T(8,128)}, f32[4,40,512]{2,1,0:T(8,128)}, f32[4,40,512]{2,1,0:T(8,128)}) custom-call(s32[17]{0:T(128)} %pad_add_fusion.tbl, f32[4,2,5,2,8,512]{5,4,3,2,1,0:T(8,128)} %x_ref.1, f32[4,2,5,2,8,512]{5,4,3,2,1,0:T(8,128)} %a_ref.1, ...), custom_call_target="tpu_custom_call" | custom-call | tf_op jit(solution)/shard_map/flow_step_0/pallas_call | solution.py:289
  23.7 1.2 %copy.300 = f32[4,40,512]{2,0,1:T(4,128)S(1)} copy(f32[4,40,512]{2,1,0:T(8,128)} %get-tuple-element.42) | data formatting | bytes 655360 | tf_op jit(solution)/shard_map/flow_step_0/pallas_call | solution.py:289
  24.9 1.2 %copy.271 = f32[4,40,512]{2,0,1:T(4,128)S(1)} copy(f32[4,40,512]{2,1,0:T(8,128)} %get-tuple-element.40) | data formatting | bytes 655360 | tf_op jit(solution)/shard_map/flow_step_0/pallas_call | solution.py:289
  26.2 0.2 collective-permute-done.2
  26.4 0.2 copy.301
  26.6 0.7 gather_fusion.1
  27.4 1.1 %convolution_select_fusion = f32[2,4,2,10,512]{4,3,2,1,0:T(8,128)S(1)} fusion(f32[2,2,4,10,512]{4,2,3,1,0:T(4,128)S(1)} %gather_fusion.1, pred[2]{0:T(512)(128)(4,1)S(1)} %get-tuple-element.122, pred[2]{0:T(512)(128)(4,1)S(1)} %get-tuple-element.48), kind=kOutput, calls=%fused_computation.4 | convolution fusion | flops 504348672 | bytes 655364 | tf_op jit(solution)/shard_map/edge_fix_0/dot_general | solution.py:358
  28.5 0.1 copy.324
  28.9 0.1 copy.303
  29.4 0.1 slice_add_fusion.1
  29.5 0.1 multiply_reduce_fusion.1
  29.6 0.2 copy.272
  29.9 0.7 gather_fusion
  30.6 1.1 %convolution_select_fusion.1 = f32[2,4,2,10,512]{4,3,2,1,0:T(8,128)S(1)} fusion(f32[2,2,4,10,512]{4,2,3,1,0:T(4,128)S(1)} %gather_fusion, pred[2]{0:T(512)(128)(4,1)S(1)} %get-tuple-element.123, pred[2]{0:T(512)(128)(4,1)S(1)} %get-tuple-element.49), kind=kOutput, calls=%fused_computation.5 | convolution fusion | flops 504348672 | bytes 655364 | tf_op jit(solution)/shard_map/edge_fix_0/dot_general | solution.py:358
  31.8 0.1 copy.274
  32.0 0.1 copy.286
  32.6 0.1 slice_add_fusion.3
  32.7 0.1 multiply_reduce_fusion
  32.8 0.1 copy.336.refs_6_
  33.0 2.5 %collective-permute-start.3 = (f32[4,40,512]{2,1,0:T(8,128)S(1)}, f32[4,40,512]{2,1,0:T(8,128)S(1)}, u32[]{:S(2)}, u32[]{:S(2)}) collective-permute-start(f32[4,40,512]{2,1,0:T(8,128)S(1)} %copy.336.refs_6_), channel_id=1, source_target_pairs={{4,0},{8,4},{12,8},{16,12},{20,16},{24,20},{28,24},{32,28},{36,32}... | collective-permute-start | bytes 983048 | tf_op jit(solution)/shard_map/edge_exchange_1/ppermute | solution.py:25
  35.5 0.1 copy.299.refs_7_
  35.6 0.3 collective-permute-start.1
  35.9 0.8 %reshape_add_fusion = f32[2,1,512]{2,1,0:T(1,128)S(1)} fusion(f32[2,512]{1,0:T(2,128)S(1)} %fusion.21, f32[2,8,512]{2,1,0:T(8,128)} %get-tuple-element.44), kind=kLoop, calls=%fused_computation.138 | loop fusion | flops 1024 | bytes 12288 | tf_op jit(solution)/shard_map/edge_fix_0/add | solution.py:408
  36.7 1.4 %scatter-add.6 = f32[2,8,512]{2,1,0:T(8,128)} dynamic-update-slice(f32[2,8,512]{2,1,0:T(8,128)} %get-tuple-element.44, f32[2,1,512]{2,1,0:T(1,128)S(1)} %reshape_add_fusion, s32[]{:T(128)} %constant.132.clone.1, s32[]{:T(128)} %constant.132.clone.1, s32[]{:T(128)} %constant.132.clone.1) | dynamic-update-slice | bytes 8196 | tf_op jit(solution)/shard_map/edge_fix_0/scatter-add | solution.py:408
  38.1 0.8 %slice_add_fusion.4 = f32[2,1,512]{2,1,0:T(1,128)S(1)} fusion(f32[2,8,512]{2,1,0:T(8,128)} %scatter-add.6, f32[2,512]{1,0:T(2,128)S(1)} %fusion.20), kind=kLoop, calls=%fused_computation.129 | loop fusion | flops 1024 | bytes 12288 | tf_op jit(solution)/shard_map/edge_fix_0/add | solution.py:408
  38.8 1.4 %scatter-add.9.refs_11_ = f32[2,8,512]{2,1,0:T(8,128)} dynamic-update-slice(f32[2,8,512]{2,1,0:T(8,128)} %scatter-add.6, f32[2,1,512]{2,1,0:T(1,128)S(1)} %slice_add_fusion.4, s32[]{:T(128)} %constant.132.clone.1, s32[]{:T(128)} %constant.146.clone.1, s32[]{:T(128)} %constant.132.clone.1) | dynamic-update-slice | bytes 8196 | tf_op jit(solution)/shard_map/edge_fix_0/scatter-add | solution.py:408
  40.2 6.9 %collective-permute-done.3.refs_3_ = f32[4,40,512]{2,1,0:T(8,128)S(1)} collective-permute-done((f32[4,40,512]{2,1,0:T(8,128)S(1)}, f32[4,40,512]{2,1,0:T(8,128)S(1)}, u32[]{:S(2)}, u32[]{:S(2)}) %collective-permute-start.3) | collective-permute-done | bytes 327712 | tf_op jit(solution)/shard_map/edge_exchange_1/ppermute | solution.py:25
  47.1 1.4 %fusion.refs_5_ = f32[4,40,512]{2,1,0:T(8,128)} fusion(f32[4,40,512]{2,1,0:T(8,128)S(1)} %collective-permute-done.3.refs_3_), kind=kOutput, calls=%fused_computation.6 | convolution fusion | flops 504102912 | bytes 655360 | tf_op jit(solution)/shard_map/flow_step_1/dot_general | solution.py:358
  48.6 3.9 %collective-permute-done.1.refs_2_ = f32[4,40,512]{2,1,0:T(8,128)S(1)} collective-permute-done((f32[4,40,512]{2,1,0:T(8,128)S(1)}, f32[4,40,512]{2,1,0:T(8,128)S(1)}, u32[]{:S(2)}, u32[]{:S(2)}) %collective-permute-start.1) | collective-permute-done | bytes 327712 | tf_op jit(solution)/shard_map/edge_exchange_1/ppermute | solution.py:25
  52.5 1.4 %fusion.1.refs_4_ = f32[4,40,512]{2,1,0:T(8,128)} fusion(f32[4,40,512]{2,1,0:T(8,128)S(1)} %collective-permute-done.1.refs_2_), kind=kOutput, calls=%fused_computation.7 | convolution fusion | flops 504102912 | bytes 655360 | tf_op jit(solution)/shard_map/flow_step_1/dot_general | solution.py:358
  53.9 7.6 %flow_step_1.1 = (f32[4,2,5,2,8,512]{5,4,3,2,1,0:T(8,128)}, f32[4,2,5,2,8,512]{5,4,3,2,1,0:T(8,128)}, f32[2,8,512]{2,1,0:T(8,128)}) custom-call(s32[17]{0:T(128)} %pad_add_fusion.tbl, f32[4,2,5,2,8,512]{5,4,3,2,1,0:T(8,128)} %get-tuple-element.38.refs_0_, f32[4,2,5,2,8,512]{5,4,3,2,1,0:T(8,128)} %get-tuple-element.39.refs_1_, f32[4,40,512]{2,1,0:T(8,128)} %copy-done.4, ...), custom_call_target="tpu_custom_call" | custom-call | tf_op jit(solution)/shard_map/flow_step_1/pallas_call | solution.py:289
  61.5 1.6 %collective-permute-start.4 = (f32[2,8,512]{2,1,0:T(8,128)}, f32[2,8,512]{2,1,0:T(8,128)S(1)}, u32[]{:S(2)}, u32[]{:S(2)}) collective-permute-start(f32[2,8,512]{2,1,0:T(8,128)} %get-tuple-element.47), channel_id=1, source_target_pairs={{3,0},{0,1},{1,2},{2,3},{7,4},{4,5},{5,6},{6,7},{11,8},{8,9},{9,10... | collective-permute-start | bytes 98312 | tf_op jit(solution)/shard_map/mode_reduce/ppermute | solution.py:25
  63.0 6.7 %collective-permute-start.5 = (f32[2,8,512]{2,1,0:T(8,128)}, f32[2,8,512]{2,1,0:T(8,128)S(1)}, u32[]{:S(2)}, u32[]{:S(2)}) collective-permute-start(f32[2,8,512]{2,1,0:T(8,128)} %get-tuple-element.47), channel_id=1, source_target_pairs={{2,0},{3,1},{0,2},{1,3},{6,4},{7,5},{4,6},{5,7},{10,8},{11,9},{8,1... | collective-permute-start | bytes 98312 | tf_op jit(solution)/shard_map/mode_reduce/ppermute | solution.py:25
  69.7 1.9 %collective-permute-start.6 = (f32[2,8,512]{2,1,0:T(8,128)}, f32[2,8,512]{2,1,0:T(8,128)S(1)}, u32[]{:S(2)}, u32[]{:S(2)}) collective-permute-start(f32[2,8,512]{2,1,0:T(8,128)} %get-tuple-element.47), channel_id=1, source_target_pairs={{1,0},{2,1},{3,2},{0,3},{5,4},{6,5},{7,6},{4,7},{9,8},{10,9},{11,1... | collective-permute-start | bytes 98312 | tf_op jit(solution)/shard_map/mode_reduce/ppermute | solution.py:25
  71.7 0.5 collective-permute-done.5
  72.2 1.7 %collective-permute-done.6 = f32[2,8,512]{2,1,0:T(8,128)S(1)} collective-permute-done((f32[2,8,512]{2,1,0:T(8,128)}, f32[2,8,512]{2,1,0:T(8,128)S(1)}, u32[]{:S(2)}, u32[]{:S(2)}) %collective-permute-start.6) | collective-permute-done | bytes 32800 | tf_op jit(solution)/shard_map/mode_reduce/ppermute | solution.py:25
  73.9 0.8 %pad_maximum_fusion.2 = f32[4,2,8,512]{3,2,1,0:T(8,128)S(1)} fusion(f32[1,2,8,512]{3,2,1,0:T(8,128)S(1)} %bitcast.384, f32[1,2,8,512]{3,2,1,0:T(8,128)S(1)} %bitcast.383, f32[1,2,8,512]{3,2,1,0:T(8,128)S(1)} %bitcast.382, f32[1,2,8,512]{3,2,1,0:T(8,128)} %bitcast.381), kind=kLoop, calls=%fused_computation.39 | loop fusion | flops 98304 | bytes 262144 | tf_op jit(solution)/shard_map/mode_reduce/stack | solution.py:419
  74.6 0.6 multiply_bitcast_fusion
  (81 shorter events, 1.2 us)
Async XLA Ops:
  0.6 14.1 %copy-start.6 = (s32[2,4]{1,0:T(2,128)S(1)}, s32[2,4]{1,0:T(2,128)}, u32[]{:S(2)}) copy-start(s32[2,4]{1,0:T(2,128)} %param.20) | copy-start | bytes 100
  0.6 14.1 %copy-start.7 = (s32[128]{0:T(128)S(1)}, s32[128]{0:T(128)}, u32[]{:S(2)}) copy-start(s32[128]{0:T(128)} %param.19) | copy-start | bytes 1540
  0.7 14.5 %copy-start.5 = (s32[2,4]{1,0:T(2,128)S(1)}, s32[2,4]{1,0:T(2,128)}, u32[]{:S(2)}) copy-start(s32[2,4]{1,0:T(2,128)} %param.21) | copy-start | bytes 100
  0.7 14.7 %copy-start.2 = (f32[2,2,8,512]{3,2,1,0:T(8,128)S(1)}, f32[2,2,8,512]{3,2,1,0:T(8,128)}, u32[]{:S(2)}) copy-start(f32[2,2,8,512]{3,2,1,0:T(8,128)} %refs_9_.1) | copy-start | bytes 196612
  3.4 23.0 %collective-permute-start.2 = (f32[4,40,512]{2,1,0:T(8,128)}, f32[4,40,512]{2,1,0:T(8,128)S(1)}, u32[]{:S(2)}, u32[]{:S(2)}) collective-permute-start(f32[4,40,512]{2,1,0:T(8,128)} %get-tuple-element.43), channel_id=1, source_target_pairs={{252,0},{0,4},{4,8},{8,12},{12,16},{16,20},{20,24},{24,28},{28,32}... | collective-permute-start | bytes 983048 | tf_op jit(solution)/shard_map/edge_exchange_0/ppermute | solution.py:25
  3.4 26.2 %collective-permute-start = (f32[4,40,512]{2,1,0:T(8,128)}, f32[4,40,512]{2,1,0:T(8,128)S(1)}, u32[]{:S(2)}, u32[]{:S(2)}) collective-permute-start(f32[4,40,512]{2,1,0:T(8,128)} %get-tuple-element.41), channel_id=1, source_target_pairs={{4,0},{8,4},{12,8},{16,12},{20,16},{24,20},{28,24},{32,28},{36,32}... | collective-permute-start | bytes 983048 | tf_op jit(solution)/shard_map/edge_exchange_0/ppermute | solution.py:25
  32.9 21.0 %copy-start = (f32[4,40,512]{2,1,0:T(8,128)}, f32[4,40,512]{2,1,0:T(8,128)S(1)}, u32[]{:S(2)}) copy-start(f32[4,40,512]{2,1,0:T(8,128)S(1)} %copy.336.refs_6_) | copy-start | bytes 983044
  33.0 14.2 %collective-permute-start.3 = (f32[4,40,512]{2,1,0:T(8,128)S(1)}, f32[4,40,512]{2,1,0:T(8,128)S(1)}, u32[]{:S(2)}, u32[]{:S(2)}) collective-permute-start(f32[4,40,512]{2,1,0:T(8,128)S(1)} %copy.336.refs_6_), channel_id=1, source_target_pairs={{4,0},{8,4},{12,8},{16,12},{20,16},{24,20},{28,24},{32,28},{36,32}... | collective-permute-start | bytes 983048 | tf_op jit(solution)/shard_map/edge_exchange_1/ppermute | solution.py:25
  35.6 18.3 %copy-start.1 = (f32[4,40,512]{2,1,0:T(8,128)}, f32[4,40,512]{2,1,0:T(8,128)S(1)}, u32[]{:S(2)}) copy-start(f32[4,40,512]{2,1,0:T(8,128)S(1)} %copy.299.refs_7_) | copy-start | bytes 983044
  35.6 16.9 %collective-permute-start.1 = (f32[4,40,512]{2,1,0:T(8,128)S(1)}, f32[4,40,512]{2,1,0:T(8,128)S(1)}, u32[]{:S(2)}, u32[]{:S(2)}) collective-permute-start(f32[4,40,512]{2,1,0:T(8,128)S(1)} %copy.299.refs_7_), channel_id=1, source_target_pairs={{252,0},{0,4},{4,8},{8,12},{12,16},{16,20},{20,24},{24,28},{28,32}... | collective-permute-start | bytes 983048 | tf_op jit(solution)/shard_map/edge_exchange_1/ppermute | solution.py:25
  47.1 6.8 %copy-start.3 = (f32[4,40,512]{2,1,0:T(8,128)}, f32[4,40,512]{2,1,0:T(8,128)S(1)}, u32[]{:S(2)}) copy-start(f32[4,40,512]{2,1,0:T(8,128)S(1)} %collective-permute-done.3.refs_3_) | copy-start | bytes 983044
  52.5 1.4 %copy-start.4 = (f32[4,40,512]{2,1,0:T(8,128)}, f32[4,40,512]{2,1,0:T(8,128)S(1)}, u32[]{:S(2)}) copy-start(f32[4,40,512]{2,1,0:T(8,128)S(1)} %collective-permute-done.1.refs_2_) | copy-start | bytes 983044
  61.5 10.2 %collective-permute-start.4 = (f32[2,8,512]{2,1,0:T(8,128)}, f32[2,8,512]{2,1,0:T(8,128)S(1)}, u32[]{:S(2)}, u32[]{:S(2)}) collective-permute-start(f32[2,8,512]{2,1,0:T(8,128)} %get-tuple-element.47), channel_id=1, source_target_pairs={{3,0},{0,1},{1,2},{2,3},{7,4},{4,5},{5,6},{6,7},{11,8},{8,9},{9,10... | collective-permute-start | bytes 98312 | tf_op jit(solution)/shard_map/mode_reduce/ppermute | solution.py:25
  63.0 9.1 %collective-permute-start.5 = (f32[2,8,512]{2,1,0:T(8,128)}, f32[2,8,512]{2,1,0:T(8,128)S(1)}, u32[]{:S(2)}, u32[]{:S(2)}) collective-permute-start(f32[2,8,512]{2,1,0:T(8,128)} %get-tuple-element.47), channel_id=1, source_target_pairs={{2,0},{3,1},{0,2},{1,3},{6,4},{7,5},{4,6},{5,7},{10,8},{11,9},{8,1... | collective-permute-start | bytes 98312 | tf_op jit(solution)/shard_map/mode_reduce/ppermute | solution.py:25
  69.7 4.1 %collective-permute-start.6 = (f32[2,8,512]{2,1,0:T(8,128)}, f32[2,8,512]{2,1,0:T(8,128)S(1)}, u32[]{:S(2)}, u32[]{:S(2)}) collective-permute-start(f32[2,8,512]{2,1,0:T(8,128)} %get-tuple-element.47), channel_id=1, source_target_pairs={{1,0},{2,1},{3,2},{0,3},{5,4},{6,5},{7,6},{4,7},{9,8},{10,9},{11,1... | collective-permute-start | bytes 98312 | tf_op jit(solution)/shard_map/mode_reduce/ppermute | solution.py:25
